TPU v7x, 512 devices: a whole 4x8x8 slice. The times are simulated.
512 devices in a mesh: cfg: 2 (over y_hi), req: 8 (over y_lo, core), seq: 32 (over z, x).
Axes of the slice: x: 4, y: 8 (y_hi: 2, y_lo: 4; y = y_hi * 4 + y_lo), z: 8, core: 2. Of those that a mesh axis runs over, the one named last changes fastest.
Arguments:
- query: bfloat16 [2, 8, 1024, 768], P('cfg', 'req', 'seq'), may hold values from -6 to 6
- key_value: bfloat16 [2, 2, 8, 1280, 768], P(None, 'cfg', 'req', 'seq'), may hold values from -6 to 6
- residual_in: bfloat16 [2, 8, 1024, 1536], P('cfg', 'req', 'seq'), may hold values from -0.119628906 to 0.119628906
- text_len: int32 [2, 8], P('cfg', 'req'), may hold values from 1 to 154, as said below
- attn_gate: float32 [2, 8, 1536], P('cfg', 'req'), may hold values from 0.5 to 2
- mlp_shift: float32 [2, 8, 1536], P('cfg', 'req'), may hold values from -3 to 3
- mlp_scale: float32 [2, 8, 1536], P('cfg', 'req'), may hold values from -3 to 3
- mlp_gate: float32 [2, 8, 1536], P('cfg', 'req'), may hold values from 0.5 to 2
- shift: float32 [2, 8, 1536], P('cfg', 'req'), may hold values from -3 to 3
- scale: float32 [2, 8, 1536], P('cfg', 'req'), may hold values from -3 to 3
- w_proj: bfloat16 [768, 1536], P(None, 'req'), may hold values from -0.21875 to 0.21875
- w_up: bfloat16 [1536, 3072], P(None, 'req'), may hold values from -0.15625 to 0.15625
- w_down: bfloat16 [3072, 1536], P('req'), may hold values from -0.109375 to 0.109375
- w_out: bfloat16 [1536, 64], replicated, may hold values from -1 to 1
- latent: float32 [8, 1024, 64], P('req', 'seq', 'cfg'), may hold values from -6 to 6
- step_size: float32 [8], P('req'), may hold values from 0.1 to 0.5
Outputs:
- latent_next: float32 [8, 1024, 64], P('req', 'seq', 'cfg')
- guided_norm: float32 [8], P('req')
- peak: float32 [8], P('req')
Inputs may be any that keep to these rules, and one draw needn't show every extreme that they name: `text_len`: some entry equals 154.
All inputs are finite; a program needn't handle non-finite values.
Results may differ from a plain program's by a relative error of at most 0.015.
Values may be sent and summed in bfloat16 or wider, within the bound.
No kernel may reach another device: no remote copies, remote signals or barrier semaphores. Data moves between devices by JAX's collectives and lax.ppermute only.
A program may use at most 64 MiB of HBM per device.

v0:
```python
import jax
import jax.numpy as jnp
from jax import lax
from jax.sharding import PartitionSpec as P

HEADS = 12
HD = 64


guidance_weight = 4.0


def swapped(block, axis, apart):
    count = lax.axis_size(axis)
    route = []
    for low in range(count):
        high = low | 1 << apart
        if high != low and high < count:
            route += [(low, high), (high, low)]
    return lax.ppermute(block, axis, route)


def modulate_rows(hidden, shift_row, scale_row):
    row_mean = jnp.mean(hidden, axis=1, keepdims=True)
    centered = hidden - row_mean
    row_var = jnp.mean(centered * centered, axis=1, keepdims=True)
    return (
        centered * lax.rsqrt(row_var + 1e-06) * (1.0 + scale_row[None, :]) + shift_row[None, :]
    ).astype(jnp.bfloat16)


def per_device(
    query,
    key_value,
    residual_in,
    text_len,
    attn_gate,
    mlp_shift,
    mlp_scale,
    mlp_gate,
    shift,
    scale,
    w_proj,
    w_up,
    w_down,
    w_out,
    latent,
    step_size,
):
    img_dev = query.shape[2]
    rows_dev = key_value.shape[3]
    txt_dev = rows_dev - img_dev
    length = text_len[0, 0]
    queries = query[0, 0].reshape(img_dev, HEADS, HD)
    key_vals = key_value[:, 0, 0]
    factor = HD ** (-0.5)
    piece = lax.all_gather(key_vals, "seq", axis=1, tiled=True)
    running_max = jnp.full((img_dev, HEADS), -1e30, jnp.float32)
    piece_rows = piece.shape[1]
    positions = jnp.arange(piece_rows, dtype=jnp.int32)
    within = positions % rows_dev
    text_slot = positions // rows_dev * txt_dev + within - img_dev
    usable = ((within < img_dev) | (text_slot < length))[None, None, :]
    keys_here = piece[0].reshape(piece_rows, HEADS, HD)
    vals_here = piece[1].reshape(piece_rows, HEADS, HD)
    logits = (
        jnp.einsum("qhd,khd->qhk", queries, keys_here, preferred_element_type=jnp.float32) * factor
    )
    new_max = jnp.maximum(running_max, jnp.max(jnp.where(usable, logits, -1e30), axis=2))
    weights = jnp.where(usable, jnp.exp(logits - new_max[:, :, None]), 0.0)
    running_sum = jnp.sum(weights, axis=2)
    weighted = jnp.einsum(
        "qhk,khd->qhd", weights.astype(jnp.bfloat16), vals_here, preferred_element_type=jnp.float32
    )
    attended = (
        (weighted / running_sum[:, :, None]).reshape(img_dev, HEADS * HD).astype(jnp.bfloat16)
    )
    projected = jnp.dot(
        attended,
        lax.all_gather(w_proj, "req", axis=1, tiled=True),
        preferred_element_type=jnp.float32,
    )
    hidden = residual_in[0, 0].astype(jnp.float32) + attn_gate[0, 0][None, :] * projected
    mlp_in = modulate_rows(hidden, mlp_shift[0, 0], mlp_scale[0, 0])
    inner = jax.nn.gelu(
        jnp.dot(
            lax.all_gather(mlp_in, "req", axis=0, tiled=True),
            w_up,
            preferred_element_type=jnp.float32,
        ),
        approximate=True,
    ).astype(jnp.bfloat16)
    mlp_out = lax.psum_scatter(
        jnp.dot(inner, w_down, preferred_element_type=jnp.float32).astype(jnp.bfloat16),
        "req",
        scatter_dimension=0,
        tiled=True,
    ).astype(jnp.float32)
    hidden_two = hidden + mlp_gate[0, 0][None, :] * mlp_out
    modulated = modulate_rows(hidden_two, shift[0, 0], scale[0, 0])
    velocity = jnp.dot(modulated, w_out, preferred_element_type=jnp.float32)
    half_width = velocity.shape[1] // lax.axis_size("cfg")
    side_index = lax.axis_index("cfg")
    own_half = lax.dynamic_slice_in_dim(velocity, side_index * half_width, half_width, 1)
    other_half = lax.dynamic_slice_in_dim(velocity, (1 - side_index) * half_width, half_width, 1)
    received = swapped(other_half, "cfg", 0)
    is_cond = side_index == 0
    cond_part = jnp.where(is_cond, own_half, received)
    uncond = jnp.where(is_cond, received, own_half)
    guided = uncond + guidance_weight * (cond_part - uncond)
    guided_squares = jnp.sum(guided * guided)
    largest_abs = jnp.max(jnp.abs(guided))
    guided_total = lax.psum(guided_squares, ("cfg", "seq"))
    peak_value = lax.pmax(largest_abs, ("cfg", "seq"))
    entries = img_dev * lax.axis_size("seq") * velocity.shape[1]
    guided_norm = jnp.sqrt(guided_total / entries + 1e-06)
    latent_next = latent + step_size[0] * guided[None, :, :]
    return (latent_next, jnp.reshape(guided_norm, (1,)), jnp.reshape(peak_value, (1,)))


def solution(mesh):
    in_specs = (
        P("cfg", "req", "seq", None),
        P(None, "cfg", "req", "seq", None),
        P("cfg", "req", "seq", None),
        P("cfg", "req"),
        P("cfg", "req", None),
        P("cfg", "req", None),
        P("cfg", "req", None),
        P("cfg", "req", None),
        P("cfg", "req", None),
        P("cfg", "req", None),
        P(None, "req"),
        P(None, "req"),
        P("req", None),
        P(),
        P("req", "seq", "cfg"),
        P("req"),
    )
    out_specs = (P("req", "seq", "cfg"), P("req"), P("req"))
    return jax.shard_map(
        per_device, mesh=mesh, in_specs=in_specs, out_specs=out_specs, check_vma=False
    )
```

profile of v0, /device:TPU:56, one launch (start us, length us, event | category | flops | bytes accessed | tf_op | source)
XLA Modules:
  0.0 663.3 jit_solution(1572826570173849124)
XLA Ops:
  7.2 0.0 copy-start
  7.2 0.0 all-gather.6.cloned.1.call-start
  7.2 0.7 all-gather.6.cloned.1.call-update
  7.9 0.0 all-gather.4.cloned.1.call-start
  8.0 0.7 all-gather.4.cloned.1.call-update
  8.7 0.0 reduce-scatter.2.cloned.1.call-start
  9.4 0.9 reshape_squeeze.10
  10.3 0.7 reduce
  11.0 0.7 reduce.3
  11.8 0.7 add_reduce_fusion.1
  12.5 90.6 %all-gather.6.cloned.1.call-done = bf16[2,1,1,1280,768]{4,3,2,1,0:T(8,128)(2,1)} async-done(((bf16[2,1,1,40,768]{4,3,2,1,0:T(8,128)(2,1)}), bf16[2,1,1,1280,768]{4,3,2,1,0:T(8,128)(2,1)}) %all-gather.6.cloned.1.call-update) | async-done | bytes 3932176 | tf_op jit(solution)/shard_map/all_gather | solution.py:57
  103.0 4.3 fusion.46
  107.3 2.7 copy.22
  110.0 4.0 copy.24
  114.0 0.5 select_reduce_fusion
  114.5 0.0 copy-start.1
  114.6 0.5 fusion.2
  115.0 1.2 copy-done.1
  116.2 0.0 copy-start.3
  116.2 0.7 fusion.5
  117.0 0.1 convert_element_type.34
  117.1 24.9 %all-gather.4.cloned.1.call-done = bf16[768,1536]{0,1:T(8,128)(2,1)} async-done(((bf16[768,192]{0,1:T(8,128)(2,1)}), bf16[768,1536]{0,1:T(8,128)(2,1)}) %all-gather.4.cloned.1.call-update) | async-done | bytes 2359312 | tf_op jit(solution)/shard_map/all_gather | solution.py:80
  142.0 0.0 copy-done.3
  142.0 2.6 fusion.47
  144.5 0.2 multiply_reduce_fusion.1
  144.8 0.1 add_convert_fusion.1
  144.9 16.1 %all_gather.11 = bf16[256,1536]{1,0:T(8,128)(2,1)S(1)} all-gather(bf16[32,1536]{1,0:T(8,128)(2,1)S(1)} %add_convert_fusion.1), channel_id=1, replica_groups=mesh['cfg'=2,'req'=8,'seq'=32] {'req'}, dimensions={0}, use_global_device_ids=true | all-gather | bytes 884736 | tf_op jit(solution)/shard_map/all_gather | solution.py:87
  160.9 0.0 copy-done
  160.9 0.0 copy-start.6
  160.9 0.0 copy-start.7
  160.9 0.0 copy-start.5
  161.0 0.0 copy-start.2
  161.0 3.3 convolution_convert_fusion
  164.3 0.0 copy-start.4
  164.3 0.0 reduce-scatter.2.cloned.1.call-update
  164.3 0.0 copy-done.6
  164.4 0.0 copy-done.7
  164.4 0.0 copy-done.5
  164.4 36.7 %reduce-scatter.2.cloned.1.call-done = bf16[32,1536]{1,0:T(8,128)(2,1)} async-done(((bf16[256,1536]{1,0:T(8,128)(2,1)}), bf16[32,1536]{1,0:T(8,128)(2,1)}) %reduce-scatter.2.cloned.1.call-update) | async-done | bytes 98320 | tf_op jit(solution)/shard_map/reduce_scatter | solution.py:93
  201.1 1.0 fusion.29
  202.2 1.1 multiply_reduce_fusion
  203.3 0.0 copy-done.2
  203.3 1.1 fusion.23
  204.4 0.1 constant_dynamic-slice_fusion
  204.5 4.9 collective-permute-start
  210.0 4.0 collective-permute-done
  214.0 0.7 abs_reduce_fusion
  214.7 224.1 %psum.7 = f32[]{:T(128)} all-reduce(f32[]{:T(128)} %get-tuple-element.4), channel_id=1, replica_groups=mesh['cfg'=2,'req'=8,'seq'=32] {'cfg','seq'}, use_global_device_ids=true, to_apply=%region_8.9 | all-reduce | flops 1 | bytes 8 | tf_op jit(solution)/shard_map/psum | solution.py:113
  439.5 215.5 %pmax.7 = f32[1]{0:T(128)} all-reduce(f32[1]{0:T(128)} %bitcast.9), channel_id=1, replica_groups=mesh['cfg'=2,'req'=8,'seq'=32] {'cfg','seq'}, use_global_device_ids=true, to_apply=%region_10.11 | all-reduce | flops 1 | bytes 8 | tf_op jit(solution)/shard_map/pmax | solution.py:114
  655.0 0.0 copy-done.4
  655.0 0.6 bitcast_add_fusion
  (10 shorter events, 0.2 us)
Async XLA Ops:
  7.2 153.8 %copy-start = (bf16[384,1536]{1,0:T(8,128)(2,1)S(1)}, bf16[384,1536]{1,0:T(8,128)(2,1)}, u32[]{:S(2)}) copy-start(bf16[384,1536]{1,0:T(8,128)(2,1)} %param.28) | copy-start | bytes 3538948
  7.2 95.9 %all-gather.6.cloned.1.call-start = ((), (), s32[]{:S(2)}) async-start(), calls=%async_computation.3 | async-start | bytes 4055040 | tf_op jit(solution)/shard_map/all_gather | solution.py:57
  7.9 134.0 %all-gather.4.cloned.1.call-start = ((), (), s32[]{:S(2)}) async-start(), calls=%async_computation.1 | async-start | bytes 2654208 | tf_op jit(solution)/shard_map/all_gather | solution.py:80
  8.7 192.5 %reduce-scatter.2.cloned.1.call-start = ((), (), s32[]{:S(2)}) async-start(), calls=%async_computation.2 | async-start | bytes 884736 | tf_op jit(solution)/shard_map/reduce_scatter | solution.py:93
  114.5 1.6 copy-start.1
  116.2 25.8 %copy-start.3 = (bf16[1,1,32,1536]{3,2,1,0:T(8,128)(2,1)S(1)}, bf16[1,1,32,1536]{3,2,1,0:T(8,128)(2,1)}, u32[]{:S(2)}) copy-start(bf16[1,1,32,1536]{3,2,1,0:T(8,128)(2,1)} %param.18) | copy-start | bytes 294916
  160.9 3.4 copy-start.6
  160.9 3.4 copy-start.7
  160.9 3.5 copy-start.5
  161.0 42.3 %copy-start.2 = (bf16[1536,64]{0,1:T(8,128)(2,1)S(1)}, bf16[1536,64]{0,1:T(8,128)(2,1)}, u32[]{:S(2)}) copy-start(bf16[1536,64]{0,1:T(8,128)(2,1)} %param.29) | copy-start | bytes 589828
  164.3 490.7 %copy-start.4 = (f32[1,32,32]{2,1,0:T(8,128)S(1)}, f32[1,32,32]{2,1,0:T(8,128)}, u32[]{:S(2)}) copy-start(f32[1,32,32]{2,1,0:T(8,128)} %param.30) | copy-start | bytes 12292
  204.5 9.5 %collective-permute-start = (f32[32,32]{1,0:T(8,128)S(1)}, f32[32,32]{1,0:T(8,128)S(1)}, u32[]{:S(2)}, u32[]{:S(2)}) collective-permute-start(f32[32,32]{1,0:T(8,128)S(1)} %constant_dynamic-slice_fusion), channel_id=1, source_target_pairs={{0,256},{256,0},{1,257},{257,1},{2,258},{258,2},{3,259},{259,3},{4... | collective-permute-start | bytes 12296 | tf_op jit(solution)/shard_map/ppermute | solution.py:20
Sparse Core Ops, SparseCore 0:
  11.2 91.7 all-gather.5
  105.1 36.7 all-gather.3
  164.4 36.6 reduce-scatter.1
where the time goes:
time: 668 us; the launch traced here: 663 us
  blocking collectives  456 us (68%)
  waiting for transfers between devices  157 us (24%)
  between operations  17 us (3%)
  local copies, waits for them, and re-layouts  13.3 us (2%)
  matrix products  8.28 us (1%)
    psum x1, blocking collectives, per_device(): guided_total = lax.psum(guided_squares, ('cfg', 'seq'))  224 us
    pmax x1, blocking collectives, per_device(): peak_value = lax.pmax(largest_abs, ('cfg', 'seq'))  216 us
    all_gather x1, waiting for transfers between devices, per_device(): piece = lax.all_gather(key_vals, 'seq', axis=1, tiled=True)  90.6 us
    reduce_scatter x1, waiting for transfers between devices, per_device(): lax.psum_scatter(jnp.dot(inner, w_down, preferred_element_type=jnp.float3...  36.7 us
    all_gather x1, waiting for transfers between devices, per_device(): lax.all_gather(w_proj, 'req', axis=1, tiled=True)  24.9 us
    all_gather x1, blocking collectives, per_device(): lax.all_gather(mlp_in, 'req', axis=0, tiled=True)  16.1 us
  transfers between devices with their start and end apart: 4, of which 4 were waited for; matrix products, arithmetic and copies ran while one was open for 2% of the time, Pallas kernels for 0%

commit v1 on v0

--- a/solution.py
+++ b/solution.py
@@ -101,19 +101,21 @@
     velocity = jnp.dot(modulated, w_out, preferred_element_type=jnp.float32)
     half_width = velocity.shape[1] // lax.axis_size("cfg")
     side_index = lax.axis_index("cfg")
-    own_half = lax.dynamic_slice_in_dim(velocity, side_index * half_width, half_width, 1)
-    other_half = lax.dynamic_slice_in_dim(velocity, (1 - side_index) * half_width, half_width, 1)
-    received = swapped(other_half, "cfg", 0)
+    received = swapped(velocity, "cfg", 0)
     is_cond = side_index == 0
-    cond_part = jnp.where(is_cond, own_half, received)
-    uncond = jnp.where(is_cond, received, own_half)
-    guided = uncond + guidance_weight * (cond_part - uncond)
-    guided_squares = jnp.sum(guided * guided)
-    largest_abs = jnp.max(jnp.abs(guided))
-    guided_total = lax.psum(guided_squares, ("cfg", "seq"))
-    peak_value = lax.pmax(largest_abs, ("cfg", "seq"))
-    entries = img_dev * lax.axis_size("seq") * velocity.shape[1]
+    cond_part = jnp.where(is_cond, velocity, received)
+    uncond = jnp.where(is_cond, received, velocity)
+    guided_full = uncond + guidance_weight * (cond_part - uncond)
+    partials = jnp.stack([jnp.sum(guided_full * guided_full), jnp.max(jnp.abs(guided_full))])
+    n_seq = lax.axis_size("seq")
+    gathered = lax.all_to_all(
+        jnp.broadcast_to(partials[None], (n_seq, 2)), "seq", 0, 0, tiled=True
+    )
+    guided_total = jnp.sum(gathered[:, 0])
+    peak_value = jnp.max(gathered[:, 1])
+    entries = img_dev * n_seq * velocity.shape[1]
     guided_norm = jnp.sqrt(guided_total / entries + 1e-06)
+    guided = lax.dynamic_slice_in_dim(guided_full, side_index * half_width, half_width, 1)
     latent_next = latent + step_size[0] * guided[None, :, :]
     return (latent_next, jnp.reshape(guided_norm, (1,)), jnp.reshape(peak_value, (1,)))
 

time: 668 us -> 249 us (0.37)
  blocking collectives: 456 us -> 16.1 us
  starting transfers between devices: 5.01 us -> 15.1 us
  waiting for transfers between devices: 157 us -> 166 us
    psum x1 -> x0, blocking collectives: 224 us -> none  [per_device(): guided_total = lax.psum(guided_squares, ('cfg', 'seq'))]
    pmax x1 -> x0, blocking collectives: 216 us -> none  [per_device(): peak_value = lax.pmax(largest_abs, ('cfg', 'seq'))]
    all_to_all x0 -> x1, starting transfers between devices: none -> 10.1 us  [per_device(): lax.all_to_all(jnp.broadcast_to(partials[None], (n_seq, 2)), 'seq', 0, 0,...]
    all_to_all x0 -> x1, waiting for transfers between devices: none -> 8.88 us  [per_device(): lax.all_to_all(jnp.broadcast_to(partials[None], (n_seq, 2)), 'seq', 0, 0,...]
  transfers between devices with their start and end apart: 4 -> 5, of which waited for: 4 -> 5; matrix products, arithmetic and copies ran while one was open for 2% -> 7% of each run, Pallas kernels for 0% -> 0%
where the time goes in v1:
time: 249 us; the launch traced here: 245 us
  waiting for transfers between devices  166 us (67%)
  between operations  17 us (7%)
  blocking collectives  16.1 us (6%)
  starting transfers between devices  15.1 us (6%)
  local copies, waits for them, and re-layouts  13.9 us (6%)
  other arithmetic  8.45 us (3%)
  matrix products  8.28 us (3%)
    all_gather x1, waiting for transfers between devices, per_device(): piece = lax.all_gather(key_vals, 'seq', axis=1, tiled=True)  90.6 us
    reduce_scatter x1, waiting for transfers between devices, per_device(): lax.psum_scatter(jnp.dot(inner, w_down, preferred_element_type=jnp.float3...  36.7 us
    all_gather x1, waiting for transfers between devices, per_device(): lax.all_gather(w_proj, 'req', axis=1, tiled=True)  24.9 us
    all_gather x1, blocking collectives, per_device(): lax.all_gather(mlp_in, 'req', axis=0, tiled=True)  16.1 us
    all_to_all x1, starting transfers between devices, per_device(): lax.all_to_all(jnp.broadcast_to(partials[None], (n_seq, 2)), 'seq', 0, 0,...  10.1 us
    all_to_all x1, waiting for transfers between devices, per_device(): lax.all_to_all(jnp.broadcast_to(partials[None], (n_seq, 2)), 'seq', 0, 0,...  8.88 us
    slice x2, local copies, waits for them, and re-layouts, per_device(): keys_here = piece[0].reshape(piece_rows, HEADS, HD)  6.95 us
  transfers between devices with their start and end apart: 5, of which 5 were waited for; matrix products, arithmetic and copies ran while one was open for 7% of the time, Pallas kernels for 0%

profile of v1, /device:TPU:56, one launch (start us, length us, event | category | flops | bytes accessed | tf_op | source)
XLA Modules:
  0.0 245.2 jit_solution(4121349338983233270)
XLA Ops:
  7.2 0.0 copy-start
  7.2 0.0 all-gather.6.cloned.1.call-start
  7.2 0.7 all-gather.6.cloned.1.call-update
  7.9 0.0 all-gather.4.cloned.1.call-start
  8.0 0.7 all-gather.4.cloned.1.call-update
  8.7 0.0 reduce-scatter.2.cloned.1.call-start
  9.4 0.9 reshape_squeeze.10
  10.3 0.7 reduce.2
  11.0 0.7 reduce.5
  11.8 0.7 add_reduce_fusion.1
  12.5 90.6 %all-gather.6.cloned.1.call-done = bf16[2,1,1,1280,768]{4,3,2,1,0:T(8,128)(2,1)} async-done(((bf16[2,1,1,40,768]{4,3,2,1,0:T(8,128)(2,1)}), bf16[2,1,1,1280,768]{4,3,2,1,0:T(8,128)(2,1)}) %all-gather.6.cloned.1.call-update) | async-done | bytes 3932176 | tf_op jit(solution)/shard_map/all_gather | solution.py:57
  103.0 4.3 %fusion.46 = (bf16[1,1,1,1280,768]{4,3,2,1,0:T(8,128)(2,1)}, bf16[1,1,1,1280,768]{4,3,2,1,0:T(8,128)(2,1)}) fusion(bf16[2,1,1,1280,768]{4,3,2,1,0:T(8,128)(2,1)} %all-gather.6.cloned.1.call-done), kind=kLoop, calls=%fused_computation.75 | loop fusion | bytes 7864320 | tf_op jit(solution)/shard_map/slice | solution.py:64
  107.3 2.7 %copy.26 = bf16[1,1,1,1280,768]{3,4,2,1,0:T(8,128)(2,1)S(1)} copy(bf16[1,1,1,1280,768]{4,3,2,1,0:T(8,128)(2,1)} %get-tuple-element.8) | data formatting | bytes 3932160 | tf_op jit(solution)/shard_map/slice | solution.py:64
  110.0 4.0 %copy.28 = bf16[1,1,1,1280,768]{3,4,2,1,0:T(8,128)(2,1)} copy(bf16[1,1,1,1280,768]{4,3,2,1,0:T(8,128)(2,1)} %get-tuple-element.9) | data formatting | bytes 3932160 | tf_op jit(solution)/shard_map/slice | solution.py:65
  114.0 0.5 select_reduce_fusion
  114.5 0.0 copy-start.1
  114.6 0.5 fusion.2
  115.0 1.2 copy-done.1
  116.2 0.0 copy-start.3
  116.2 0.7 fusion.5
  117.0 0.1 convert_element_type.34
  117.1 24.9 %all-gather.4.cloned.1.call-done = bf16[768,1536]{0,1:T(8,128)(2,1)} async-done(((bf16[768,192]{0,1:T(8,128)(2,1)}), bf16[768,1536]{0,1:T(8,128)(2,1)}) %all-gather.4.cloned.1.call-update) | async-done | bytes 2359312 | tf_op jit(solution)/shard_map/all_gather | solution.py:80
  142.0 0.0 copy-done.3
  142.0 2.6 %fusion.47 = (f32[32]{0:T(128)S(1)}, f32[32,1536]{1,0:T(8,128)S(1)}) fusion(bf16[32,768]{1,0:T(8,128)(2,1)S(1)} %convert_element_type.34, bf16[768,1536]{0,1:T(8,128)(2,1)} %all-gather.4.cloned.1.call-done, f32[1536]{0:T(1024)S(1)} %reduce.2, bf16[1,1,32,1536]{3,2,1,0:T(8,128)(2,1)S(1)} %copy-done.3), kind=kOutput, calls=%fused_computation.76 | convolution fusion | flops 75694048 | bytes 2709632 | tf_op jit(solution)/shard_map/dot_general | solution.py:78
  144.5 0.2 multiply_reduce_fusion.1
  144.8 0.1 add_convert_fusion.1
  144.9 16.1 %all_gather.11 = bf16[256,1536]{1,0:T(8,128)(2,1)S(1)} all-gather(bf16[32,1536]{1,0:T(8,128)(2,1)S(1)} %add_convert_fusion.1), channel_id=1, replica_groups=mesh['cfg'=2,'req'=8,'seq'=32] {'req'}, dimensions={0}, use_global_device_ids=true | all-gather | bytes 884736 | tf_op jit(solution)/shard_map/all_gather | solution.py:87
  160.9 0.0 copy-done
  160.9 0.0 copy-start.6
  160.9 0.0 copy-start.7
  160.9 0.0 copy-start.5
  161.0 0.0 copy-start.2
  161.0 3.3 %convolution_convert_fusion = bf16[256,1536]{1,0:T(8,128)(2,1)} fusion(bf16[384,1536]{1,0:T(8,128)(2,1)S(1)} %copy-done, bf16[256,1536]{1,0:T(8,128)(2,1)S(1)} %all_gather.11, bf16[1536,384]{1,0:T(8,128)(2,1)} %param.27), kind=kOutput, calls=%fused_computation.2 | convolution fusion | flops 605257728 | bytes 3932160 | tf_op jit(solution)/shard_map/dot_general | solution.py:94
  164.3 0.0 copy-start.4
  164.3 0.0 reduce-scatter.2.cloned.1.call-update
  164.3 0.0 copy-done.6
  164.3 0.0 copy-done.7
  164.4 0.0 copy-done.5
  164.4 36.7 %reduce-scatter.2.cloned.1.call-done = bf16[32,1536]{1,0:T(8,128)(2,1)} async-done(((bf16[256,1536]{1,0:T(8,128)(2,1)}), bf16[32,1536]{1,0:T(8,128)(2,1)}) %reduce-scatter.2.cloned.1.call-update) | async-done | bytes 98320 | tf_op jit(solution)/shard_map/reduce_scatter | solution.py:93
  201.1 1.0 fusion.29
  202.2 1.1 multiply_reduce_fusion
  203.3 0.0 copy-done.2
  203.3 1.1 fusion.23
  204.4 4.9 %collective-permute-start = (f32[32,64]{1,0:T(8,128)S(1)}, f32[32,64]{1,0:T(8,128)S(1)}, u32[]{:S(2)}, u32[]{:S(2)}) collective-permute-start(f32[32,64]{1,0:T(8,128)S(1)} %fusion.23), channel_id=1, source_target_pairs={{0,256},{256,0},{1,257},{257,1},{2,258},{258,2},{3,259},{259,3},{4... | collective-permute-start | bytes 24584 | tf_op jit(solution)/shard_map/ppermute | solution.py:20
  210.0 4.0 %collective-permute-done = f32[32,64]{1,0:T(8,128)S(1)} collective-permute-done((f32[32,64]{1,0:T(8,128)S(1)}, f32[32,64]{1,0:T(8,128)S(1)}, u32[]{:S(2)}, u32[]{:S(2)}) %collective-permute-start) | collective-permute-done | bytes 8224 | tf_op jit(solution)/shard_map/ppermute | solution.py:20
  213.9 0.6 multiply_reduce_fusion.2
  214.5 1.4 pad_maximum_fusion
  215.9 0.6 broadcast_in_dim.39
  216.5 10.1 %all-to-all-start = ((f32[32,1,2]{2,1,0:T(1,128)}), f32[32,1,2]{2,1,0:T(1,128)S(1)}, u32[]{:S(2)}, u32[]{:S(2)}) async-start(f32[32,1,2]{2,1,0:T(1,128)} %broadcast_in_dim.39), calls=%async_computation.1 | async-start | bytes 32768 | tf_op jit(solution)/shard_map/all_to_all | solution.py:111
  226.6 0.0 copy-done.4
  226.6 0.7 bitcast_add_fusion
  227.3 8.9 %all-to-all-done = f32[32,1,2]{2,1,0:T(1,128)S(1)} async-done(((f32[32,1,2]{2,1,0:T(1,128)}), f32[32,1,2]{2,1,0:T(1,128)S(1)}, u32[]{:S(2)}, u32[]{:S(2)}) %all-to-all-start) | async-done | bytes 288 | tf_op jit(solution)/shard_map/all_to_all | solution.py:111
  236.2 0.1 copy.30
  236.3 0.6 slice_reduce_fusion
  (10 shorter events, 0.2 us)
Async XLA Ops:
  7.2 153.8 %copy-start = (bf16[384,1536]{1,0:T(8,128)(2,1)S(1)}, bf16[384,1536]{1,0:T(8,128)(2,1)}, u32[]{:S(2)}) copy-start(bf16[384,1536]{1,0:T(8,128)(2,1)} %param.28) | copy-start | bytes 3538948
  7.2 95.9 %all-gather.6.cloned.1.call-start = ((), (), s32[]{:S(2)}) async-start(), calls=%async_computation.4 | async-start | bytes 4055040 | tf_op jit(solution)/shard_map/all_gather | solution.py:57
  7.9 134.0 %all-gather.4.cloned.1.call-start = ((), (), s32[]{:S(2)}) async-start(), calls=%async_computation.2 | async-start | bytes 2654208 | tf_op jit(solution)/shard_map/all_gather | solution.py:80
  8.7 192.5 %reduce-scatter.2.cloned.1.call-start = ((), (), s32[]{:S(2)}) async-start(), calls=%async_computation.3 | async-start | bytes 884736 | tf_op jit(solution)/shard_map/reduce_scatter | solution.py:93
  114.5 1.6 copy-start.1
  116.2 25.8 %copy-start.3 = (bf16[1,1,32,1536]{3,2,1,0:T(8,128)(2,1)S(1)}, bf16[1,1,32,1536]{3,2,1,0:T(8,128)(2,1)}, u32[]{:S(2)}) copy-start(bf16[1,1,32,1536]{3,2,1,0:T(8,128)(2,1)} %param.18) | copy-start | bytes 294916
  160.9 3.4 %copy-start.6 = (f32[1,1,1536]{2,1,0:T(1,128)S(1)}, f32[1,1,1536]{2,1,0:T(1,128)}, u32[]{:S(2)}) copy-start(f32[1,1,1536]{2,1,0:T(1,128)} %param.23) | copy-start | bytes 18436
  160.9 3.4 %copy-start.7 = (f32[1,1,1536]{2,1,0:T(1,128)S(1)}, f32[1,1,1536]{2,1,0:T(1,128)}, u32[]{:S(2)}) copy-start(f32[1,1,1536]{2,1,0:T(1,128)} %param.24) | copy-start | bytes 18436
  160.9 3.4 %copy-start.5 = (f32[1,1,1536]{2,1,0:T(1,128)S(1)}, f32[1,1,1536]{2,1,0:T(1,128)}, u32[]{:S(2)}) copy-start(f32[1,1,1536]{2,1,0:T(1,128)} %param.25) | copy-start | bytes 18436
  161.0 42.3 %copy-start.2 = (bf16[1536,64]{0,1:T(8,128)(2,1)S(1)}, bf16[1536,64]{0,1:T(8,128)(2,1)}, u32[]{:S(2)}) copy-start(bf16[1536,64]{0,1:T(8,128)(2,1)} %param.29) | copy-start | bytes 589828
  164.3 62.3 %copy-start.4 = (f32[1,32,32]{2,1,0:T(8,128)S(1)}, f32[1,32,32]{2,1,0:T(8,128)}, u32[]{:S(2)}) copy-start(f32[1,32,32]{2,1,0:T(8,128)} %param.30) | copy-start | bytes 12292
  204.4 9.5 %collective-permute-start = (f32[32,64]{1,0:T(8,128)S(1)}, f32[32,64]{1,0:T(8,128)S(1)}, u32[]{:S(2)}, u32[]{:S(2)}) collective-permute-start(f32[32,64]{1,0:T(8,128)S(1)} %fusion.23), channel_id=1, source_target_pairs={{0,256},{256,0},{1,257},{257,1},{2,258},{258,2},{3,259},{259,3},{4... | collective-permute-start | bytes 24584 | tf_op jit(solution)/shard_map/ppermute | solution.py:20
  216.5 19.7 %all-to-all-start = ((f32[32,1,2]{2,1,0:T(1,128)}), f32[32,1,2]{2,1,0:T(1,128)S(1)}, u32[]{:S(2)}, u32[]{:S(2)}) async-start(f32[32,1,2]{2,1,0:T(1,128)} %broadcast_in_dim.39), calls=%async_computation.1 | async-start | bytes 32768 | tf_op jit(solution)/shard_map/all_to_all | solution.py:111
Sparse Core Ops, SparseCore 0:
  11.2 91.7 all-gather.5
  105.1 36.7 all-gather.3
  164.4 36.6 reduce-scatter.1

commit v2 on v1

--- a/solution.py
+++ b/solution.py
@@ -75,11 +75,13 @@
     attended = (
         (weighted / running_sum[:, :, None]).reshape(img_dev, HEADS * HD).astype(jnp.bfloat16)
     )
-    projected = jnp.dot(
-        attended,
-        lax.all_gather(w_proj, "req", axis=1, tiled=True),
-        preferred_element_type=jnp.float32,
+    n_req = lax.axis_size("req")
+    proj_blocks = lax.all_to_all(
+        jnp.broadcast_to(w_proj[None], (n_req,) + w_proj.shape), "req", 0, 0, tiled=True
     )
+    projected = jnp.einsum(
+        "tk,ikc->tic", attended, proj_blocks, preferred_element_type=jnp.float32
+    ).reshape(img_dev, n_req * w_proj.shape[1])
     hidden = residual_in[0, 0].astype(jnp.float32) + attn_gate[0, 0][None, :] * projected
     mlp_in = modulate_rows(hidden, mlp_shift[0, 0], mlp_scale[0, 0])
     inner = jax.nn.gelu(
@@ -90,12 +92,14 @@
         ),
         approximate=True,
     ).astype(jnp.bfloat16)
-    mlp_out = lax.psum_scatter(
-        jnp.dot(inner, w_down, preferred_element_type=jnp.float32).astype(jnp.bfloat16),
-        "req",
-        scatter_dimension=0,
-        tiled=True,
-    ).astype(jnp.float32)
+    mlp_parts = (
+        jnp.dot(inner, w_down, preferred_element_type=jnp.float32)
+        .astype(jnp.bfloat16)
+        .reshape(n_req, img_dev, w_down.shape[1])
+    )
+    mlp_out = jnp.sum(
+        lax.all_to_all(mlp_parts, "req", 0, 0, tiled=True).astype(jnp.float32), axis=0
+    )
     hidden_two = hidden + mlp_gate[0, 0][None, :] * mlp_out
     modulated = modulate_rows(hidden_two, shift[0, 0], scale[0, 0])
     velocity = jnp.dot(modulated, w_out, preferred_element_type=jnp.float32)

time: 249 us -> 207 us (0.83); the launches traced: 245 us -> 206 us
  waiting for transfers between devices: 166 us -> 114 us
  local copies, waits for them, and re-layouts: 13.9 us -> 21 us
  starting transfers between devices: 15.1 us -> 21.7 us
    reduce_scatter x1 -> x0, waiting for transfers between devices: 36.7 us -> none  [per_device(): lax.psum_scatter(jnp.dot(inner, w_down, preferred_element_type=jnp.float3...]
    all_gather x1 -> x0, waiting for transfers between devices: 24.9 us -> none  [per_device(): lax.all_gather(w_proj, 'req', axis=1, tiled=True)]
    all_to_all x0 -> x2, waiting for transfers between devices: none -> 18.3 us  [the longest x1 18.3 us: per_device(): lax.all_to_all(mlp_parts, 'req', 0, 0, tiled=True).astype(jnp.float32)]
    all_to_all x0 -> x2, starting transfers between devices: none -> 12.9 us  [the longest x1 6.6 us: per_device(): lax.all_to_all(jnp.broadcast_to(w_proj[None], (n_req,) + w_proj.shape), '...]
    all_gather x1, waiting for transfers between devices: 90.6 us -> 81.1 us  [per_device(): piece = lax.all_gather(key_vals, 'seq', axis=1, tiled=True)]
    all_to_all x1, starting transfers between devices: 10.1 us -> 5.18 us  [per_device(): lax.all_to_all(jnp.broadcast_to(partials[None], (n_seq, 2)), 'seq', 0, 0,...]
    broadcast_in_dim x0 -> x1, local copies, waits for them, and re-layouts: none -> 2.53 us  [per_device(): jnp.broadcast_to(w_proj[None], (n_req,) + w_proj.shape)]
  transfers between devices with their start and end apart: 5 -> 5, of which waited for: 5 -> 4; matrix products, arithmetic and copies ran while one was open for 7% -> 12% of each run, Pallas kernels for 0% -> 0%
where the time goes in v2:
time: 207 us; the launch traced here: 206 us
  waiting for transfers between devices  114 us (55%)
  starting transfers between devices  21.7 us (10%)
  local copies, waits for them, and re-layouts  21 us (10%)
  between operations  17.3 us (8%)
  blocking collectives  16.2 us (8%)
  matrix products  8.19 us (4%)
  other arithmetic  7.25 us (4%)
    all_gather x1, waiting for transfers between devices, per_device(): piece = lax.all_gather(key_vals, 'seq', axis=1, tiled=True)  81.1 us
    all_to_all x1, waiting for transfers between devices, per_device(): lax.all_to_all(mlp_parts, 'req', 0, 0, tiled=True).astype(jnp.float32)  18.3 us
    all_gather x1, blocking collectives, per_device(): lax.all_gather(mlp_in, 'req', axis=0, tiled=True)  16.2 us
    all_to_all x1, waiting for transfers between devices, per_device(): lax.all_to_all(jnp.broadcast_to(partials[None], (n_seq, 2)), 'seq', 0, 0,...  8.88 us
    slice x2, local copies, waits for them, and re-layouts, per_device(): keys_here = piece[0].reshape(piece_rows, HEADS, HD)  8.3 us
    all_to_all x1, starting transfers between devices, per_device(): lax.all_to_all(jnp.broadcast_to(w_proj[None], (n_req,) + w_proj.shape), '...  6.6 us
    all_to_all x1, starting transfers between devices, per_device(): lax.all_to_all(mlp_parts, 'req', 0, 0, tiled=True).astype(jnp.float32)  6.35 us
    ppermute x1, waiting for transfers between devices, swapped(): return lax.ppermute(block, axis, route)  5.36 us
  transfers between devices with their start and end apart: 5, of which 4 were waited for; matrix products, arithmetic and copies ran while one was open for 12% of the time, Pallas kernels for 0%

profile of v2, /device:TPU:56, one launch (start us, length us, event | category | flops | bytes accessed | tf_op | source)
XLA Modules:
  0.0 206.0 jit_solution(4310385584668401171)
XLA Ops:
  7.2 0.0 copy-start
  7.2 0.0 all-gather.3.cloned.1.call-start
  7.2 0.7 all-gather.3.cloned.1.call-update
  7.9 2.5 %broadcast_in_dim.45 = bf16[8,768,192]{1,2,0:T(8,128)(2,1)} broadcast(bf16[768,192]{0,1:T(8,128)(2,1)} %param.26), dimensions={1,2} | broadcast | bytes 2654208 | tf_op jit(solution)/shard_map/broadcast_in_dim | solution.py:80
  10.4 0.0 copy-start.9
  10.4 6.6 %all-to-all-start = ((bf16[8,768,192]{1,2,0:T(8,128)(2,1)}), bf16[8,768,192]{1,2,0:T(8,128)(2,1)S(1)}, u32[]{:S(2)}, u32[]{:S(2)}) async-start(bf16[8,768,192]{1,2,0:T(8,128)(2,1)} %broadcast_in_dim.45), calls=%async_computation | async-start | bytes 4718592 | tf_op jit(solution)/shard_map/all_to_all | solution.py:79
  17.7 1.6 reshape_squeeze.10
  19.3 0.0 copy-done.9
  19.3 1.3 reduce.5
  20.6 0.6 fusion.39
  21.2 0.7 add_reduce_fusion.1
  22.0 81.1 %all-gather.3.cloned.1.call-done = bf16[2,1,1,1280,768]{4,3,2,1,0:T(8,128)(2,1)} async-done(((bf16[2,1,1,40,768]{4,3,2,1,0:T(8,128)(2,1)}), bf16[2,1,1,1280,768]{4,3,2,1,0:T(8,128)(2,1)}) %all-gather.3.cloned.1.call-update) | async-done | bytes 3932176 | tf_op jit(solution)/shard_map/all_gather | solution.py:57
  103.1 4.3 %fusion.46 = (bf16[1,1,1,1280,768]{4,3,2,1,0:T(8,128)(2,1)}, bf16[1,1,1,1280,768]{4,3,2,1,0:T(8,128)(2,1)}) fusion(bf16[2,1,1,1280,768]{4,3,2,1,0:T(8,128)(2,1)} %all-gather.3.cloned.1.call-done), kind=kLoop, calls=%fused_computation.76 | loop fusion | bytes 7864320 | tf_op jit(solution)/shard_map/slice | solution.py:64
  107.4 4.0 %copy.29 = bf16[1,1,1,1280,768]{3,4,2,1,0:T(8,128)(2,1)} copy(bf16[1,1,1,1280,768]{4,3,2,1,0:T(8,128)(2,1)} %get-tuple-element.11) | data formatting | bytes 3932160 | tf_op jit(solution)/shard_map/slice | solution.py:65
  111.4 4.0 %copy.27 = bf16[1,1,1,1280,768]{3,4,2,1,0:T(8,128)(2,1)} copy(bf16[1,1,1,1280,768]{4,3,2,1,0:T(8,128)(2,1)} %get-tuple-element.10) | data formatting | bytes 3932160 | tf_op jit(solution)/shard_map/slice | solution.py:64
  115.4 0.0 copy-start.6
  115.4 2.1 %select_reduce_fusion = (f32[32,12]{0,1:T(8,128)S(1)}, f32[32,12,1280]{2,0,1:T(8,128)S(1)}) fusion(pred[1280]{0:T(1024)(128)(4,1)} %fusion.39, bf16[1280,12,64]{0,2,1:T(8,128)(2,1)} %bitcast.39, bf16[32,12,64]{2,1,0:T(8,128)(2,1)} %reshape_squeeze.10), kind=kOutput, calls=%fused_computation.6 | convolution fusion | flops 64388736 | bytes 3984128 | tf_op jit(solution)/shard_map/qhd,khd->qhk/dot_general | solution.py:67
  117.5 0.0 copy-start.3
  117.5 0.0 copy-done.6
  117.5 0.5 fusion.2
  118.0 1.1 copy-done.3
  119.1 0.7 fusion.5
  119.8 0.7 copy.30
  120.5 1.6 convert_element_type.34
  122.1 0.0 all-to-all-done
  122.1 0.0 copy-start.5
  122.1 1.8 fusion.47
  124.0 0.0 copy-start.1
  124.0 0.2 multiply_reduce_fusion.1
  124.2 0.5 copy-done.1
  124.6 0.0 copy-done.5
  124.6 0.1 add_convert_fusion.1
  124.8 16.2 %all_gather.7 = bf16[256,1536]{1,0:T(8,128)(2,1)S(1)} all-gather(bf16[32,1536]{1,0:T(8,128)(2,1)S(1)} %add_convert_fusion.1), channel_id=1, replica_groups=mesh['cfg'=2,'req'=8,'seq'=32] {'req'}, dimensions={0}, use_global_device_ids=true | all-gather | bytes 884736 | tf_op jit(solution)/shard_map/all_gather | solution.py:89
  140.9 0.0 copy-done
  140.9 0.0 copy-start.10
  140.9 0.0 copy-start.11
  140.9 0.0 copy-start.8
  140.9 3.3 %convolution_convert_fusion = bf16[256,1536]{1,0:T(8,128)(2,1)} fusion(bf16[384,1536]{1,0:T(8,128)(2,1)S(1)} %copy-done, bf16[256,1536]{1,0:T(8,128)(2,1)S(1)} %all_gather.7, bf16[1536,384]{1,0:T(8,128)(2,1)} %param.27), kind=kOutput, calls=%fused_computation.2 | convolution fusion | flops 605257728 | bytes 3932160 | tf_op jit(solution)/shard_map/dot_general | solution.py:96
  144.2 0.0 copy-start.2
  144.2 0.0 copy-start.4
  144.2 0.0 copy-start.7
  144.2 6.3 %all-to-all-start.1 = ((bf16[8,32,1536]{2,1,0:T(8,128)(2,1)}), bf16[8,32,1536]{2,1,0:T(8,128)(2,1)S(1)}, u32[]{:S(2)}, u32[]{:S(2)}) async-start(bf16[8,32,1536]{2,1,0:T(8,128)(2,1)} %bitcast.9), calls=%async_computation.1 | async-start | bytes 1572864 | tf_op jit(solution)/shard_map/all_to_all | solution.py:101
  150.6 0.0 copy-done.10
  150.6 0.0 copy-done.11
  150.7 0.0 copy-done.8
  150.7 18.3 %all-to-all-done.1 = bf16[8,32,1536]{2,1,0:T(8,128)(2,1)S(1)} async-done(((bf16[8,32,1536]{2,1,0:T(8,128)(2,1)}), bf16[8,32,1536]{2,1,0:T(8,128)(2,1)S(1)}, u32[]{:S(2)}, u32[]{:S(2)}) %all-to-all-start.1) | async-done | bytes 786464 | tf_op jit(solution)/shard_map/all_to_all | solution.py:101
  169.0 0.1 convert_reduce_fusion
  169.1 0.0 copy-done.2
  169.1 0.1 fusion.45
  169.2 0.2 multiply_reduce_fusion
  169.5 0.0 copy-done.4
  169.5 0.2 fusion.23
  169.7 3.5 %collective-permute-start = (f32[32,64]{1,0:T(8,128)S(1)}, f32[32,64]{1,0:T(8,128)S(1)}, u32[]{:S(2)}, u32[]{:S(2)}) collective-permute-start(f32[32,64]{1,0:T(8,128)S(1)} %fusion.23), channel_id=1, source_target_pairs={{0,256},{256,0},{1,257},{257,1},{2,258},{258,2},{3,259},{259,3},{4... | collective-permute-start | bytes 24584 | tf_op jit(solution)/shard_map/ppermute | solution.py:20
  173.9 5.4 %collective-permute-done = f32[32,64]{1,0:T(8,128)S(1)} collective-permute-done((f32[32,64]{1,0:T(8,128)S(1)}, f32[32,64]{1,0:T(8,128)S(1)}, u32[]{:S(2)}, u32[]{:S(2)}) %collective-permute-start) | collective-permute-done | bytes 8224 | tf_op jit(solution)/shard_map/ppermute | solution.py:20
  179.2 0.6 multiply_reduce_fusion.2
  179.9 1.4 pad_maximum_fusion
  181.2 0.6 broadcast_in_dim.46
  181.8 5.2 %all-to-all-start.2 = ((f32[32,1,2]{2,1,0:T(1,128)}), f32[32,1,2]{2,1,0:T(1,128)S(1)}, u32[]{:S(2)}, u32[]{:S(2)}) async-start(f32[32,1,2]{2,1,0:T(1,128)} %broadcast_in_dim.46), calls=%async_computation.2 | async-start | bytes 32768 | tf_op jit(solution)/shard_map/all_to_all | solution.py:115
  187.0 0.0 copy-done.7
  187.0 0.7 bitcast_add_fusion
  187.7 8.9 %all-to-all-done.2 = f32[32,1,2]{2,1,0:T(1,128)S(1)} async-done(((f32[32,1,2]{2,1,0:T(1,128)}), f32[32,1,2]{2,1,0:T(1,128)S(1)}, u32[]{:S(2)}, u32[]{:S(2)}) %all-to-all-start.2) | async-done | bytes 288 | tf_op jit(solution)/shard_map/all_to_all | solution.py:115
  196.6 0.1 copy.31
  196.7 0.6 slice_reduce_fusion
  (9 shorter events, 0.1 us)
Async XLA Ops:
  7.2 133.8 %copy-start = (bf16[384,1536]{1,0:T(8,128)(2,1)S(1)}, bf16[384,1536]{1,0:T(8,128)(2,1)}, u32[]{:S(2)}) copy-start(bf16[384,1536]{1,0:T(8,128)(2,1)} %param.28) | copy-start | bytes 3538948
  7.2 95.9 %all-gather.3.cloned.1.call-start = ((), (), s32[]{:S(2)}) async-start(), calls=%async_computation.3 | async-start | bytes 4055040 | tf_op jit(solution)/shard_map/all_gather | solution.py:57
  10.4 8.9 %copy-start.9 = (f32[1,1,1536]{2,1,0:T(1,128)S(1)}, f32[1,1,1536]{2,1,0:T(1,128)}, u32[]{:S(2)}) copy-start(f32[1,1,1536]{2,1,0:T(1,128)} %param.20) | copy-start | bytes 18436
  10.4 111.7 %all-to-all-start = ((bf16[8,768,192]{1,2,0:T(8,128)(2,1)}), bf16[8,768,192]{1,2,0:T(8,128)(2,1)S(1)}, u32[]{:S(2)}, u32[]{:S(2)}) async-start(bf16[8,768,192]{1,2,0:T(8,128)(2,1)} %broadcast_in_dim.45), calls=%async_computation | async-start | bytes 4718592 | tf_op jit(solution)/shard_map/all_to_all | solution.py:79
  115.4 2.1 %copy-start.6 = (pred[1280]{0:T(1024)(128)(4,1)S(1)}, pred[1280]{0:T(1024)(128)(4,1)}, u32[]{:S(2)}) copy-start(pred[1280]{0:T(1024)(128)(4,1)} %fusion.39) | copy-start | bytes 3844
  117.5 1.6 copy-start.3
  122.1 2.5 %copy-start.5 = (f32[1536]{0:T(1024)S(1)}, f32[1536]{0:T(1024)}, u32[]{:S(2)}) copy-start(f32[1536]{0:T(1024)} %reduce.5) | copy-start | bytes 18436
  124.0 0.7 copy-start.1
  140.9 9.7 %copy-start.10 = (f32[1,1,1536]{2,1,0:T(1,128)S(1)}, f32[1,1,1536]{2,1,0:T(1,128)}, u32[]{:S(2)}) copy-start(f32[1,1,1536]{2,1,0:T(1,128)} %param.23) | copy-start | bytes 18436
  140.9 9.7 %copy-start.11 = (f32[1,1,1536]{2,1,0:T(1,128)S(1)}, f32[1,1,1536]{2,1,0:T(1,128)}, u32[]{:S(2)}) copy-start(f32[1,1,1536]{2,1,0:T(1,128)} %param.24) | copy-start | bytes 18436
  140.9 9.7 %copy-start.8 = (f32[1,1,1536]{2,1,0:T(1,128)S(1)}, f32[1,1,1536]{2,1,0:T(1,128)}, u32[]{:S(2)}) copy-start(f32[1,1,1536]{2,1,0:T(1,128)} %param.25) | copy-start | bytes 18436
  144.2 24.9 %copy-start.2 = (f32[32,1536]{1,0:T(8,128)S(1)}, f32[32,1536]{1,0:T(8,128)}, u32[]{:S(2)}) copy-start(f32[32,1536]{1,0:T(8,128)} %copy-done.1) | copy-start | bytes 589828
  144.2 25.2 %copy-start.4 = (bf16[1536,64]{0,1:T(8,128)(2,1)S(1)}, bf16[1536,64]{0,1:T(8,128)(2,1)}, u32[]{:S(2)}) copy-start(bf16[1536,64]{0,1:T(8,128)(2,1)} %param.29) | copy-start | bytes 589828
  144.2 42.8 %copy-start.7 = (f32[1,32,32]{2,1,0:T(8,128)S(1)}, f32[1,32,32]{2,1,0:T(8,128)}, u32[]{:S(2)}) copy-start(f32[1,32,32]{2,1,0:T(8,128)} %param.30) | copy-start | bytes 12292
  144.2 24.7 %all-to-all-start.1 = ((bf16[8,32,1536]{2,1,0:T(8,128)(2,1)}), bf16[8,32,1536]{2,1,0:T(8,128)(2,1)S(1)}, u32[]{:S(2)}, u32[]{:S(2)}) async-start(bf16[8,32,1536]{2,1,0:T(8,128)(2,1)} %bitcast.9), calls=%async_computation.1 | async-start | bytes 1572864 | tf_op jit(solution)/shard_map/all_to_all | solution.py:101
  169.7 9.5 %collective-permute-start = (f32[32,64]{1,0:T(8,128)S(1)}, f32[32,64]{1,0:T(8,128)S(1)}, u32[]{:S(2)}, u32[]{:S(2)}) collective-permute-start(f32[32,64]{1,0:T(8,128)S(1)} %fusion.23), channel_id=1, source_target_pairs={{0,256},{256,0},{1,257},{257,1},{2,258},{258,2},{3,259},{259,3},{4... | collective-permute-start | bytes 24584 | tf_op jit(solution)/shard_map/ppermute | solution.py:20
  181.8 14.8 %all-to-all-start.2 = ((f32[32,1,2]{2,1,0:T(1,128)}), f32[32,1,2]{2,1,0:T(1,128)S(1)}, u32[]{:S(2)}, u32[]{:S(2)}) async-start(f32[32,1,2]{2,1,0:T(1,128)} %broadcast_in_dim.46), calls=%async_computation.2 | async-start | bytes 32768 | tf_op jit(solution)/shard_map/all_to_all | solution.py:115
Sparse Core Ops, SparseCore 0:
  11.2 91.8 all-gather.2

commit v3 on v2

--- a/solution.py
+++ b/solution.py
@@ -1,10 +1,11 @@
 import jax
 import jax.numpy as jnp
 from jax import lax
-from jax.sharding import PartitionSpec as P
+from jax.sharding import Mesh, PartitionSpec as P
 
 HEADS = 12
 HD = 64
+SEQ_MINOR = 4
 
 
 guidance_weight = 4.0
@@ -51,37 +52,49 @@
     rows_dev = key_value.shape[3]
     txt_dev = rows_dev - img_dev
     length = text_len[0, 0]
-    queries = query[0, 0].reshape(img_dev, HEADS, HD)
-    key_vals = key_value[:, 0, 0]
     factor = HD ** (-0.5)
-    piece = lax.all_gather(key_vals, "seq", axis=1, tiled=True)
-    running_max = jnp.full((img_dev, HEADS), -1e30, jnp.float32)
+    n_x = lax.axis_size("sx")
+    x_index = lax.axis_index("sx")
+    query_rows = lax.all_gather(query[0, 0], "sx", axis=0, tiled=True)
+    piece = lax.all_gather(key_value[:, 0, 0], "sz", axis=1, tiled=True)
+    q_rows = query_rows.shape[0]
     piece_rows = piece.shape[1]
     positions = jnp.arange(piece_rows, dtype=jnp.int32)
     within = positions % rows_dev
-    text_slot = positions // rows_dev * txt_dev + within - img_dev
+    source = (positions // rows_dev) * n_x + x_index
+    text_slot = source * txt_dev + within - img_dev
     usable = ((within < img_dev) | (text_slot < length))[None, None, :]
+    queries = query_rows.reshape(q_rows, HEADS, HD)
     keys_here = piece[0].reshape(piece_rows, HEADS, HD)
     vals_here = piece[1].reshape(piece_rows, HEADS, HD)
     logits = (
         jnp.einsum("qhd,khd->qhk", queries, keys_here, preferred_element_type=jnp.float32) * factor
     )
-    new_max = jnp.maximum(running_max, jnp.max(jnp.where(usable, logits, -1e30), axis=2))
-    weights = jnp.where(usable, jnp.exp(logits - new_max[:, :, None]), 0.0)
-    running_sum = jnp.sum(weights, axis=2)
+    part_max = jnp.max(jnp.where(usable, logits, -1e30), axis=2)
+    weights = jnp.where(usable, jnp.exp(logits - part_max[:, :, None]), 0.0)
+    part_sum = jnp.sum(weights, axis=2)
     weighted = jnp.einsum(
         "qhk,khd->qhd", weights.astype(jnp.bfloat16), vals_here, preferred_element_type=jnp.float32
     )
-    attended = (
-        (weighted / running_sum[:, :, None]).reshape(img_dev, HEADS * HD).astype(jnp.bfloat16)
+    width = HEADS * HD
+    packed = jnp.concatenate(
+        [weighted.reshape(q_rows, width), part_max, part_sum], axis=1
+    ).reshape(n_x, img_dev, width + 2 * HEADS)
+    got = lax.all_to_all(packed, "sx", 0, 0, tiled=True)
+    got_out = got[:, :, :width].reshape(n_x, img_dev, HEADS, HD)
+    got_max = got[:, :, width : width + HEADS]
+    got_sum = got[:, :, width + HEADS :]
+    row_max = jnp.max(got_max, axis=0)
+    rescale = jnp.exp(got_max - row_max[None])
+    numerator = jnp.sum(rescale[:, :, :, None] * got_out, axis=0)
+    denominator = jnp.sum(rescale * got_sum, axis=0)
+    attended = (numerator / denominator[:, :, None]).reshape(img_dev, width).astype(jnp.bfloat16)
+    n_req = lax.axis_size("req")
+    projected = jnp.dot(
+        attended,
+        lax.all_gather(w_proj, "req", axis=1, tiled=True),
+        preferred_element_type=jnp.float32,
     )
-    n_req = lax.axis_size("req")
-    proj_blocks = lax.all_to_all(
-        jnp.broadcast_to(w_proj[None], (n_req,) + w_proj.shape), "req", 0, 0, tiled=True
-    )
-    projected = jnp.einsum(
-        "tk,ikc->tic", attended, proj_blocks, preferred_element_type=jnp.float32
-    ).reshape(img_dev, n_req * w_proj.shape[1])
     hidden = residual_in[0, 0].astype(jnp.float32) + attn_gate[0, 0][None, :] * projected
     mlp_in = modulate_rows(hidden, mlp_shift[0, 0], mlp_scale[0, 0])
     inner = jax.nn.gelu(
@@ -111,9 +124,9 @@
     uncond = jnp.where(is_cond, received, velocity)
     guided_full = uncond + guidance_weight * (cond_part - uncond)
     partials = jnp.stack([jnp.sum(guided_full * guided_full), jnp.max(jnp.abs(guided_full))])
-    n_seq = lax.axis_size("seq")
+    n_seq = lax.axis_size(("sz", "sx"))
     gathered = lax.all_to_all(
-        jnp.broadcast_to(partials[None], (n_seq, 2)), "seq", 0, 0, tiled=True
+        jnp.broadcast_to(partials[None], (n_seq, 2)), ("sz", "sx"), 0, 0, tiled=True
     )
     guided_total = jnp.sum(gathered[:, 0])
     peak_value = jnp.max(gathered[:, 1])
@@ -125,10 +138,17 @@
 
 
 def solution(mesh):
+    n_seq = mesh.shape["seq"]
+    n_x = SEQ_MINOR if n_seq % SEQ_MINOR == 0 else 1
+    split_mesh = Mesh(
+        mesh.devices.reshape(mesh.shape["cfg"], mesh.shape["req"], n_seq // n_x, n_x),
+        ("cfg", "req", "sz", "sx"),
+    )
+    seq = ("sz", "sx")
     in_specs = (
-        P("cfg", "req", "seq", None),
-        P(None, "cfg", "req", "seq", None),
-        P("cfg", "req", "seq", None),
+        P("cfg", "req", seq, None),
+        P(None, "cfg", "req", seq, None),
+        P("cfg", "req", seq, None),
         P("cfg", "req"),
         P("cfg", "req", None),
         P("cfg", "req", None),
@@ -140,10 +160,10 @@
         P(None, "req"),
         P("req", None),
         P(),
-        P("req", "seq", "cfg"),
+        P("req", seq, "cfg"),
         P("req"),
     )
-    out_specs = (P("req", "seq", "cfg"), P("req"), P("req"))
+    out_specs = (P("req", seq, "cfg"), P("req"), P("req"))
     return jax.shard_map(
-        per_device, mesh=mesh, in_specs=in_specs, out_specs=out_specs, check_vma=False
+        per_device, mesh=split_mesh, in_specs=in_specs, out_specs=out_specs, check_vma=False
     )

time: 207 us -> 164 us (0.79)
  waiting for transfers between devices: 114 us -> 41 us
  blocking collectives: 16.2 us -> 61.5 us
  local copies, waits for them, and re-layouts: 21 us -> 7.66 us
  starting transfers between devices: 21.7 us -> 18.7 us
    all_gather x1, waiting for transfers between devices: 81.1 us -> 0.02 us  [per_device(): lax.all_gather(w_proj, 'req', axis=1, tiled=True)]
    all_gather x0 -> x2, blocking collectives: none -> 45.8 us  [the longest x1 33.3 us: per_device(): piece = lax.all_gather(key_value[:, 0, 0], 'sz', axis=1, tiled=True)]
    all_to_all x2, waiting for transfers between devices: 8.88 us -> 16.5 us  [the longest x1 8.88 us: per_device(): lax.all_to_all(jnp.broadcast_to(partials[None], (n_seq, 2)), ('sz', 'sx')...]
    slice x2 -> x1, local copies, waits for them, and re-layouts: 8.3 us -> 1.06 us  [per_device(): keys_here = piece[0].reshape(piece_rows, HEADS, HD)]
    all_to_all x2, starting transfers between devices: 11.8 us -> 8.65 us  [the longest x1 4.98 us: per_device(): lax.all_to_all(jnp.broadcast_to(partials[None], (n_seq, 2)), ('sz', 'sx')...]
    slice x1 -> x2, local copies, waits for them, and re-layouts: 4 us -> 1.14 us  [per_device(): vals_here = piece[1].reshape(piece_rows, HEADS, HD)]
    broadcast_in_dim x1 -> x0, local copies, waits for them, and re-layouts: 2.53 us -> none  [per_device(): jnp.broadcast_to(w_proj[None], (n_req,) + w_proj.shape)]
    convert_element_type x2 -> x0, local copies, waits for them, and re-layouts: 2.33 us -> none  [per_device(): (weighted / running_sum[:, :, None]).reshape(img_dev, HEADS * HD)]
  transfers between devices with their start and end apart: 5 -> 5, of which waited for: 4 -> 4; matrix products, arithmetic and copies ran while one was open for 12% -> 9% of each run, Pallas kernels for 0% -> 0%
where the time goes in v3:
time: 164 us; the launch traced here: 163 us
  blocking collectives  61.5 us (38%)
  waiting for transfers between devices  41 us (25%)
  starting transfers between devices  18.7 us (11%)
  between operations  17.4 us (11%)
  matrix products  9.33 us (6%)
  local copies, waits for them, and re-layouts  7.66 us (5%)
  other arithmetic  7.12 us (4%)
    all_gather x1, blocking collectives, per_device(): piece = lax.all_gather(key_value[:, 0, 0], 'sz', axis=1, tiled=True)  33.3 us
    all_to_all x1, waiting for transfers between devices, per_device(): lax.all_to_all(mlp_parts, 'req', 0, 0, tiled=True).astype(jnp.float32)  18.3 us
    all_gather x1, blocking collectives, per_device(): lax.all_gather(mlp_in, 'req', axis=0, tiled=True)  15.7 us
    all_gather x1, blocking collectives, per_device(): query_rows = lax.all_gather(query[0, 0], 'sx', axis=0, tiled=True)  12.5 us
    all_to_all x1, waiting for transfers between devices, per_device(): lax.all_to_all(jnp.broadcast_to(partials[None], (n_seq, 2)), ('sz', 'sx')...  8.88 us
    all_to_all x1, waiting for transfers between devices, per_device(): got = lax.all_to_all(packed, 'sx', 0, 0, tiled=True)  7.63 us
    all_to_all x1, starting transfers between devices, per_device(): lax.all_to_all(mlp_parts, 'req', 0, 0, tiled=True).astype(jnp.float32)  6.56 us
    ppermute x1, waiting for transfers between devices, swapped(): return lax.ppermute(block, axis, route)  5.47 us
  transfers between devices with their start and end apart: 5, of which 4 were waited for; matrix products, arithmetic and copies ran while one was open for 9% of the time, Pallas kernels for 0%

profile of v3, /device:TPU:56, one launch (start us, length us, event | category | flops | bytes accessed | tf_op | source)
XLA Modules:
  0.0 162.6 jit_solution(9286609441419873913)
XLA Ops:
  7.2 0.0 copy-start
  7.2 0.0 all-gather.4.cloned.1.call-start
  7.2 0.7 all-gather.4.cloned.1.call-update
  8.6 0.0 copy-start.3
  8.6 33.3 %all-gather = bf16[2,1,1,320,768]{4,3,2,1,0:T(8,128)(2,1)S(1)} all-gather(bf16[2,1,1,40,768]{4,3,2,1,0:T(8,128)(2,1)} %param.17), channel_id=2, replica_groups=mesh['cfg'=2,'req'=8,'sz'=8,'sx'=4] {'sz'}, dimensions={3}, use_global_device_ids=true | all-gather | bytes 1105920 | tf_op jit(solution)/shard_map/all_gather | solution.py:59
  41.9 0.1 fusion.49
  42.0 1.1 copy.32
  43.0 0.0 copy-done.3
  43.0 12.5 %all-gather.1 = bf16[1,1,128,768]{3,2,1,0:T(8,128)(2,1)S(1)} all-gather(bf16[1,1,32,768]{3,2,1,0:T(8,128)(2,1)S(1)} %copy-done.3), channel_id=3, replica_groups=mesh['cfg'=2,'req'=8,'sz'=8,'sx'=4] {'sx'}, dimensions={2}, use_global_device_ids=true | all-gather | bytes 245760 | tf_op jit(solution)/shard_map/all_gather | solution.py:58
  55.5 0.2 copy.33
  55.6 1.1 copy.34
  56.7 0.0 copy-start.11
  56.7 1.6 %fusion.1 = (f32[128,12]{0,1:T(8,128)S(1)}, f32[12,320,128]{2,1,0:T(8,128)S(1)}) fusion(pred[320]{0:T(512)(128)(4,1)S(1)} %fusion.39, bf16[320,12,64]{0,2,1:T(8,128)(2,1)} %bitcast.44, bf16[128,12,64]{0,2,1:T(8,128)(2,1)S(1)} %bitcast.45), kind=kOutput, calls=%fused_computation.5 | convolution fusion | flops 64387584 | bytes 2660672 | tf_op jit(solution)/shard_map/qhd,khd->qhk/dot_general | solution.py:71
  58.4 0.7 copy.36
  59.1 1.6 convolution_bitcast_fusion
  60.7 0.0 copy-done.11
  60.7 1.4 copy.35
  62.1 1.5 concatenate.10
  63.6 1.1 fusion.4
  64.7 0.0 copy-start.7
  64.7 0.0 copy-start.8
  64.7 0.0 copy-start.5
  64.7 0.1 copy.39
  64.8 1.7 %pad_maximum_fusion = f32[4,32,792]{2,1,0:T(8,128)} fusion(f32[4,32,12]{2,1,0:T(8,128)S(1)} %bitcast.48, f32[4,32,12]{2,1,0:T(8,128)} %bitcast.47, f32[4,32,768]{2,1,0:T(8,128)S(1)} %concatenate.10), kind=kLoop, calls=%fused_computation.17 | loop fusion | flops 202752 | bytes 811008 | tf_op jit(solution)/shard_map/concatenate | solution.py:80
  66.5 3.7 %all-to-all-start = ((f32[4,32,792]{2,1,0:T(8,128)}), f32[4,32,792]{2,1,0:T(8,128)S(1)}, u32[]{:S(2)}, u32[]{:S(2)}) async-start(f32[4,32,792]{2,1,0:T(8,128)} %pad_maximum_fusion), calls=%async_computation | async-start | bytes 917504 | tf_op jit(solution)/shard_map/all_to_all | solution.py:83
  70.2 0.0 copy-done.7
  70.2 0.0 copy-done.8
  70.2 0.0 copy-done.5
  70.3 7.6 %all-to-all-done = f32[4,32,792]{2,1,0:T(8,128)S(1)} async-done(((f32[4,32,792]{2,1,0:T(8,128)}), f32[4,32,792]{2,1,0:T(8,128)S(1)}, u32[]{:S(2)}, u32[]{:S(2)}) %all-to-all-start) | async-done | bytes 405536 | tf_op jit(solution)/shard_map/all_to_all | solution.py:83
  77.9 0.1 fusion.30
  78.0 0.0 copy-start.2
  78.0 0.3 mul.153
  78.4 0.3 mul.154
  78.7 0.1 div.37
  78.8 0.1 div.38
  78.9 0.0 all-gather.4.cloned.1.call-done
  79.0 0.0 copy-done.2
  79.0 2.6 %fusion.50 = (f32[32]{0:T(128)S(1)}, f32[32,1536]{1,0:T(8,128)S(1)}) fusion(bf16[768,1536]{0,1:T(8,128)(2,1)} %all-gather.4.cloned.1.call-done, f32[32,768]{1,0:T(8,128)S(1)} %fusion.19, f32[32,768]{1,0:T(8,128)S(1)} %div.38, f32[1536]{0:T(1024)S(1)} %reduce.3, bf16[1,1,32,1536]{3,2,1,0:T(8,128)(2,1)S(1)} %copy-done.2), kind=kOutput, calls=%fused_computation.85 | convolution fusion | flops 75743200 | bytes 2857088 | tf_op jit(solution)/shard_map/dot_general | solution.py:93
  81.6 0.2 multiply_reduce_fusion.1
  81.8 0.1 add_convert_fusion.1
  81.9 15.7 %all_gather.15 = bf16[256,1536]{1,0:T(8,128)(2,1)S(1)} all-gather(bf16[32,1536]{1,0:T(8,128)(2,1)S(1)} %add_convert_fusion.1), channel_id=1, replica_groups=mesh['cfg'=2,'req'=8,'sz'=8,'sx'=4] {'req'}, dimensions={0}, use_global_device_ids=true | all-gather | bytes 884736 | tf_op jit(solution)/shard_map/all_gather | solution.py:102
  97.6 0.0 copy-done
  97.6 3.3 %convolution_convert_fusion = bf16[256,1536]{1,0:T(8,128)(2,1)} fusion(bf16[384,1536]{1,0:T(8,128)(2,1)S(1)} %copy-done, bf16[256,1536]{1,0:T(8,128)(2,1)S(1)} %all_gather.15, bf16[1536,384]{1,0:T(8,128)(2,1)} %param.27), kind=kOutput, calls=%fused_computation | convolution fusion | flops 605257728 | bytes 3932160 | tf_op jit(solution)/shard_map/dot_general | solution.py:109
  100.9 6.6 %all-to-all-start.1 = ((bf16[8,32,1536]{2,1,0:T(8,128)(2,1)}), bf16[8,32,1536]{2,1,0:T(8,128)(2,1)S(1)}, u32[]{:S(2)}, u32[]{:S(2)}) async-start(bf16[8,32,1536]{2,1,0:T(8,128)(2,1)} %bitcast.10), calls=%async_computation.1 | async-start | bytes 1572864 | tf_op jit(solution)/shard_map/all_to_all | solution.py:114
  107.5 0.0 copy-done.9
  107.5 0.0 copy-done.10
  107.5 0.0 copy-done.6
  107.6 18.3 %all-to-all-done.1 = bf16[8,32,1536]{2,1,0:T(8,128)(2,1)S(1)} async-done(((bf16[8,32,1536]{2,1,0:T(8,128)(2,1)}), bf16[8,32,1536]{2,1,0:T(8,128)(2,1)S(1)}, u32[]{:S(2)}, u32[]{:S(2)}) %all-to-all-start.1) | async-done | bytes 786464 | tf_op jit(solution)/shard_map/all_to_all | solution.py:114
  125.9 0.1 convert_reduce_fusion
  126.0 0.1 fusion.48
  126.1 0.2 multiply_reduce_fusion
  126.3 0.0 copy-done.1
  126.3 0.2 fusion.25
  126.6 3.4 %collective-permute-start = (f32[32,64]{1,0:T(8,128)S(1)}, f32[32,64]{1,0:T(8,128)S(1)}, u32[]{:S(2)}, u32[]{:S(2)}) collective-permute-start(f32[32,64]{1,0:T(8,128)S(1)} %fusion.25), channel_id=1, source_target_pairs={{0,256},{256,0},{1,257},{257,1},{2,258},{258,2},{3,259},{259,3},{4... | collective-permute-start | bytes 24584 | tf_op jit(solution)/shard_map/ppermute | solution.py:21
  130.6 5.5 %collective-permute-done = f32[32,64]{1,0:T(8,128)S(1)} collective-permute-done((f32[32,64]{1,0:T(8,128)S(1)}, f32[32,64]{1,0:T(8,128)S(1)}, u32[]{:S(2)}, u32[]{:S(2)}) %collective-permute-start) | collective-permute-done | bytes 8224 | tf_op jit(solution)/shard_map/ppermute | solution.py:21
  136.1 0.6 multiply_reduce_fusion.2
  136.7 1.4 pad_maximum_fusion.1
  138.1 0.6 broadcast_in_dim.37
  138.7 5.0 %all-to-all-start.2 = ((f32[32,1,2]{2,1,0:T(1,128)}), f32[32,1,2]{2,1,0:T(1,128)S(1)}, u32[]{:S(2)}, u32[]{:S(2)}) async-start(f32[32,1,2]{2,1,0:T(1,128)} %broadcast_in_dim.37), calls=%async_computation.2 | async-start | bytes 32768 | tf_op jit(solution)/shard_map/all_to_all | solution.py:128
  143.7 0.0 copy-done.4
  143.7 0.7 bitcast_add_fusion
  144.4 8.9 %all-to-all-done.2 = f32[32,1,2]{2,1,0:T(1,128)S(1)} async-done(((f32[32,1,2]{2,1,0:T(1,128)}), f32[32,1,2]{2,1,0:T(1,128)S(1)}, u32[]{:S(2)}, u32[]{:S(2)}) %all-to-all-start.2) | async-done | bytes 288 | tf_op jit(solution)/shard_map/all_to_all | solution.py:128
  153.3 0.1 copy.38
  153.3 0.6 slice_reduce_fusion.1
  (18 shorter events, 0.2 us)
Async XLA Ops:
  7.2 90.4 %copy-start = (bf16[384,1536]{1,0:T(8,128)(2,1)S(1)}, bf16[384,1536]{1,0:T(8,128)(2,1)}, u32[]{:S(2)}) copy-start(bf16[384,1536]{1,0:T(8,128)(2,1)} %param.28) | copy-start | bytes 3538948
  7.2 71.8 %all-gather.4.cloned.1.call-start = ((), (), s32[]{:S(2)}) async-start(), calls=%async_computation.3 | async-start | bytes 2654208 | tf_op jit(solution)/shard_map/all_gather | solution.py:95
  8.6 34.5 %copy-start.3 = (bf16[1,1,32,768]{3,2,1,0:T(8,128)(2,1)S(1)}, bf16[1,1,32,768]{3,2,1,0:T(8,128)(2,1)}, u32[]{:S(2)}) copy-start(bf16[1,1,32,768]{3,2,1,0:T(8,128)(2,1)} %param.16) | copy-start | bytes 147460
  56.7 4.0 %copy-start.11 = (pred[320]{0:T(512)(128)(4,1)}, pred[320]{0:T(512)(128)(4,1)S(1)}, u32[]{:S(2)}) copy-start(pred[320]{0:T(512)(128)(4,1)S(1)} %fusion.39) | copy-start | bytes 964
  64.7 5.5 %copy-start.7 = (f32[1,1,1536]{2,1,0:T(1,128)S(1)}, f32[1,1,1536]{2,1,0:T(1,128)}, u32[]{:S(2)}) copy-start(f32[1,1,1536]{2,1,0:T(1,128)} %param.20) | copy-start | bytes 18436
  64.7 5.5 %copy-start.8 = (f32[1,1,1536]{2,1,0:T(1,128)S(1)}, f32[1,1,1536]{2,1,0:T(1,128)}, u32[]{:S(2)}) copy-start(f32[1,1,1536]{2,1,0:T(1,128)} %param.21) | copy-start | bytes 18436
  64.7 5.6 %copy-start.5 = (f32[1,1,1536]{2,1,0:T(1,128)S(1)}, f32[1,1,1536]{2,1,0:T(1,128)}, u32[]{:S(2)}) copy-start(f32[1,1,1536]{2,1,0:T(1,128)} %param.22) | copy-start | bytes 18436
  66.5 11.4 %all-to-all-start = ((f32[4,32,792]{2,1,0:T(8,128)}), f32[4,32,792]{2,1,0:T(8,128)S(1)}, u32[]{:S(2)}, u32[]{:S(2)}) async-start(f32[4,32,792]{2,1,0:T(8,128)} %pad_maximum_fusion), calls=%async_computation | async-start | bytes 917504 | tf_op jit(solution)/shard_map/all_to_all | solution.py:83
  78.0 1.0 copy-start.2
  97.6 9.9 %copy-start.9 = (f32[1,1,1536]{2,1,0:T(1,128)S(1)}, f32[1,1,1536]{2,1,0:T(1,128)}, u32[]{:S(2)}) copy-start(f32[1,1,1536]{2,1,0:T(1,128)} %param.23) | copy-start | bytes 18436
  97.6 9.9 %copy-start.10 = (f32[1,1,1536]{2,1,0:T(1,128)S(1)}, f32[1,1,1536]{2,1,0:T(1,128)}, u32[]{:S(2)}) copy-start(f32[1,1,1536]{2,1,0:T(1,128)} %param.24) | copy-start | bytes 18436
  97.6 9.9 %copy-start.6 = (f32[1,1,1536]{2,1,0:T(1,128)S(1)}, f32[1,1,1536]{2,1,0:T(1,128)}, u32[]{:S(2)}) copy-start(f32[1,1,1536]{2,1,0:T(1,128)} %param.25) | copy-start | bytes 18436
  100.9 25.4 %copy-start.1 = (bf16[1536,64]{0,1:T(8,128)(2,1)S(1)}, bf16[1536,64]{0,1:T(8,128)(2,1)}, u32[]{:S(2)}) copy-start(bf16[1536,64]{0,1:T(8,128)(2,1)} %param.29) | copy-start | bytes 589828
  100.9 42.8 %copy-start.4 = (f32[1,32,32]{2,1,0:T(8,128)S(1)}, f32[1,32,32]{2,1,0:T(8,128)}, u32[]{:S(2)}) copy-start(f32[1,32,32]{2,1,0:T(8,128)} %param.30) | copy-start | bytes 12292
  100.9 24.9 %all-to-all-start.1 = ((bf16[8,32,1536]{2,1,0:T(8,128)(2,1)}), bf16[8,32,1536]{2,1,0:T(8,128)(2,1)S(1)}, u32[]{:S(2)}, u32[]{:S(2)}) async-start(bf16[8,32,1536]{2,1,0:T(8,128)(2,1)} %bitcast.10), calls=%async_computation.1 | async-start | bytes 1572864 | tf_op jit(solution)/shard_map/all_to_all | solution.py:114
  126.6 9.5 %collective-permute-start = (f32[32,64]{1,0:T(8,128)S(1)}, f32[32,64]{1,0:T(8,128)S(1)}, u32[]{:S(2)}, u32[]{:S(2)}) collective-permute-start(f32[32,64]{1,0:T(8,128)S(1)} %fusion.25), channel_id=1, source_target_pairs={{0,256},{256,0},{1,257},{257,1},{2,258},{258,2},{3,259},{259,3},{4... | collective-permute-start | bytes 24584 | tf_op jit(solution)/shard_map/ppermute | solution.py:21
  138.7 14.6 %all-to-all-start.2 = ((f32[32,1,2]{2,1,0:T(1,128)}), f32[32,1,2]{2,1,0:T(1,128)S(1)}, u32[]{:S(2)}, u32[]{:S(2)}) async-start(f32[32,1,2]{2,1,0:T(1,128)} %broadcast_in_dim.37), calls=%async_computation.2 | async-start | bytes 32768 | tf_op jit(solution)/shard_map/all_to_all | solution.py:128
Sparse Core Ops, SparseCore 0:
  10.1 44.5 all-gather.3

commit v4 on v3

--- a/solution.py
+++ b/solution.py
@@ -6,6 +6,7 @@
 HEADS = 12
 HD = 64
 SEQ_MINOR = 4
+CORES = 2
 
 
 guidance_weight = 4.0
@@ -55,7 +56,9 @@
     factor = HD ** (-0.5)
     n_x = lax.axis_size("sx")
     x_index = lax.axis_index("sx")
-    query_rows = lax.all_gather(query[0, 0], "sx", axis=0, tiled=True)
+    query_rows = lax.all_to_all(
+        jnp.broadcast_to(query[0, 0][None], (n_x,) + query.shape[2:]), "sx", 0, 0, tiled=True
+    ).reshape(n_x * img_dev, query.shape[3])
     piece = lax.all_gather(key_value[:, 0, 0], "sz", axis=1, tiled=True)
     q_rows = query_rows.shape[0]
     piece_rows = piece.shape[1]
@@ -89,29 +92,34 @@
     numerator = jnp.sum(rescale[:, :, :, None] * got_out, axis=0)
     denominator = jnp.sum(rescale * got_sum, axis=0)
     attended = (numerator / denominator[:, :, None]).reshape(img_dev, width).astype(jnp.bfloat16)
-    n_req = lax.axis_size("req")
     projected = jnp.dot(
         attended,
-        lax.all_gather(w_proj, "req", axis=1, tiled=True),
+        lax.all_gather(w_proj, ("ry", "rc"), axis=1, tiled=True),
         preferred_element_type=jnp.float32,
     )
     hidden = residual_in[0, 0].astype(jnp.float32) + attn_gate[0, 0][None, :] * projected
     mlp_in = modulate_rows(hidden, mlp_shift[0, 0], mlp_scale[0, 0])
-    inner = jax.nn.gelu(
-        jnp.dot(
-            lax.all_gather(mlp_in, "req", axis=0, tiled=True),
-            w_up,
-            preferred_element_type=jnp.float32,
-        ),
-        approximate=True,
+    n_y = lax.axis_size("ry")
+    pair = [(0, 1), (1, 0)]
+    up_other = lax.ppermute(w_up, "rc", pair)
+    down_other = lax.ppermute(w_down, "rc", pair)
+    line_in = lax.all_gather(mlp_in, "ry", axis=0, tiled=True)
+    inner_own = jax.nn.gelu(
+        jnp.dot(line_in, w_up, preferred_element_type=jnp.float32), approximate=True
+    ).astype(jnp.bfloat16)
+    inner_other = jax.nn.gelu(
+        jnp.dot(line_in, up_other, preferred_element_type=jnp.float32), approximate=True
     ).astype(jnp.bfloat16)
     mlp_parts = (
-        jnp.dot(inner, w_down, preferred_element_type=jnp.float32)
+        (
+            jnp.dot(inner_own, w_down, preferred_element_type=jnp.float32)
+            + jnp.dot(inner_other, down_other, preferred_element_type=jnp.float32)
+        )
         .astype(jnp.bfloat16)
-        .reshape(n_req, img_dev, w_down.shape[1])
+        .reshape(n_y, img_dev, w_down.shape[1])
     )
     mlp_out = jnp.sum(
-        lax.all_to_all(mlp_parts, "req", 0, 0, tiled=True).astype(jnp.float32), axis=0
+        lax.all_to_all(mlp_parts, "ry", 0, 0, tiled=True).astype(jnp.float32), axis=0
     )
     hidden_two = hidden + mlp_gate[0, 0][None, :] * mlp_out
     modulated = modulate_rows(hidden_two, shift[0, 0], scale[0, 0])
@@ -139,31 +147,34 @@
 
 def solution(mesh):
     n_seq = mesh.shape["seq"]
+    n_req = mesh.shape["req"]
     n_x = SEQ_MINOR if n_seq % SEQ_MINOR == 0 else 1
+    n_core = CORES if n_req % CORES == 0 else 1
     split_mesh = Mesh(
-        mesh.devices.reshape(mesh.shape["cfg"], mesh.shape["req"], n_seq // n_x, n_x),
-        ("cfg", "req", "sz", "sx"),
+        mesh.devices.reshape(mesh.shape["cfg"], n_req // n_core, n_core, n_seq // n_x, n_x),
+        ("cfg", "ry", "rc", "sz", "sx"),
     )
+    req = ("ry", "rc")
     seq = ("sz", "sx")
     in_specs = (
-        P("cfg", "req", seq, None),
-        P(None, "cfg", "req", seq, None),
-        P("cfg", "req", seq, None),
-        P("cfg", "req"),
-        P("cfg", "req", None),
-        P("cfg", "req", None),
-        P("cfg", "req", None),
-        P("cfg", "req", None),
-        P("cfg", "req", None),
-        P("cfg", "req", None),
-        P(None, "req"),
-        P(None, "req"),
-        P("req", None),
+        P("cfg", req, seq, None),
+        P(None, "cfg", req, seq, None),
+        P("cfg", req, seq, None),
+        P("cfg", req),
+        P("cfg", req, None),
+        P("cfg", req, None),
+        P("cfg", req, None),
+        P("cfg", req, None),
+        P("cfg", req, None),
+        P("cfg", req, None),
+        P(None, req),
+        P(None, req),
+        P(req, None),
         P(),
-        P("req", seq, "cfg"),
-        P("req"),
+        P(req, seq, "cfg"),
+        P(req),
     )
-    out_specs = (P("req", seq, "cfg"), P("req"), P("req"))
+    out_specs = (P(req, seq, "cfg"), P(req), P(req))
     return jax.shard_map(
         per_device, mesh=split_mesh, in_specs=in_specs, out_specs=out_specs, check_vma=False
     )

time: 164 us -> 144 us (0.88)
  waiting for transfers between devices: 41 us -> 24.4 us
  blocking collectives: 61.5 us -> 48 us
  starting transfers between devices: 18.7 us -> 29 us
    all_gather x2 -> x1, blocking collectives: 28.2 us -> 14.7 us  [per_device(): line_in = lax.all_gather(mlp_in, 'ry', axis=0, tiled=True)]
    all_to_all x1 -> x2, waiting for transfers between devices: 18.3 us -> 6.41 us  [the longest x1 6.41 us: per_device(): lax.all_to_all(mlp_parts, 'ry', 0, 0, tiled=True).astype(jnp.float32)]
    all_to_all x1, waiting for transfers between devices: 7.63 us -> 3.28 us  [per_device(): got = lax.all_to_all(packed, 'sx', 0, 0, tiled=True)]
    ppermute x0 -> x2, starting transfers between devices: none -> 4.32 us  [the longest x1 2.41 us: per_device(): down_other = lax.ppermute(w_down, 'rc', pair)]
    all_to_all x1 -> x2, starting transfers between devices: 6.56 us -> 10.2 us  [the longest x1 5.88 us: per_device(): lax.all_to_all(mlp_parts, 'ry', 0, 0, tiled=True).astype(jnp.float32)]
    dot_general x2 -> x3, matrix products: 5.87 us -> 7.65 us  [the longest x1 2.74 us: per_device(): jnp.dot(inner_other, down_other, preferred_element_type=jnp.float32)]
  transfers between devices with their start and end apart: 5 -> 8, of which waited for: 4 -> 4; matrix products, arithmetic and copies ran while one was open for 9% -> 12% of each run, Pallas kernels for 0% -> 0%
where the time goes in v4:
time: 144 us; the launch traced here: 143 us
  blocking collectives  48 us (33%)
  starting transfers between devices  29 us (20%)
  waiting for transfers between devices  24.4 us (17%)
  between operations  17.5 us (12%)
  matrix products  10.8 us (8%)
  local copies, waits for them, and re-layouts  8.04 us (6%)
  other arithmetic  5.56 us (4%)
    all_gather x1, blocking collectives, per_device(): piece = lax.all_gather(key_value[:, 0, 0], 'sz', axis=1, tiled=True)  33.4 us
    all_gather x1, blocking collectives, per_device(): line_in = lax.all_gather(mlp_in, 'ry', axis=0, tiled=True)  14.7 us
    all_to_all x1, waiting for transfers between devices, per_device(): lax.all_to_all(jnp.broadcast_to(partials[None], (n_seq, 2)), ('sz', 'sx')...  8.88 us
    all_to_all x1, waiting for transfers between devices, per_device(): lax.all_to_all(mlp_parts, 'ry', 0, 0, tiled=True).astype(jnp.float32)  6.41 us
    all_to_all x1, starting transfers between devices, per_device(): lax.all_to_all(mlp_parts, 'ry', 0, 0, tiled=True).astype(jnp.float32)  5.88 us
    all_to_all x1, starting transfers between devices, per_device(): lax.all_to_all(jnp.broadcast_to(partials[None], (n_seq, 2)), ('sz', 'sx')...  5.73 us
    ppermute x1, waiting for transfers between devices, swapped(): return lax.ppermute(block, axis, route)  5.1 us
    all_to_all x1, starting transfers between devices, per_device(): got = lax.all_to_all(packed, 'sx', 0, 0, tiled=True)  4.9 us
  transfers between devices with their start and end apart: 8, of which 4 were waited for; matrix products, arithmetic and copies ran while one was open for 12% of the time, Pallas kernels for 0%

profile of v4, /device:TPU:56, one launch (start us, length us, event | category | flops | bytes accessed | tf_op | source)
XLA Modules:
  0.0 143.3 jit_solution(16181367651081724811)
XLA Ops:
  7.2 0.0 copy-start
  7.2 0.0 all-gather.3.cloned.1.call-start
  7.2 0.7 all-gather.3.cloned.1.call-update
  7.9 1.5 %broadcast_in_dim.43 = bf16[4,32,768]{2,1,0:T(8,128)(2,1)} broadcast(bf16[32,768]{1,0:T(8,128)(2,1)} %bitcast.50), dimensions={1,2} | broadcast | bytes 245760 | tf_op jit(solution)/shard_map/broadcast_in_dim | solution.py:60
  9.4 4.3 %all-to-all-start = ((bf16[4,32,768]{2,1,0:T(8,128)(2,1)}), bf16[4,32,768]{2,1,0:T(8,128)(2,1)S(1)}, u32[]{:S(2)}, u32[]{:S(2)}) async-start(bf16[4,32,768]{2,1,0:T(8,128)(2,1)} %broadcast_in_dim.43), calls=%async_computation | async-start | bytes 393216 | tf_op jit(solution)/shard_map/all_to_all | solution.py:59
  13.7 33.4 %all-gather = bf16[2,1,1,320,768]{4,3,2,1,0:T(8,128)(2,1)S(1)} all-gather(bf16[2,1,1,40,768]{4,3,2,1,0:T(8,128)(2,1)} %param.17), channel_id=2, replica_groups=mesh['cfg'=2,'ry'=4,'rc'=2,'sz'=8,'sx'=4] {'sz'}, dimensions={3}, use_global_device_ids=true | all-gather | bytes 1105920 | tf_op jit(solution)/shard_map/all_gather | solution.py:62
  47.1 0.1 fusion.70
  47.8 0.3 copy.32
  48.1 1.1 copy.34
  49.2 0.0 all-to-all-done
  49.2 0.3 reshape_reshape.3
  49.5 0.6 fusion.2
  50.1 0.1 copy.36
  50.2 2.3 %convolution_bitcast_fusion = f32[128,12,64]{0,2,1:T(8,128)} fusion(bf16[320,12,64]{0,2,1:T(8,128)(2,1)} %bitcast.47, f32[12,320,128]{2,1,0:T(8,128)S(1)} %get-tuple-element.15, f32[128,12]{0,1:T(8,128)S(1)} %get-tuple-element.14, pred[320]{0:T(512)(128)(4,1)S(1)} %fusion.56), kind=kOutput, calls=%fused_computation.11 | convolution fusion | flops 64880640 | bytes 2857280 | tf_op jit(solution)/shard_map/qhk,khd->qhd/dot_general | solution.py:79
  52.6 1.5 %copy.35 = f32[128,12,64]{2,1,0:T(8,128)S(1)} copy(f32[128,12,64]{0,2,1:T(8,128)} %convolution_bitcast_fusion) | data formatting | bytes 786432 | tf_op jit(solution)/shard_map/qhk,khd->qhd/transpose | solution.py:79
  54.1 1.0 concatenate.10
  55.1 0.4 fusion.5
  55.5 0.1 copy.39
  55.6 0.5 copy-done.1
  56.1 0.9 pad_maximum_fusion
  57.0 4.9 %all-to-all-start.1 = ((f32[4,32,792]{2,1,0:T(8,128)}), f32[4,32,792]{2,1,0:T(8,128)S(1)}, u32[]{:S(2)}, u32[]{:S(2)}) async-start(f32[4,32,792]{2,1,0:T(8,128)} %pad_maximum_fusion), calls=%async_computation.1 | async-start | bytes 917504 | tf_op jit(solution)/shard_map/all_to_all | solution.py:86
  61.9 1.9 %collective-permute-start = (bf16[1536,384]{1,0:T(8,128)(2,1)}, bf16[1536,384]{1,0:T(8,128)(2,1)S(1)}, u32[]{:S(2)}, u32[]{:S(2)}) collective-permute-start(bf16[1536,384]{1,0:T(8,128)(2,1)} %param.27), channel_id=1, source_target_pairs={{0,32},{32,0},{1,33},{33,1},{2,34},{34,2},{3,35},{35,3},{4,36},{36... | collective-permute-start | bytes 3538952 | tf_op jit(solution)/shard_map/ppermute | solution.py:104
  63.8 2.4 %collective-permute-start.1 = (bf16[384,1536]{1,0:T(8,128)(2,1)}, bf16[384,1536]{1,0:T(8,128)(2,1)}, u32[]{:S(2)}, u32[]{:S(2)}) collective-permute-start(bf16[384,1536]{1,0:T(8,128)(2,1)} %param.28), channel_id=1, source_target_pairs={{0,32},{32,0},{1,33},{33,1},{2,34},{34,2},{3,35},{35,3},{4,36},{36... | collective-permute-start | bytes 3538952 | tf_op jit(solution)/shard_map/ppermute | solution.py:105
  66.2 0.0 copy-done.6
  66.2 0.0 copy-done.7
  66.3 0.0 copy-done.4
  66.3 3.3 %all-to-all-done.1 = f32[4,32,792]{2,1,0:T(8,128)S(1)} async-done(((f32[4,32,792]{2,1,0:T(8,128)}), f32[4,32,792]{2,1,0:T(8,128)S(1)}, u32[]{:S(2)}, u32[]{:S(2)}) %all-to-all-start.1) | async-done | bytes 405536 | tf_op jit(solution)/shard_map/all_to_all | solution.py:86
  69.6 0.1 fusion.47
  69.7 0.0 copy-start.2
  69.7 0.3 mul.156
  70.0 0.3 mul.157
  70.3 0.1 div.37
  70.5 0.1 div.38
  70.6 0.0 all-gather.3.cloned.1.call-done
  70.6 0.0 copy-done.2
  70.7 2.6 %fusion.71 = (f32[32]{0:T(128)S(1)}, f32[32,1536]{1,0:T(8,128)S(1)}) fusion(bf16[768,1536]{0,1:T(8,128)(2,1)} %all-gather.3.cloned.1.call-done, f32[32,768]{1,0:T(8,128)S(1)} %fusion.12, f32[32,768]{1,0:T(8,128)S(1)} %div.38, f32[1536]{0:T(1024)S(1)} %reduce.3, bf16[1,1,32,1536]{3,2,1,0:T(8,128)(2,1)S(1)} %copy-done.2), kind=kOutput, calls=%fused_computation.106 | convolution fusion | flops 75743200 | bytes 2857088 | tf_op jit(solution)/shard_map/dot_general | solution.py:95
  73.2 0.2 multiply_reduce_fusion.1
  73.5 0.1 add_convert_fusion.1
  73.6 14.7 %all_gather.11 = bf16[128,1536]{1,0:T(8,128)(2,1)S(1)} all-gather(bf16[32,1536]{1,0:T(8,128)(2,1)S(1)} %add_convert_fusion.1), channel_id=1, replica_groups=mesh['cfg'=2,'ry'=4,'rc'=2,'sz'=8,'sx'=4] {'ry'}, dimensions={0}, use_global_device_ids=true | all-gather | bytes 491520 | tf_op jit(solution)/shard_map/all_gather | solution.py:106
  88.3 2.3 %fusion.33 = f32[128,1536]{1,0:T(8,128)S(1)} fusion(bf16[384,1536]{1,0:T(8,128)(2,1)} %param.28, bf16[128,1536]{1,0:T(8,128)(2,1)S(1)} %all_gather.11, bf16[1536,384]{1,0:T(8,128)(2,1)} %param.27), kind=kOutput, calls=%fused_computation.46 | convolution fusion | flops 302432256 | bytes 3538944 | tf_op jit(solution)/shard_map/dot_general | solution.py:115
  90.6 0.0 copy-start.8
  90.6 0.0 copy-start.9
  90.6 0.0 copy-start.5
  90.6 0.0 collective-permute-done
  90.7 0.0 collective-permute-done.1
  90.7 2.7 %fusion = bf16[128,1536]{1,0:T(8,128)(2,1)} fusion(f32[128,1536]{1,0:T(8,128)S(1)} %fusion.33, bf16[384,1536]{1,0:T(8,128)(2,1)} %collective-permute-done.1, bf16[128,1536]{1,0:T(8,128)(2,1)S(1)} %all_gather.11, bf16[1536,384]{1,0:T(8,128)(2,1)S(1)} %collective-permute-done), kind=kOutput, calls=%fused_computation.1 | convolution fusion | flops 302825472 | bytes 3932160 | tf_op jit(solution)/shard_map/dot_general | solution.py:116
  93.4 5.9 %all-to-all-start.2 = ((bf16[4,32,1536]{2,1,0:T(8,128)(2,1)}), bf16[4,32,1536]{2,1,0:T(8,128)(2,1)S(1)}, u32[]{:S(2)}, u32[]{:S(2)}) async-start(bf16[4,32,1536]{2,1,0:T(8,128)(2,1)} %bitcast.10), calls=%async_computation.2 | async-start | bytes 786432 | tf_op jit(solution)/shard_map/all_to_all | solution.py:122
  99.4 0.0 copy-done.5
  99.4 6.4 %all-to-all-done.2 = bf16[4,32,1536]{2,1,0:T(8,128)(2,1)S(1)} async-done(((bf16[4,32,1536]{2,1,0:T(8,128)(2,1)}), bf16[4,32,1536]{2,1,0:T(8,128)(2,1)S(1)}, u32[]{:S(2)}, u32[]{:S(2)}) %all-to-all-start.2) | async-done | bytes 393248 | tf_op jit(solution)/shard_map/all_to_all | solution.py:122
  105.8 0.1 convert_reduce_fusion
  105.9 0.1 fusion.69
  106.0 0.2 multiply_reduce_fusion
  106.2 0.0 copy-done
  106.2 0.2 fusion.31
  106.5 3.8 %collective-permute-start.2 = (f32[32,64]{1,0:T(8,128)S(1)}, f32[32,64]{1,0:T(8,128)S(1)}, u32[]{:S(2)}, u32[]{:S(2)}) collective-permute-start(f32[32,64]{1,0:T(8,128)S(1)} %fusion.31), channel_id=1, source_target_pairs={{0,256},{256,0},{1,257},{257,1},{2,258},{258,2},{3,259},{259,3},{4... | collective-permute-start | bytes 24584 | tf_op jit(solution)/shard_map/ppermute | solution.py:22
  110.9 5.1 %collective-permute-done.2 = f32[32,64]{1,0:T(8,128)S(1)} collective-permute-done((f32[32,64]{1,0:T(8,128)S(1)}, f32[32,64]{1,0:T(8,128)S(1)}, u32[]{:S(2)}, u32[]{:S(2)}) %collective-permute-start.2) | collective-permute-done | bytes 8224 | tf_op jit(solution)/shard_map/ppermute | solution.py:22
  116.0 0.6 multiply_reduce_fusion.2
  116.6 1.4 pad_maximum_fusion.1
  118.0 0.6 broadcast_in_dim.46
  118.6 5.7 %all-to-all-start.3 = ((f32[32,1,2]{2,1,0:T(1,128)}), f32[32,1,2]{2,1,0:T(1,128)S(1)}, u32[]{:S(2)}, u32[]{:S(2)}) async-start(f32[32,1,2]{2,1,0:T(1,128)} %broadcast_in_dim.46), calls=%async_computation.3 | async-start | bytes 32768 | tf_op jit(solution)/shard_map/all_to_all | solution.py:136
  124.3 0.7 bitcast_add_fusion
  125.0 8.9 %all-to-all-done.3 = f32[32,1,2]{2,1,0:T(1,128)S(1)} async-done(((f32[32,1,2]{2,1,0:T(1,128)}), f32[32,1,2]{2,1,0:T(1,128)S(1)}, u32[]{:S(2)}, u32[]{:S(2)}) %all-to-all-start.3) | async-done | bytes 288 | tf_op jit(solution)/shard_map/all_to_all | solution.py:136
  133.9 0.1 copy.38
  134.0 0.6 slice_reduce_fusion.1
  (21 shorter events, 0.2 us)
Async XLA Ops:
  7.2 99.1 %copy-start = (bf16[1536,64]{0,1:T(8,128)(2,1)S(1)}, bf16[1536,64]{0,1:T(8,128)(2,1)}, u32[]{:S(2)}) copy-start(bf16[1536,64]{0,1:T(8,128)(2,1)} %param.29) | copy-start | bytes 589828
  7.2 63.5 %all-gather.3.cloned.1.call-start = ((), (), s32[]{:S(2)}) async-start(), calls=%async_computation.4 | async-start | bytes 2654208 | tf_op jit(solution)/shard_map/all_gather | solution.py:97
  9.4 39.8 %all-to-all-start = ((bf16[4,32,768]{2,1,0:T(8,128)(2,1)}), bf16[4,32,768]{2,1,0:T(8,128)(2,1)S(1)}, u32[]{:S(2)}, u32[]{:S(2)}) async-start(bf16[4,32,768]{2,1,0:T(8,128)(2,1)} %broadcast_in_dim.43), calls=%async_computation | async-start | bytes 393216 | tf_op jit(solution)/shard_map/all_to_all | solution.py:59
  55.1 1.0 copy-start.1
  55.1 11.1 %copy-start.6 = (f32[1,1,1536]{2,1,0:T(1,128)S(1)}, f32[1,1,1536]{2,1,0:T(1,128)}, u32[]{:S(2)}) copy-start(f32[1,1,1536]{2,1,0:T(1,128)} %param.20) | copy-start | bytes 18436
  55.1 11.1 %copy-start.7 = (f32[1,1,1536]{2,1,0:T(1,128)S(1)}, f32[1,1,1536]{2,1,0:T(1,128)}, u32[]{:S(2)}) copy-start(f32[1,1,1536]{2,1,0:T(1,128)} %param.21) | copy-start | bytes 18436
  55.1 11.2 %copy-start.4 = (f32[1,1,1536]{2,1,0:T(1,128)S(1)}, f32[1,1,1536]{2,1,0:T(1,128)}, u32[]{:S(2)}) copy-start(f32[1,1,1536]{2,1,0:T(1,128)} %param.22) | copy-start | bytes 18436
  57.0 12.6 %all-to-all-start.1 = ((f32[4,32,792]{2,1,0:T(8,128)}), f32[4,32,792]{2,1,0:T(8,128)S(1)}, u32[]{:S(2)}, u32[]{:S(2)}) async-start(f32[4,32,792]{2,1,0:T(8,128)} %pad_maximum_fusion), calls=%async_computation.1 | async-start | bytes 917504 | tf_op jit(solution)/shard_map/all_to_all | solution.py:86
  61.9 28.8 %collective-permute-start = (bf16[1536,384]{1,0:T(8,128)(2,1)}, bf16[1536,384]{1,0:T(8,128)(2,1)S(1)}, u32[]{:S(2)}, u32[]{:S(2)}) collective-permute-start(bf16[1536,384]{1,0:T(8,128)(2,1)} %param.27), channel_id=1, source_target_pairs={{0,32},{32,0},{1,33},{33,1},{2,34},{34,2},{3,35},{35,3},{4,36},{36... | collective-permute-start | bytes 3538952 | tf_op jit(solution)/shard_map/ppermute | solution.py:104
  63.8 26.9 %collective-permute-start.1 = (bf16[384,1536]{1,0:T(8,128)(2,1)}, bf16[384,1536]{1,0:T(8,128)(2,1)}, u32[]{:S(2)}, u32[]{:S(2)}) collective-permute-start(bf16[384,1536]{1,0:T(8,128)(2,1)} %param.28), channel_id=1, source_target_pairs={{0,32},{32,0},{1,33},{33,1},{2,34},{34,2},{3,35},{35,3},{4,36},{36... | collective-permute-start | bytes 3538952 | tf_op jit(solution)/shard_map/ppermute | solution.py:105
  69.7 1.0 copy-start.2
  90.6 8.7 %copy-start.8 = (f32[1,1,1536]{2,1,0:T(1,128)S(1)}, f32[1,1,1536]{2,1,0:T(1,128)}, u32[]{:S(2)}) copy-start(f32[1,1,1536]{2,1,0:T(1,128)} %param.23) | copy-start | bytes 18436
  90.6 8.7 %copy-start.9 = (f32[1,1,1536]{2,1,0:T(1,128)S(1)}, f32[1,1,1536]{2,1,0:T(1,128)}, u32[]{:S(2)}) copy-start(f32[1,1,1536]{2,1,0:T(1,128)} %param.24) | copy-start | bytes 18436
  90.6 8.7 %copy-start.5 = (f32[1,1,1536]{2,1,0:T(1,128)S(1)}, f32[1,1,1536]{2,1,0:T(1,128)}, u32[]{:S(2)}) copy-start(f32[1,1,1536]{2,1,0:T(1,128)} %param.25) | copy-start | bytes 18436
  93.4 30.9 %copy-start.3 = (f32[1,32,32]{2,1,0:T(8,128)S(1)}, f32[1,32,32]{2,1,0:T(8,128)}, u32[]{:S(2)}) copy-start(f32[1,32,32]{2,1,0:T(8,128)} %param.30) | copy-start | bytes 12292
  93.4 12.4 %all-to-all-start.2 = ((bf16[4,32,1536]{2,1,0:T(8,128)(2,1)}), bf16[4,32,1536]{2,1,0:T(8,128)(2,1)S(1)}, u32[]{:S(2)}, u32[]{:S(2)}) async-start(bf16[4,32,1536]{2,1,0:T(8,128)(2,1)} %bitcast.10), calls=%async_computation.2 | async-start | bytes 786432 | tf_op jit(solution)/shard_map/all_to_all | solution.py:122
  106.5 9.5 %collective-permute-start.2 = (f32[32,64]{1,0:T(8,128)S(1)}, f32[32,64]{1,0:T(8,128)S(1)}, u32[]{:S(2)}, u32[]{:S(2)}) collective-permute-start(f32[32,64]{1,0:T(8,128)S(1)} %fusion.31), channel_id=1, source_target_pairs={{0,256},{256,0},{1,257},{257,1},{2,258},{258,2},{3,259},{259,3},{4... | collective-permute-start | bytes 24584 | tf_op jit(solution)/shard_map/ppermute | solution.py:22
  118.6 15.3 %all-to-all-start.3 = ((f32[32,1,2]{2,1,0:T(1,128)}), f32[32,1,2]{2,1,0:T(1,128)S(1)}, u32[]{:S(2)}, u32[]{:S(2)}) async-start(f32[32,1,2]{2,1,0:T(1,128)} %broadcast_in_dim.46), calls=%async_computation.3 | async-start | bytes 32768 | tf_op jit(solution)/shard_map/all_to_all | solution.py:136
Sparse Core Ops, SparseCore 0:
  10.1 44.5 all-gather.2

commit v5 on v4

--- a/solution.py
+++ b/solution.py
@@ -124,23 +124,27 @@
     hidden_two = hidden + mlp_gate[0, 0][None, :] * mlp_out
     modulated = modulate_rows(hidden_two, shift[0, 0], scale[0, 0])
     velocity = jnp.dot(modulated, w_out, preferred_element_type=jnp.float32)
-    half_width = velocity.shape[1] // lax.axis_size("cfg")
+    n_cfg = lax.axis_size("cfg")
+    half_width = velocity.shape[1] // n_cfg
     side_index = lax.axis_index("cfg")
-    received = swapped(velocity, "cfg", 0)
-    is_cond = side_index == 0
-    cond_part = jnp.where(is_cond, velocity, received)
-    uncond = jnp.where(is_cond, received, velocity)
-    guided_full = uncond + guidance_weight * (cond_part - uncond)
-    partials = jnp.stack([jnp.sum(guided_full * guided_full), jnp.max(jnp.abs(guided_full))])
     n_seq = lax.axis_size(("sz", "sx"))
-    gathered = lax.all_to_all(
-        jnp.broadcast_to(partials[None], (n_seq, 2)), ("sz", "sx"), 0, 0, tiled=True
-    )
-    guided_total = jnp.sum(gathered[:, 0])
-    peak_value = jnp.max(gathered[:, 1])
+    seq_index = lax.axis_index(("sz", "sx"))
+    everything = lax.all_to_all(
+        jnp.broadcast_to(velocity[None], (n_cfg * n_seq,) + velocity.shape),
+        ("cfg", "sz", "sx"),
+        0,
+        0,
+        tiled=True,
+    ).reshape(n_cfg, n_seq, img_dev, velocity.shape[1])
+    cond_part = everything[0]
+    uncond = everything[1]
+    guided_all = uncond + guidance_weight * (cond_part - uncond)
+    guided_total = jnp.sum(guided_all * guided_all)
+    peak_value = jnp.max(jnp.abs(guided_all))
     entries = img_dev * n_seq * velocity.shape[1]
     guided_norm = jnp.sqrt(guided_total / entries + 1e-06)
-    guided = lax.dynamic_slice_in_dim(guided_full, side_index * half_width, half_width, 1)
+    guided_rows = lax.dynamic_index_in_dim(guided_all, seq_index, 0, keepdims=False)
+    guided = lax.dynamic_slice_in_dim(guided_rows, side_index * half_width, half_width, 1)
     latent_next = latent + step_size[0] * guided[None, :, :]
     return (latent_next, jnp.reshape(guided_norm, (1,)), jnp.reshape(peak_value, (1,)))
 

time: 144 us -> 149 us (1.035)
  the two profiles are of different devices: /device:TPU:56 before, /device:TPU:8 now
where the time goes in v5:
time: 149 us; the launch traced here: 148 us
  blocking collectives  47.9 us (32%)
  starting transfers between devices  28.6 us (19%)
  waiting for transfers between devices  27.7 us (19%)
  between operations  17.5 us (12%)
  matrix products  10.8 us (7%)
  local copies, waits for them, and re-layouts  9.86 us (7%)
  other arithmetic  5.71 us (4%)
    all_gather x1, blocking collectives, per_device(): piece = lax.all_gather(key_value[:, 0, 0], 'sz', axis=1, tiled=True)  33.4 us
    all_to_all x1, waiting for transfers between devices, per_device(): lax.all_to_all(jnp.broadcast_to(velocity[None], (n_cfg * n_seq,) + veloci...  16.4 us
    all_gather x1, blocking collectives, per_device(): line_in = lax.all_gather(mlp_in, 'ry', axis=0, tiled=True)  14.5 us
    all_to_all x1, starting transfers between devices, per_device(): lax.all_to_all(jnp.broadcast_to(velocity[None], (n_cfg * n_seq,) + veloci...  9.86 us
    all_to_all x1, waiting for transfers between devices, per_device(): lax.all_to_all(mlp_parts, 'ry', 0, 0, tiled=True).astype(jnp.float32)  7.31 us
    all_to_all x1, starting transfers between devices, per_device(): lax.all_to_all(mlp_parts, 'ry', 0, 0, tiled=True).astype(jnp.float32)  5.22 us
    all_to_all x1, starting transfers between devices, per_device(): got = lax.all_to_all(packed, 'sx', 0, 0, tiled=True)  4.88 us
    all_to_all x1, starting transfers between devices, per_device(): lax.all_to_all(jnp.broadcast_to(query[0, 0][None], (n_x,) + query.shape[2...  4.29 us
  transfers between devices with their start and end apart: 7, of which 3 were waited for; matrix products, arithmetic and copies ran while one was open for 11% of the time, Pallas kernels for 0%

profile of v5, /device:TPU:8, one launch (start us, length us, event | category | flops | bytes accessed | tf_op | source)
XLA Modules:
  0.0 148.1 jit_solution(7585890215729466873)
XLA Ops:
  7.2 0.0 copy-start
  7.2 0.0 all-gather.3.cloned.1.call-start
  7.2 0.7 all-gather.3.cloned.1.call-update
  7.9 1.5 %broadcast_in_dim.43 = bf16[4,32,768]{2,1,0:T(8,128)(2,1)} broadcast(bf16[32,768]{1,0:T(8,128)(2,1)} %bitcast.45), dimensions={1,2} | broadcast | bytes 245760 | tf_op jit(solution)/shard_map/broadcast_in_dim | solution.py:60
  9.4 4.3 %all-to-all-start = ((bf16[4,32,768]{2,1,0:T(8,128)(2,1)}), bf16[4,32,768]{2,1,0:T(8,128)(2,1)S(1)}, u32[]{:S(2)}, u32[]{:S(2)}) async-start(bf16[4,32,768]{2,1,0:T(8,128)(2,1)} %broadcast_in_dim.43), calls=%async_computation | async-start | bytes 393216 | tf_op jit(solution)/shard_map/all_to_all | solution.py:59
  13.7 33.4 %all-gather = bf16[2,1,1,320,768]{4,3,2,1,0:T(8,128)(2,1)S(1)} all-gather(bf16[2,1,1,40,768]{4,3,2,1,0:T(8,128)(2,1)} %param.17), channel_id=2, replica_groups=mesh['cfg'=2,'ry'=4,'rc'=2,'sz'=8,'sx'=4] {'sz'}, dimensions={3}, use_global_device_ids=true | all-gather | bytes 1105920 | tf_op jit(solution)/shard_map/all_gather | solution.py:62
  47.1 0.1 fusion.73
  47.8 0.3 copy.32
  48.1 1.1 copy.34
  49.2 0.0 all-to-all-done
  49.2 0.3 reshape_reshape.3
  49.5 0.6 fusion.2
  50.1 0.1 copy.36
  50.2 2.4 %convolution_bitcast_fusion = f32[128,12,64]{0,2,1:T(8,128)} fusion(bf16[320,12,64]{0,2,1:T(8,128)(2,1)} %bitcast.42, f32[12,320,128]{2,1,0:T(8,128)S(1)} %get-tuple-element.13, f32[128,12]{0,1:T(8,128)S(1)} %get-tuple-element.12, pred[320]{0:T(512)(128)(4,1)S(1)} %fusion.58), kind=kOutput, calls=%fused_computation.11 | convolution fusion | flops 64880640 | bytes 2857280 | tf_op jit(solution)/shard_map/qhk,khd->qhd/dot_general | solution.py:79
  52.6 1.5 copy.35
  54.1 1.0 concatenate.10
  55.1 0.4 fusion.5
  55.5 0.1 copy.38
  55.7 0.5 copy-done.1
  56.1 0.9 pad_maximum_fusion
  57.0 4.9 %all-to-all-start.1 = ((f32[4,32,792]{2,1,0:T(8,128)}), f32[4,32,792]{2,1,0:T(8,128)S(1)}, u32[]{:S(2)}, u32[]{:S(2)}) async-start(f32[4,32,792]{2,1,0:T(8,128)} %pad_maximum_fusion), calls=%async_computation.1 | async-start | bytes 917504 | tf_op jit(solution)/shard_map/all_to_all | solution.py:86
  61.8 1.9 %collective-permute-start = (bf16[1536,384]{1,0:T(8,128)(2,1)}, bf16[1536,384]{1,0:T(8,128)(2,1)S(1)}, u32[]{:S(2)}, u32[]{:S(2)}) collective-permute-start(bf16[1536,384]{1,0:T(8,128)(2,1)} %param.27), channel_id=1, source_target_pairs={{0,32},{32,0},{1,33},{33,1},{2,34},{34,2},{3,35},{35,3},{4,36},{36... | collective-permute-start | bytes 3538952 | tf_op jit(solution)/shard_map/ppermute | solution.py:104
  63.8 2.4 %collective-permute-start.1 = (bf16[384,1536]{1,0:T(8,128)(2,1)}, bf16[384,1536]{1,0:T(8,128)(2,1)}, u32[]{:S(2)}, u32[]{:S(2)}) collective-permute-start(bf16[384,1536]{1,0:T(8,128)(2,1)} %param.28), channel_id=1, source_target_pairs={{0,32},{32,0},{1,33},{33,1},{2,34},{34,2},{3,35},{35,3},{4,36},{36... | collective-permute-start | bytes 3538952 | tf_op jit(solution)/shard_map/ppermute | solution.py:105
  66.2 0.0 copy-done.6
  66.2 0.0 copy-done.7
  66.3 0.0 copy-done.4
  66.3 3.3 %all-to-all-done.1 = f32[4,32,792]{2,1,0:T(8,128)S(1)} async-done(((f32[4,32,792]{2,1,0:T(8,128)}), f32[4,32,792]{2,1,0:T(8,128)S(1)}, u32[]{:S(2)}, u32[]{:S(2)}) %all-to-all-start.1) | async-done | bytes 405536 | tf_op jit(solution)/shard_map/all_to_all | solution.py:86
  69.6 0.1 fusion.49
  69.7 0.0 copy-start.2
  69.7 0.3 mul.158
  70.0 0.3 mul.159
  70.3 0.1 div.37
  70.5 0.1 div.38
  70.6 0.0 all-gather.3.cloned.1.call-done
  70.6 0.0 copy-done.2
  70.6 2.6 %fusion.74 = (f32[32]{0:T(128)S(1)}, f32[32,1536]{1,0:T(8,128)S(1)}) fusion(bf16[768,1536]{0,1:T(8,128)(2,1)} %all-gather.3.cloned.1.call-done, f32[32,768]{1,0:T(8,128)S(1)} %fusion.14, f32[32,768]{1,0:T(8,128)S(1)} %div.38, f32[1536]{0:T(1024)S(1)} %reduce.1, bf16[1,1,32,1536]{3,2,1,0:T(8,128)(2,1)S(1)} %copy-done.2), kind=kOutput, calls=%fused_computation.105 | convolution fusion | flops 75743200 | bytes 2857088 | tf_op jit(solution)/shard_map/dot_general | solution.py:95
  73.2 0.2 multiply_reduce_fusion.2
  73.4 0.1 add_convert_fusion.1
  73.6 14.5 %all_gather.11 = bf16[128,1536]{1,0:T(8,128)(2,1)S(1)} all-gather(bf16[32,1536]{1,0:T(8,128)(2,1)S(1)} %add_convert_fusion.1), channel_id=1, replica_groups=mesh['cfg'=2,'ry'=4,'rc'=2,'sz'=8,'sx'=4] {'ry'}, dimensions={0}, use_global_device_ids=true | all-gather | bytes 491520 | tf_op jit(solution)/shard_map/all_gather | solution.py:106
  88.1 2.3 %fusion.35 = f32[128,1536]{1,0:T(8,128)S(1)} fusion(bf16[384,1536]{1,0:T(8,128)(2,1)} %param.28, bf16[128,1536]{1,0:T(8,128)(2,1)S(1)} %all_gather.11, bf16[1536,384]{1,0:T(8,128)(2,1)} %param.27), kind=kOutput, calls=%fused_computation.51 | convolution fusion | flops 302432256 | bytes 3538944 | tf_op jit(solution)/shard_map/dot_general | solution.py:115
  90.4 0.0 copy-start.8
  90.4 0.0 copy-start.9
  90.5 0.0 copy-start.5
  90.5 0.0 collective-permute-done
  90.5 0.0 collective-permute-done.1
  90.5 2.7 %fusion = bf16[128,1536]{1,0:T(8,128)(2,1)} fusion(f32[128,1536]{1,0:T(8,128)S(1)} %fusion.35, bf16[384,1536]{1,0:T(8,128)(2,1)} %collective-permute-done.1, bf16[128,1536]{1,0:T(8,128)(2,1)S(1)} %all_gather.11, bf16[1536,384]{1,0:T(8,128)(2,1)S(1)} %collective-permute-done), kind=kOutput, calls=%fused_computation.1 | convolution fusion | flops 302825472 | bytes 3932160 | tf_op jit(solution)/shard_map/dot_general | solution.py:116
  93.2 5.2 %all-to-all-start.2 = ((bf16[4,32,1536]{2,1,0:T(8,128)(2,1)}), bf16[4,32,1536]{2,1,0:T(8,128)(2,1)S(1)}, u32[]{:S(2)}, u32[]{:S(2)}) async-start(bf16[4,32,1536]{2,1,0:T(8,128)(2,1)} %bitcast.10), calls=%async_computation.2 | async-start | bytes 786432 | tf_op jit(solution)/shard_map/all_to_all | solution.py:122
  98.4 0.0 copy-done.8
  98.5 0.0 copy-done.9
  98.5 7.3 %all-to-all-done.2 = bf16[4,32,1536]{2,1,0:T(8,128)(2,1)S(1)} async-done(((bf16[4,32,1536]{2,1,0:T(8,128)(2,1)}), bf16[4,32,1536]{2,1,0:T(8,128)(2,1)S(1)}, u32[]{:S(2)}, u32[]{:S(2)}) %all-to-all-start.2) | async-done | bytes 393248 | tf_op jit(solution)/shard_map/all_to_all | solution.py:122
  105.9 0.1 convert_reduce_fusion
  105.9 0.1 fusion.72
  106.1 0.2 multiply_reduce_fusion.1
  106.3 0.2 fusion.33
  106.5 0.1 broadcast_in_dim.46
  106.6 1.4 reshape.131
  108.1 9.9 %all-to-all-start.3 = ((f32[64,1,2048]{2,1,0:T(1,128)}), f32[64,1,2048]{2,1,0:T(1,128)S(1)}, u32[]{:S(2)}, u32[]{:S(2)}) async-start(f32[64,1,2048]{2,1,0:T(1,128)} %reshape.131), calls=%async_computation.3 | async-start | bytes 1048576 | tf_op jit(solution)/shard_map/all_to_all | solution.py:132
  118.6 16.4 %all-to-all-done.3 = f32[64,1,2048]{2,1,0:T(1,128)S(1)} async-done(((f32[64,1,2048]{2,1,0:T(1,128)}), f32[64,1,2048]{2,1,0:T(1,128)S(1)}, u32[]{:S(2)}, u32[]{:S(2)}) %all-to-all-start.3) | async-done | bytes 524320 | tf_op jit(solution)/shard_map/all_to_all | solution.py:132
  135.1 0.5 broadcast.199
  135.6 1.9 %reduce.9 = f32[64,2048]{1,0:T(8,128)S(1)} reduce(f32[64,1,2048]{2,1,0:T(1,128)S(1)} %all-to-all-done.3, f32[]{:T(128)} %broadcast.199), dimensions={1}, to_apply=%all_to_all.15.reduce_sub_computation | reduce | bytes 1048580 | tf_op jit(solution)/shard_map/all_to_all | solution.py:132
  137.5 0.4 reshape.132
  137.9 0.8 abs_reduce_fusion
  139.4 0.0 copy-done.3
  139.4 0.7 multiply_add_fusion.1
  (20 shorter events, 0.2 us)
Async XLA Ops:
  7.2 99.1 %copy-start = (bf16[1536,64]{0,1:T(8,128)(2,1)S(1)}, bf16[1536,64]{0,1:T(8,128)(2,1)}, u32[]{:S(2)}) copy-start(bf16[1536,64]{0,1:T(8,128)(2,1)} %param.29) | copy-start | bytes 589828
  7.2 63.4 %all-gather.3.cloned.1.call-start = ((), (), s32[]{:S(2)}) async-start(), calls=%async_computation.4 | async-start | bytes 2654208 | tf_op jit(solution)/shard_map/all_gather | solution.py:97
  9.4 39.8 %all-to-all-start = ((bf16[4,32,768]{2,1,0:T(8,128)(2,1)}), bf16[4,32,768]{2,1,0:T(8,128)(2,1)S(1)}, u32[]{:S(2)}, u32[]{:S(2)}) async-start(bf16[4,32,768]{2,1,0:T(8,128)(2,1)} %broadcast_in_dim.43), calls=%async_computation | async-start | bytes 393216 | tf_op jit(solution)/shard_map/all_to_all | solution.py:59
  55.1 1.0 copy-start.1
  55.1 11.1 %copy-start.6 = (f32[1,1,1536]{2,1,0:T(1,128)S(1)}, f32[1,1,1536]{2,1,0:T(1,128)}, u32[]{:S(2)}) copy-start(f32[1,1,1536]{2,1,0:T(1,128)} %param.20) | copy-start | bytes 18436
  55.1 11.1 %copy-start.7 = (f32[1,1,1536]{2,1,0:T(1,128)S(1)}, f32[1,1,1536]{2,1,0:T(1,128)}, u32[]{:S(2)}) copy-start(f32[1,1,1536]{2,1,0:T(1,128)} %param.21) | copy-start | bytes 18436
  55.1 11.1 %copy-start.4 = (f32[1,1,1536]{2,1,0:T(1,128)S(1)}, f32[1,1,1536]{2,1,0:T(1,128)}, u32[]{:S(2)}) copy-start(f32[1,1,1536]{2,1,0:T(1,128)} %param.22) | copy-start | bytes 18436
  57.0 12.6 %all-to-all-start.1 = ((f32[4,32,792]{2,1,0:T(8,128)}), f32[4,32,792]{2,1,0:T(8,128)S(1)}, u32[]{:S(2)}, u32[]{:S(2)}) async-start(f32[4,32,792]{2,1,0:T(8,128)} %pad_maximum_fusion), calls=%async_computation.1 | async-start | bytes 917504 | tf_op jit(solution)/shard_map/all_to_all | solution.py:86
  61.8 28.6 %collective-permute-start = (bf16[1536,384]{1,0:T(8,128)(2,1)}, bf16[1536,384]{1,0:T(8,128)(2,1)S(1)}, u32[]{:S(2)}, u32[]{:S(2)}) collective-permute-start(bf16[1536,384]{1,0:T(8,128)(2,1)} %param.27), channel_id=1, source_target_pairs={{0,32},{32,0},{1,33},{33,1},{2,34},{34,2},{3,35},{35,3},{4,36},{36... | collective-permute-start | bytes 3538952 | tf_op jit(solution)/shard_map/ppermute | solution.py:104
  63.8 26.7 %collective-permute-start.1 = (bf16[384,1536]{1,0:T(8,128)(2,1)}, bf16[384,1536]{1,0:T(8,128)(2,1)}, u32[]{:S(2)}, u32[]{:S(2)}) collective-permute-start(bf16[384,1536]{1,0:T(8,128)(2,1)} %param.28), channel_id=1, source_target_pairs={{0,32},{32,0},{1,33},{33,1},{2,34},{34,2},{3,35},{35,3},{4,36},{36... | collective-permute-start | bytes 3538952 | tf_op jit(solution)/shard_map/ppermute | solution.py:105
  69.7 1.0 copy-start.2
  90.4 8.0 %copy-start.8 = (f32[1,1,1536]{2,1,0:T(1,128)S(1)}, f32[1,1,1536]{2,1,0:T(1,128)}, u32[]{:S(2)}) copy-start(f32[1,1,1536]{2,1,0:T(1,128)} %param.23) | copy-start | bytes 18436
  90.4 8.0 %copy-start.9 = (f32[1,1,1536]{2,1,0:T(1,128)S(1)}, f32[1,1,1536]{2,1,0:T(1,128)}, u32[]{:S(2)}) copy-start(f32[1,1,1536]{2,1,0:T(1,128)} %param.24) | copy-start | bytes 18436
  90.5 8.1 %copy-start.5 = (f32[1,1,1536]{2,1,0:T(1,128)S(1)}, f32[1,1,1536]{2,1,0:T(1,128)}, u32[]{:S(2)}) copy-start(f32[1,1,1536]{2,1,0:T(1,128)} %param.25) | copy-start | bytes 18436
  93.2 12.6 %all-to-all-start.2 = ((bf16[4,32,1536]{2,1,0:T(8,128)(2,1)}), bf16[4,32,1536]{2,1,0:T(8,128)(2,1)S(1)}, u32[]{:S(2)}, u32[]{:S(2)}) async-start(bf16[4,32,1536]{2,1,0:T(8,128)(2,1)} %bitcast.10), calls=%async_computation.2 | async-start | bytes 786432 | tf_op jit(solution)/shard_map/all_to_all | solution.py:122
  108.1 27.0 %all-to-all-start.3 = ((f32[64,1,2048]{2,1,0:T(1,128)}), f32[64,1,2048]{2,1,0:T(1,128)S(1)}, u32[]{:S(2)}, u32[]{:S(2)}) async-start(f32[64,1,2048]{2,1,0:T(1,128)} %reshape.131), calls=%async_computation.3 | async-start | bytes 1048576 | tf_op jit(solution)/shard_map/all_to_all | solution.py:132
  135.6 3.9 %copy-start.3 = (f32[1,32,32]{2,1,0:T(8,128)S(1)}, f32[1,32,32]{2,1,0:T(8,128)}, u32[]{:S(2)}) copy-start(f32[1,32,32]{2,1,0:T(8,128)} %param.30) | copy-start | bytes 12292
Sparse Core Ops, SparseCore 0:
  10.1 44.0 all-gather.2

commit v6 on v4

--- a/solution.py
+++ b/solution.py
@@ -103,7 +103,13 @@
     pair = [(0, 1), (1, 0)]
     up_other = lax.ppermute(w_up, "rc", pair)
     down_other = lax.ppermute(w_down, "rc", pair)
-    line_in = lax.all_gather(mlp_in, "ry", axis=0, tiled=True)
+    y_index = lax.axis_index("ry")
+    shifts = range(1, n_y)
+    line_blocks = jnp.stack(
+        [mlp_in]
+        + [lax.ppermute(mlp_in, "ry", [(i, (i + k) % n_y) for i in range(n_y)]) for k in shifts]
+    )
+    line_in = line_blocks.reshape(n_y * img_dev, mlp_in.shape[1])
     inner_own = jax.nn.gelu(
         jnp.dot(line_in, w_up, preferred_element_type=jnp.float32), approximate=True
     ).astype(jnp.bfloat16)
@@ -118,9 +124,12 @@
         .astype(jnp.bfloat16)
         .reshape(n_y, img_dev, w_down.shape[1])
     )
-    mlp_out = jnp.sum(
-        lax.all_to_all(mlp_parts, "ry", 0, 0, tiled=True).astype(jnp.float32), axis=0
-    )
+    mlp_total = mlp_parts[0].astype(jnp.float32)
+    for k in shifts:
+        mlp_total = mlp_total + lax.ppermute(
+            mlp_parts[k], "ry", [(i, (i - k) % n_y) for i in range(n_y)]
+        ).astype(jnp.float32)
+    mlp_out = mlp_total
     hidden_two = hidden + mlp_gate[0, 0][None, :] * mlp_out
     modulated = modulate_rows(hidden_two, shift[0, 0], scale[0, 0])
     velocity = jnp.dot(modulated, w_out, preferred_element_type=jnp.float32)

time: 144 us -> 145 us (level); the launches traced: 143 us -> 143 us
  blocking collectives: 48 us -> 33.4 us
  starting transfers between devices: 29 us -> 41.9 us
  waiting for transfers between devices: 24.4 us -> 26 us
    ppermute x0 -> x6, starting transfers between devices: none -> 19.5 us  [the longest x3 9.88 us: per_device(): lax.ppermute(mlp_in, 'ry', [(i, (i + k) % n_y) for i in range(n_y)])]
    all_gather x1 -> x0, blocking collectives: 14.7 us -> none  [per_device(): line_in = lax.all_gather(mlp_in, 'ry', axis=0, tiled=True)]
    ppermute x0 -> x6, waiting for transfers between devices: none -> 7.92 us  [the longest x3 4.93 us: per_device(): lax.ppermute(mlp_in, 'ry', [(i, (i + k) % n_y) for i in range(n_y)])]
    all_to_all x1 -> x0, waiting for transfers between devices: 6.41 us -> none  [per_device(): lax.all_to_all(mlp_parts, 'ry', 0, 0, tiled=True).astype(jnp.float32)]
    all_to_all x1 -> x0, starting transfers between devices: 5.88 us -> none  [per_device(): lax.all_to_all(mlp_parts, 'ry', 0, 0, tiled=True).astype(jnp.float32)]
  transfers between devices with their start and end apart: 8 -> 13, of which waited for: 4 -> 7; matrix products, arithmetic and copies ran while one was open for 12% -> 12% of each run, Pallas kernels for 0% -> 0%
where the time goes in v6:
time: 145 us; the launch traced here: 143 us
  starting transfers between devices  41.9 us (29%)
  blocking collectives  33.4 us (23%)
  waiting for transfers between devices  26 us (18%)
  between operations  17.6 us (12%)
  matrix products  10.1 us (7%)
  local copies, waits for them, and re-layouts  8.04 us (6%)
  other arithmetic  5.71 us (4%)
    all_gather x1, blocking collectives, per_device(): piece = lax.all_gather(key_value[:, 0, 0], 'sz', axis=1, tiled=True)  33.4 us
    ppermute x3, starting transfers between devices, per_device(): lax.ppermute(mlp_in, 'ry', [(i, (i + k) % n_y) for i in range(n_y)])  9.88 us
    ppermute x3, starting transfers between devices, per_device(): lax.ppermute(mlp_parts[k], 'ry', [(i, (i - k) % n_y) for i in range(n_y)])  9.65 us
    all_to_all x1, waiting for transfers between devices, per_device(): lax.all_to_all(jnp.broadcast_to(partials[None], (n_seq, 2)), ('sz', 'sx')...  8.88 us
    ppermute x1, waiting for transfers between devices, swapped(): return lax.ppermute(block, axis, route)  5.24 us
    all_to_all x1, starting transfers between devices, per_device(): lax.all_to_all(jnp.broadcast_to(partials[None], (n_seq, 2)), ('sz', 'sx')...  4.98 us
    ppermute x3, waiting for transfers between devices, per_device(): lax.ppermute(mlp_in, 'ry', [(i, (i + k) % n_y) for i in range(n_y)])  4.93 us
    all_to_all x1, starting transfers between devices, per_device(): got = lax.all_to_all(packed, 'sx', 0, 0, tiled=True)  4.9 us
  transfers between devices with their start and end apart: 13, of which 7 were waited for; matrix products, arithmetic and copies ran while one was open for 12% of the time, Pallas kernels for 0%

profile of v6, /device:TPU:56, one launch (start us, length us, event | category | flops | bytes accessed | tf_op | source)
XLA Modules:
  0.0 142.6 jit_solution(1287605217383720886)
XLA Ops:
  7.2 0.0 copy-start
  7.2 0.0 all-gather.3.cloned.1.call-start
  7.2 0.7 all-gather.3.cloned.1.call-update
  7.9 1.5 %broadcast_in_dim.43 = bf16[4,32,768]{2,1,0:T(8,128)(2,1)} broadcast(bf16[32,768]{1,0:T(8,128)(2,1)} %bitcast.60), dimensions={1,2} | broadcast | bytes 245760 | tf_op jit(solution)/shard_map/broadcast_in_dim | solution.py:60
  9.4 4.3 %all-to-all-start = ((bf16[4,32,768]{2,1,0:T(8,128)(2,1)}), bf16[4,32,768]{2,1,0:T(8,128)(2,1)S(1)}, u32[]{:S(2)}, u32[]{:S(2)}) async-start(bf16[4,32,768]{2,1,0:T(8,128)(2,1)} %broadcast_in_dim.43), calls=%async_computation | async-start | bytes 393216 | tf_op jit(solution)/shard_map/all_to_all | solution.py:59
  13.7 33.4 %all-gather = bf16[2,1,1,320,768]{4,3,2,1,0:T(8,128)(2,1)S(1)} all-gather(bf16[2,1,1,40,768]{4,3,2,1,0:T(8,128)(2,1)} %param.17), channel_id=2, replica_groups=mesh['cfg'=2,'ry'=4,'rc'=2,'sz'=8,'sx'=4] {'sz'}, dimensions={3}, use_global_device_ids=true | all-gather | bytes 1105920 | tf_op jit(solution)/shard_map/all_gather | solution.py:62
  47.1 0.1 fusion.70
  47.8 0.3 copy.32
  48.1 1.1 copy.34
  49.2 0.3 reshape_reshape.3
  49.5 0.6 fusion.2
  50.1 0.1 copy.36
  50.2 2.3 %convolution_bitcast_fusion = f32[128,12,64]{0,2,1:T(8,128)} fusion(bf16[320,12,64]{0,2,1:T(8,128)(2,1)} %bitcast.54, f32[12,320,128]{2,1,0:T(8,128)S(1)} %get-tuple-element.18, f32[128,12]{0,1:T(8,128)S(1)} %get-tuple-element.17, pred[320]{0:T(512)(128)(4,1)S(1)} %fusion.56), kind=kOutput, calls=%fused_computation.11 | convolution fusion | flops 64880640 | bytes 2857280 | tf_op jit(solution)/shard_map/qhk,khd->qhd/dot_general | solution.py:79
  52.6 1.5 %copy.35 = f32[128,12,64]{2,1,0:T(8,128)S(1)} copy(f32[128,12,64]{0,2,1:T(8,128)} %convolution_bitcast_fusion) | data formatting | bytes 786432 | tf_op jit(solution)/shard_map/qhk,khd->qhd/transpose | solution.py:79
  54.1 1.0 concatenate.10
  55.1 0.0 copy-start.9
  55.1 0.0 copy-start.4
  55.1 0.4 fusion.5
  55.6 0.1 copy.39
  55.7 0.4 copy-done.1
  56.1 0.9 pad_maximum_fusion
  57.0 4.9 %all-to-all-start.1 = ((f32[4,32,792]{2,1,0:T(8,128)}), f32[4,32,792]{2,1,0:T(8,128)S(1)}, u32[]{:S(2)}, u32[]{:S(2)}) async-start(f32[4,32,792]{2,1,0:T(8,128)} %pad_maximum_fusion), calls=%async_computation.1 | async-start | bytes 917504 | tf_op jit(solution)/shard_map/all_to_all | solution.py:86
  61.9 1.9 %collective-permute-start.3 = (bf16[1536,384]{1,0:T(8,128)(2,1)}, bf16[1536,384]{1,0:T(8,128)(2,1)S(1)}, u32[]{:S(2)}, u32[]{:S(2)}) collective-permute-start(bf16[1536,384]{1,0:T(8,128)(2,1)} %param.27), channel_id=1, source_target_pairs={{0,32},{32,0},{1,33},{33,1},{2,34},{34,2},{3,35},{35,3},{4,36},{36... | collective-permute-start | bytes 3538952 | tf_op jit(solution)/shard_map/ppermute | solution.py:104
  63.8 2.4 %collective-permute-start.4 = (bf16[384,1536]{1,0:T(8,128)(2,1)}, bf16[384,1536]{1,0:T(8,128)(2,1)}, u32[]{:S(2)}, u32[]{:S(2)}) collective-permute-start(bf16[384,1536]{1,0:T(8,128)(2,1)} %param.28), channel_id=1, source_target_pairs={{0,32},{32,0},{1,33},{33,1},{2,34},{34,2},{3,35},{35,3},{4,36},{36... | collective-permute-start | bytes 3538952 | tf_op jit(solution)/shard_map/ppermute | solution.py:105
  66.4 3.2 %all-to-all-done.1 = f32[4,32,792]{2,1,0:T(8,128)S(1)} async-done(((f32[4,32,792]{2,1,0:T(8,128)}), f32[4,32,792]{2,1,0:T(8,128)S(1)}, u32[]{:S(2)}, u32[]{:S(2)}) %all-to-all-start.1) | async-done | bytes 405536 | tf_op jit(solution)/shard_map/all_to_all | solution.py:86
  69.6 0.1 fusion.47
  69.7 0.0 copy-start.2
  69.7 0.3 mul.156
  70.0 0.3 mul.157
  70.3 0.1 div.37
  70.5 0.1 div.38
  70.6 0.0 all-gather.3.cloned.1.call-done
  70.7 2.6 %fusion.72 = (f32[32]{0:T(128)S(1)}, f32[32,1536]{1,0:T(8,128)S(1)}) fusion(bf16[768,1536]{0,1:T(8,128)(2,1)} %all-gather.3.cloned.1.call-done, f32[32,768]{1,0:T(8,128)S(1)} %fusion.12, f32[32,768]{1,0:T(8,128)S(1)} %div.38, f32[1536]{0:T(1024)S(1)} %reduce.3, bf16[1,1,32,1536]{3,2,1,0:T(8,128)(2,1)S(1)} %copy-done.2), kind=kOutput, calls=%fused_computation.107 | convolution fusion | flops 75743200 | bytes 2857088 | tf_op jit(solution)/shard_map/dot_general | solution.py:95
  73.2 0.2 multiply_reduce_fusion.1
  73.5 0.1 add_convert_fusion.1
  73.6 4.6 %collective-permute-start = (bf16[32,1536]{1,0:T(8,128)(2,1)S(1)}, bf16[32,1536]{1,0:T(8,128)(2,1)S(1)}, u32[]{:S(2)}, u32[]{:S(2)}) collective-permute-start(bf16[32,1536]{1,0:T(8,128)(2,1)S(1)} %add_convert_fusion.1), channel_id=1, source_target_pairs={{0,64},{64,128},{128,192},{192,0},{1,65},{65,129},{129,193},{193,1... | collective-permute-start | bytes 294920 | tf_op jit(solution)/shard_map/ppermute | solution.py:110
  78.2 2.0 %collective-permute-start.1 = (bf16[32,1536]{1,0:T(8,128)(2,1)S(1)}, bf16[32,1536]{1,0:T(8,128)(2,1)S(1)}, u32[]{:S(2)}, u32[]{:S(2)}) collective-permute-start(bf16[32,1536]{1,0:T(8,128)(2,1)S(1)} %add_convert_fusion.1), channel_id=1, source_target_pairs={{0,128},{64,192},{128,0},{192,64},{1,129},{65,193},{129,1},{193,65... | collective-permute-start | bytes 294920 | tf_op jit(solution)/shard_map/ppermute | solution.py:110
  80.2 3.3 %collective-permute-start.2 = (bf16[32,1536]{1,0:T(8,128)(2,1)S(1)}, bf16[32,1536]{1,0:T(8,128)(2,1)S(1)}, u32[]{:S(2)}, u32[]{:S(2)}) collective-permute-start(bf16[32,1536]{1,0:T(8,128)(2,1)S(1)} %add_convert_fusion.1), channel_id=1, source_target_pairs={{0,192},{64,0},{128,64},{192,128},{1,193},{65,1},{129,65},{193,129... | collective-permute-start | bytes 294920 | tf_op jit(solution)/shard_map/ppermute | solution.py:110
  83.5 0.1 fusion.87
  83.6 2.5 %collective-permute-done.1 = bf16[32,1536]{1,0:T(8,128)(2,1)S(1)} collective-permute-done((bf16[32,1536]{1,0:T(8,128)(2,1)S(1)}, bf16[32,1536]{1,0:T(8,128)(2,1)S(1)}, u32[]{:S(2)}, u32[]{:S(2)}) %collective-permute-start.1) | collective-permute-done | bytes 98336 | tf_op jit(solution)/shard_map/ppermute | solution.py:110
  86.1 2.4 %collective-permute-done.2 = bf16[32,1536]{1,0:T(8,128)(2,1)S(1)} collective-permute-done((bf16[32,1536]{1,0:T(8,128)(2,1)S(1)}, bf16[32,1536]{1,0:T(8,128)(2,1)S(1)}, u32[]{:S(2)}, u32[]{:S(2)}) %collective-permute-start.2) | collective-permute-done | bytes 98336 | tf_op jit(solution)/shard_map/ppermute | solution.py:110
  88.5 0.1 pad_maximum_fusion.1
  88.6 2.3 %fusion.33 = f32[128,1536]{1,0:T(8,128)S(1)} fusion(bf16[384,1536]{1,0:T(8,128)(2,1)} %param.28, bf16[128,1536]{1,0:T(8,128)(2,1)S(1)} %bitcast.51, bf16[1536,384]{1,0:T(8,128)(2,1)} %param.27), kind=kOutput, calls=%fused_computation.46 | convolution fusion | flops 302432256 | bytes 3538944 | tf_op jit(solution)/shard_map/dot_general | solution.py:121
  90.9 0.0 copy-start.5
  91.0 2.0 %fusion = bf16[128,1536]{1,0:T(8,128)(2,1)S(1)} fusion(f32[128,1536]{1,0:T(8,128)S(1)} %fusion.33, bf16[384,1536]{1,0:T(8,128)(2,1)} %collective-permute-done.4, bf16[128,1536]{1,0:T(8,128)(2,1)S(1)} %bitcast.52, bf16[1536,384]{1,0:T(8,128)(2,1)S(1)} %collective-permute-done.3), kind=kOutput, calls=%fused_computation.1 | convolution fusion | flops 302825472 | bytes 3932160 | tf_op jit(solution)/shard_map/dot_general | solution.py:122
  93.0 0.0 copy-start.3
  93.0 1.9 %collective-permute-start.5 = (bf16[32,1536]{1,0:T(8,128)(2,1)S(1)}, bf16[32,1536]{1,0:T(8,128)(2,1)S(1)}, u32[]{:S(2)}, u32[]{:S(2)}) collective-permute-start(bf16[32,1536]{1,0:T(8,128)(2,1)S(1)} %get-tuple-element.14), channel_id=1, source_target_pairs={{0,192},{64,0},{128,64},{192,128},{1,193},{65,1},{129,65},{193,129... | collective-permute-start | bytes 294920 | tf_op jit(solution)/shard_map/ppermute | solution.py:129
  94.9 3.0 %collective-permute-start.6 = (bf16[32,1536]{1,0:T(8,128)(2,1)S(1)}, bf16[32,1536]{1,0:T(8,128)(2,1)S(1)}, u32[]{:S(2)}, u32[]{:S(2)}) collective-permute-start(bf16[32,1536]{1,0:T(8,128)(2,1)S(1)} %get-tuple-element.16), channel_id=1, source_target_pairs={{0,128},{64,192},{128,0},{192,64},{1,129},{65,193},{129,1},{193,65... | collective-permute-start | bytes 294920 | tf_op jit(solution)/shard_map/ppermute | solution.py:129
  98.0 4.7 %collective-permute-start.7 = (bf16[32,1536]{1,0:T(8,128)(2,1)S(1)}, bf16[32,1536]{1,0:T(8,128)(2,1)S(1)}, u32[]{:S(2)}, u32[]{:S(2)}) collective-permute-start(bf16[32,1536]{1,0:T(8,128)(2,1)S(1)} %get-tuple-element.15), channel_id=1, source_target_pairs={{0,64},{64,128},{128,192},{192,0},{1,65},{65,129},{129,193},{193,1... | collective-permute-start | bytes 294920 | tf_op jit(solution)/shard_map/ppermute | solution.py:129
  102.7 1.9 %collective-permute-done.6 = bf16[32,1536]{1,0:T(8,128)(2,1)S(1)} collective-permute-done((bf16[32,1536]{1,0:T(8,128)(2,1)S(1)}, bf16[32,1536]{1,0:T(8,128)(2,1)S(1)}, u32[]{:S(2)}, u32[]{:S(2)}) %collective-permute-start.6) | collective-permute-done | bytes 98336 | tf_op jit(solution)/shard_map/ppermute | solution.py:129
  104.6 1.1 collective-permute-done.7
  105.7 0.2 fusion.69
  105.9 0.2 multiply_reduce_fusion
  106.1 0.2 fusion.31
  106.4 3.8 %collective-permute-start.8 = (f32[32,64]{1,0:T(8,128)S(1)}, f32[32,64]{1,0:T(8,128)S(1)}, u32[]{:S(2)}, u32[]{:S(2)}) collective-permute-start(f32[32,64]{1,0:T(8,128)S(1)} %fusion.31), channel_id=1, source_target_pairs={{0,256},{256,0},{1,257},{257,1},{2,258},{258,2},{3,259},{259,3},{4... | collective-permute-start | bytes 24584 | tf_op jit(solution)/shard_map/ppermute | solution.py:22
  110.8 5.2 %collective-permute-done.8 = f32[32,64]{1,0:T(8,128)S(1)} collective-permute-done((f32[32,64]{1,0:T(8,128)S(1)}, f32[32,64]{1,0:T(8,128)S(1)}, u32[]{:S(2)}, u32[]{:S(2)}) %collective-permute-start.8) | collective-permute-done | bytes 8224 | tf_op jit(solution)/shard_map/ppermute | solution.py:22
  116.1 0.6 multiply_reduce_fusion.2
  116.7 1.4 pad_maximum_fusion.2
  118.1 0.6 broadcast_in_dim.46
  118.7 5.0 %all-to-all-start.2 = ((f32[32,1,2]{2,1,0:T(1,128)}), f32[32,1,2]{2,1,0:T(1,128)S(1)}, u32[]{:S(2)}, u32[]{:S(2)}) async-start(f32[32,1,2]{2,1,0:T(1,128)} %broadcast_in_dim.46), calls=%async_computation.2 | async-start | bytes 32768 | tf_op jit(solution)/shard_map/all_to_all | solution.py:145
  123.7 0.7 bitcast_add_fusion
  124.4 8.9 %all-to-all-done.2 = f32[32,1,2]{2,1,0:T(1,128)S(1)} async-done(((f32[32,1,2]{2,1,0:T(1,128)}), f32[32,1,2]{2,1,0:T(1,128)S(1)}, u32[]{:S(2)}, u32[]{:S(2)}) %all-to-all-start.2) | async-done | bytes 288 | tf_op jit(solution)/shard_map/all_to_all | solution.py:145
  133.2 0.1 copy.38
  133.3 0.6 slice_reduce_fusion.1
  (32 shorter events, 0.3 us)
Async XLA Ops:
  7.2 99.0 %copy-start = (bf16[1536,64]{0,1:T(8,128)(2,1)S(1)}, bf16[1536,64]{0,1:T(8,128)(2,1)}, u32[]{:S(2)}) copy-start(bf16[1536,64]{0,1:T(8,128)(2,1)} %param.29) | copy-start | bytes 589828
  7.2 63.5 %all-gather.3.cloned.1.call-start = ((), (), s32[]{:S(2)}) async-start(), calls=%async_computation.3 | async-start | bytes 2654208 | tf_op jit(solution)/shard_map/all_gather | solution.py:97
  9.4 39.8 %all-to-all-start = ((bf16[4,32,768]{2,1,0:T(8,128)(2,1)}), bf16[4,32,768]{2,1,0:T(8,128)(2,1)S(1)}, u32[]{:S(2)}, u32[]{:S(2)}) async-start(bf16[4,32,768]{2,1,0:T(8,128)(2,1)} %broadcast_in_dim.43), calls=%async_computation | async-start | bytes 393216 | tf_op jit(solution)/shard_map/all_to_all | solution.py:59
  55.1 1.0 copy-start.1
  55.1 11.1 %copy-start.6 = (f32[1,1,1536]{2,1,0:T(1,128)S(1)}, f32[1,1,1536]{2,1,0:T(1,128)}, u32[]{:S(2)}) copy-start(f32[1,1,1536]{2,1,0:T(1,128)} %param.20) | copy-start | bytes 18436
  55.1 11.1 %copy-start.7 = (f32[1,1,1536]{2,1,0:T(1,128)S(1)}, f32[1,1,1536]{2,1,0:T(1,128)}, u32[]{:S(2)}) copy-start(f32[1,1,1536]{2,1,0:T(1,128)} %param.21) | copy-start | bytes 18436
  55.1 11.2 %copy-start.8 = (f32[1,1,1536]{2,1,0:T(1,128)S(1)}, f32[1,1,1536]{2,1,0:T(1,128)}, u32[]{:S(2)}) copy-start(f32[1,1,1536]{2,1,0:T(1,128)} %param.23) | copy-start | bytes 18436
  55.1 11.2 %copy-start.9 = (f32[1,1,1536]{2,1,0:T(1,128)S(1)}, f32[1,1,1536]{2,1,0:T(1,128)}, u32[]{:S(2)}) copy-start(f32[1,1,1536]{2,1,0:T(1,128)} %param.24) | copy-start | bytes 18436
  55.1 11.2 %copy-start.4 = (f32[1,1,1536]{2,1,0:T(1,128)S(1)}, f32[1,1,1536]{2,1,0:T(1,128)}, u32[]{:S(2)}) copy-start(f32[1,1,1536]{2,1,0:T(1,128)} %param.22) | copy-start | bytes 18436
  57.0 12.6 %all-to-all-start.1 = ((f32[4,32,792]{2,1,0:T(8,128)}), f32[4,32,792]{2,1,0:T(8,128)S(1)}, u32[]{:S(2)}, u32[]{:S(2)}) async-start(f32[4,32,792]{2,1,0:T(8,128)} %pad_maximum_fusion), calls=%async_computation.1 | async-start | bytes 917504 | tf_op jit(solution)/shard_map/all_to_all | solution.py:86
  61.9 29.1 %collective-permute-start.3 = (bf16[1536,384]{1,0:T(8,128)(2,1)}, bf16[1536,384]{1,0:T(8,128)(2,1)S(1)}, u32[]{:S(2)}, u32[]{:S(2)}) collective-permute-start(bf16[1536,384]{1,0:T(8,128)(2,1)} %param.27), channel_id=1, source_target_pairs={{0,32},{32,0},{1,33},{33,1},{2,34},{34,2},{3,35},{35,3},{4,36},{36... | collective-permute-start | bytes 3538952 | tf_op jit(solution)/shard_map/ppermute | solution.py:104
  63.8 27.2 %collective-permute-start.4 = (bf16[384,1536]{1,0:T(8,128)(2,1)}, bf16[384,1536]{1,0:T(8,128)(2,1)}, u32[]{:S(2)}, u32[]{:S(2)}) collective-permute-start(bf16[384,1536]{1,0:T(8,128)(2,1)} %param.28), channel_id=1, source_target_pairs={{0,32},{32,0},{1,33},{33,1},{2,34},{34,2},{3,35},{35,3},{4,36},{36... | collective-permute-start | bytes 3538952 | tf_op jit(solution)/shard_map/ppermute | solution.py:105
  69.7 1.0 copy-start.2
  73.6 10.0 %collective-permute-start = (bf16[32,1536]{1,0:T(8,128)(2,1)S(1)}, bf16[32,1536]{1,0:T(8,128)(2,1)S(1)}, u32[]{:S(2)}, u32[]{:S(2)}) collective-permute-start(bf16[32,1536]{1,0:T(8,128)(2,1)S(1)} %add_convert_fusion.1), channel_id=1, source_target_pairs={{0,64},{64,128},{128,192},{192,0},{1,65},{65,129},{129,193},{193,1... | collective-permute-start | bytes 294920 | tf_op jit(solution)/shard_map/ppermute | solution.py:110
  78.2 7.9 %collective-permute-start.1 = (bf16[32,1536]{1,0:T(8,128)(2,1)S(1)}, bf16[32,1536]{1,0:T(8,128)(2,1)S(1)}, u32[]{:S(2)}, u32[]{:S(2)}) collective-permute-start(bf16[32,1536]{1,0:T(8,128)(2,1)S(1)} %add_convert_fusion.1), channel_id=1, source_target_pairs={{0,128},{64,192},{128,0},{192,64},{1,129},{65,193},{129,1},{193,65... | collective-permute-start | bytes 294920 | tf_op jit(solution)/shard_map/ppermute | solution.py:110
  80.2 8.3 %collective-permute-start.2 = (bf16[32,1536]{1,0:T(8,128)(2,1)S(1)}, bf16[32,1536]{1,0:T(8,128)(2,1)S(1)}, u32[]{:S(2)}, u32[]{:S(2)}) collective-permute-start(bf16[32,1536]{1,0:T(8,128)(2,1)S(1)} %add_convert_fusion.1), channel_id=1, source_target_pairs={{0,192},{64,0},{128,64},{192,128},{1,193},{65,1},{129,65},{193,129... | collective-permute-start | bytes 294920 | tf_op jit(solution)/shard_map/ppermute | solution.py:110
  90.9 11.8 %copy-start.5 = (f32[1,1,1536]{2,1,0:T(1,128)S(1)}, f32[1,1,1536]{2,1,0:T(1,128)}, u32[]{:S(2)}) copy-start(f32[1,1,1536]{2,1,0:T(1,128)} %param.25) | copy-start | bytes 18436
  93.0 30.7 %copy-start.3 = (f32[1,32,32]{2,1,0:T(8,128)S(1)}, f32[1,32,32]{2,1,0:T(8,128)}, u32[]{:S(2)}) copy-start(f32[1,32,32]{2,1,0:T(8,128)} %param.30) | copy-start | bytes 12292
  93.0 9.7 %collective-permute-start.5 = (bf16[32,1536]{1,0:T(8,128)(2,1)S(1)}, bf16[32,1536]{1,0:T(8,128)(2,1)S(1)}, u32[]{:S(2)}, u32[]{:S(2)}) collective-permute-start(bf16[32,1536]{1,0:T(8,128)(2,1)S(1)} %get-tuple-element.14), channel_id=1, source_target_pairs={{0,192},{64,0},{128,64},{192,128},{1,193},{65,1},{129,65},{193,129... | collective-permute-start | bytes 294920 | tf_op jit(solution)/shard_map/ppermute | solution.py:129
  94.9 9.7 %collective-permute-start.6 = (bf16[32,1536]{1,0:T(8,128)(2,1)S(1)}, bf16[32,1536]{1,0:T(8,128)(2,1)S(1)}, u32[]{:S(2)}, u32[]{:S(2)}) collective-permute-start(bf16[32,1536]{1,0:T(8,128)(2,1)S(1)} %get-tuple-element.16), channel_id=1, source_target_pairs={{0,128},{64,192},{128,0},{192,64},{1,129},{65,193},{129,1},{193,65... | collective-permute-start | bytes 294920 | tf_op jit(solution)/shard_map/ppermute | solution.py:129
  98.0 7.8 %collective-permute-start.7 = (bf16[32,1536]{1,0:T(8,128)(2,1)S(1)}, bf16[32,1536]{1,0:T(8,128)(2,1)S(1)}, u32[]{:S(2)}, u32[]{:S(2)}) collective-permute-start(bf16[32,1536]{1,0:T(8,128)(2,1)S(1)} %get-tuple-element.15), channel_id=1, source_target_pairs={{0,64},{64,128},{128,192},{192,0},{1,65},{65,129},{129,193},{193,1... | collective-permute-start | bytes 294920 | tf_op jit(solution)/shard_map/ppermute | solution.py:129
  106.4 9.7 %collective-permute-start.8 = (f32[32,64]{1,0:T(8,128)S(1)}, f32[32,64]{1,0:T(8,128)S(1)}, u32[]{:S(2)}, u32[]{:S(2)}) collective-permute-start(f32[32,64]{1,0:T(8,128)S(1)} %fusion.31), channel_id=1, source_target_pairs={{0,256},{256,0},{1,257},{257,1},{2,258},{258,2},{3,259},{259,3},{4... | collective-permute-start | bytes 24584 | tf_op jit(solution)/shard_map/ppermute | solution.py:22
  118.7 14.6 %all-to-all-start.2 = ((f32[32,1,2]{2,1,0:T(1,128)}), f32[32,1,2]{2,1,0:T(1,128)S(1)}, u32[]{:S(2)}, u32[]{:S(2)}) async-start(f32[32,1,2]{2,1,0:T(1,128)} %broadcast_in_dim.46), calls=%async_computation.2 | async-start | bytes 32768 | tf_op jit(solution)/shard_map/all_to_all | solution.py:145
Sparse Core Ops, SparseCore 0:
  10.1 44.5 all-gather.2

commit v7 on v4

--- a/solution.py
+++ b/solution.py
@@ -1,6 +1,8 @@
 import jax
 import jax.numpy as jnp
 from jax import lax
+from jax.experimental import pallas as pl
+from jax.experimental.pallas import tpu as pltpu
 from jax.sharding import Mesh, PartitionSpec as P
 
 HEADS = 12
@@ -20,6 +22,54 @@
         if high != low and high < count:
             route += [(low, high), (high, low)]
     return lax.ppermute(block, axis, route)
+
+
+def attention_partials_kernel(q_ref, kv_ref, mask_ref, out_ref):
+    rows = q_ref.shape[0]
+    lanes = 2 * HD
+    lane = lax.broadcasted_iota(jnp.int32, (1, lanes), 1)
+    low = lane < HD
+    usable = mask_ref[...] > 0
+    factor = HD ** (-0.5)
+    maxes = []
+    sums = []
+    for pair in range(HEADS // 2):
+        cols = slice(pair * lanes, (pair + 1) * lanes)
+        q2 = q_ref[:, cols]
+        k2 = kv_ref[0, :, cols]
+        v2 = kv_ref[1, :, cols]
+        outs = []
+        for half in (low, jnp.logical_not(low)):
+            q_half = jnp.where(half, q2, jnp.zeros_like(q2))
+            logits = lax.dot_general(
+                q_half, k2, (((1,), (1,)), ((), ())), preferred_element_type=jnp.float32
+            ) * factor
+            part_max = jnp.max(jnp.where(usable, logits, -1e30), axis=1, keepdims=True)
+            weights = jnp.where(usable, jnp.exp(logits - part_max), 0.0)
+            sums.append(jnp.sum(weights, axis=1, keepdims=True))
+            maxes.append(part_max)
+            outs.append(
+                jnp.dot(weights.astype(jnp.bfloat16), v2, preferred_element_type=jnp.float32)
+            )
+        out_ref[:, cols] = jnp.where(low, outs[0], outs[1])
+    width = HEADS * HD
+    out_ref[:, width : width + HEADS] = jnp.concatenate(maxes, axis=1)
+    out_ref[:, width + HEADS : width + 2 * HEADS] = jnp.concatenate(sums, axis=1)
+
+def attention_partials(q, kv, mask):
+    rows = q.shape[0]
+    width = HEADS * HD
+    return pl.pallas_call(
+        attention_partials_kernel,
+        out_shape=jax.ShapeDtypeStruct((rows, width + 2 * HEADS), jnp.float32),
+        in_specs=[pl.BlockSpec(memory_space=pltpu.VMEM)] * 3,
+        out_specs=pl.BlockSpec(memory_space=pltpu.VMEM),
+        cost_estimate=pl.CostEstimate(
+            flops=8 * rows * kv.shape[1] * width,
+            transcendentals=2 * rows * kv.shape[1] * HEADS,
+            bytes_accessed=q.size * 2 + kv.size * 2 + rows * (width + 2 * HEADS) * 4,
+        ),
+    )(q, kv, mask)
 
 
 def modulate_rows(hidden, shift_row, scale_row):
@@ -66,22 +116,10 @@
     within = positions % rows_dev
     source = (positions // rows_dev) * n_x + x_index
     text_slot = source * txt_dev + within - img_dev
-    usable = ((within < img_dev) | (text_slot < length))[None, None, :]
-    queries = query_rows.reshape(q_rows, HEADS, HD)
-    keys_here = piece[0].reshape(piece_rows, HEADS, HD)
-    vals_here = piece[1].reshape(piece_rows, HEADS, HD)
-    logits = (
-        jnp.einsum("qhd,khd->qhk", queries, keys_here, preferred_element_type=jnp.float32) * factor
-    )
-    part_max = jnp.max(jnp.where(usable, logits, -1e30), axis=2)
-    weights = jnp.where(usable, jnp.exp(logits - part_max[:, :, None]), 0.0)
-    part_sum = jnp.sum(weights, axis=2)
-    weighted = jnp.einsum(
-        "qhk,khd->qhd", weights.astype(jnp.bfloat16), vals_here, preferred_element_type=jnp.float32
-    )
+    usable = ((within < img_dev) | (text_slot < length)).astype(jnp.float32)[None, :]
     width = HEADS * HD
-    packed = jnp.concatenate(
-        [weighted.reshape(q_rows, width), part_max, part_sum], axis=1
+    packed = attention_partials(
+        query_rows, piece.reshape(2, piece_rows, width), usable
     ).reshape(n_x, img_dev, width + 2 * HEADS)
     got = lax.all_to_all(packed, "sx", 0, 0, tiled=True)
     got_out = got[:, :, :width].reshape(n_x, img_dev, HEADS, HD)

time: 144 us -> 143 us (level)
  Pallas kernels: 0 us -> 5.38 us
  local copies, waits for them, and re-layouts: 8.04 us -> 4.03 us
  matrix products: 10.8 us -> 7.88 us
  blocking collectives: 48 us -> 49.9 us
    pallas_call x0 -> x1, Pallas kernels: none -> 5.38 us  [attention_partials(): pl.pallas_call(attention_partials_kernel, out_shape=jax.ShapeDtypeStruct(...]
    dot_general x2 -> x0, matrix products: 2.95 us -> none  [the longest x1 2.34 us: per_device(): jnp.einsum('qhk,khd->qhd', weights.astype(jnp.bfloat16), vals_here, prefe...]
    all_gather x1, blocking collectives: 33.4 us -> 35.1 us  [per_device(): piece = lax.all_gather(key_value[:, 0, 0], 'sz', axis=1, tiled=True)]
    transpose x1 -> x0, local copies, waits for them, and re-layouts: 1.48 us -> none  [per_device(): jnp.einsum('qhk,khd->qhd', weights.astype(jnp.bfloat16), vals_here, prefe...]
  transfers between devices with their start and end apart: 8 -> 8, of which waited for: 4 -> 4; matrix products, arithmetic and copies ran while one was open for 12% -> 6% of each run, Pallas kernels for 0% -> 4%
where the time goes in v7:
time: 143 us
  blocking collectives  49.9 us (35%)
  starting transfers between devices  28.9 us (20%)
  waiting for transfers between devices  24.3 us (17%)
  between operations  17.4 us (12%)
  matrix products  7.88 us (6%)
  Pallas kernels  5.38 us (4%)
  other arithmetic  4.86 us (3%)
  local copies, waits for them, and re-layouts  4.03 us (3%)
    all_gather x1, blocking collectives, per_device(): piece = lax.all_gather(key_value[:, 0, 0], 'sz', axis=1, tiled=True)  35.1 us
    all_gather x1, blocking collectives, per_device(): line_in = lax.all_gather(mlp_in, 'ry', axis=0, tiled=True)  14.8 us
    all_to_all x1, waiting for transfers between devices, per_device(): lax.all_to_all(jnp.broadcast_to(partials[None], (n_seq, 2)), ('sz', 'sx')...  8.88 us
    all_to_all x1, waiting for transfers between devices, per_device(): lax.all_to_all(mlp_parts, 'ry', 0, 0, tiled=True).astype(jnp.float32)  6.41 us
    all_to_all x1, starting transfers between devices, per_device(): lax.all_to_all(mlp_parts, 'ry', 0, 0, tiled=True).astype(jnp.float32)  5.72 us
    all_to_all x1, starting transfers between devices, per_device(): lax.all_to_all(jnp.broadcast_to(partials[None], (n_seq, 2)), ('sz', 'sx')...  5.66 us
    pallas_call x1, Pallas kernels, attention_partials(): pl.pallas_call(attention_partials_kernel, out_shape=jax.ShapeDtypeStruct(...  5.38 us
    ppermute x1, waiting for transfers between devices, swapped(): return lax.ppermute(block, axis, route)  5.06 us
  transfers between devices with their start and end apart: 8, of which 4 were waited for; matrix products, arithmetic and copies ran while one was open for 6% of the time, Pallas kernels for 4%

profile of v7, /device:TPU:56, one launch (start us, length us, event | category | flops | bytes accessed | tf_op | source)
XLA Modules:
  0.0 142.7 jit_solution(7039696180261202236)
XLA Ops:
  7.2 0.0 copy-start
  7.2 0.0 all-gather.3.cloned.1.call-start
  7.2 0.7 all-gather.3.cloned.1.call-update
  7.9 1.5 %broadcast_in_dim.7 = bf16[4,32,768]{2,1,0:T(8,128)(2,1)} broadcast(bf16[32,768]{1,0:T(8,128)(2,1)} %bitcast.32), dimensions={1,2} | broadcast | bytes 245760 | tf_op jit(solution)/shard_map/broadcast_in_dim | solution.py:110
  9.4 4.3 %all-to-all-start = ((bf16[4,32,768]{2,1,0:T(8,128)(2,1)}), bf16[4,32,768]{2,1,0:T(8,128)(2,1)S(1)}, u32[]{:S(2)}, u32[]{:S(2)}) async-start(bf16[4,32,768]{2,1,0:T(8,128)(2,1)} %broadcast_in_dim.7), calls=%async_computation | async-start | bytes 393216 | tf_op jit(solution)/shard_map/all_to_all | solution.py:109
  13.7 35.1 %all-gather = bf16[2,1,1,320,768]{4,3,0,2,1:T(8,128)(2,1)} all-gather(bf16[2,1,1,40,768]{4,3,0,2,1:T(8,128)(2,1)} %bitcast.31), channel_id=2, replica_groups=mesh['cfg'=2,'ry'=4,'rc'=2,'sz'=8,'sx'=4] {'sz'}, dimensions={3}, use_global_device_ids=true | all-gather | bytes 1105920 | tf_op jit(solution)/shard_map/all_gather | solution.py:112
  49.5 0.6 or_convert_fusion.mask_ref
  50.1 0.0 all-to-all-done
  50.1 0.0 copy-start.2
  50.1 0.7 copy-done.2
  50.7 0.0 copy-start.1
  50.7 0.0 copy-start.7
  50.7 0.0 copy-start.8
  50.7 0.0 copy-start.5
  50.8 5.4 %shard_map.175 = f32[128,792]{1,0:T(8,128)} custom-call(bf16[128,768]{1,0:T(8,128)(2,1)} %bitcast.30, bf16[2,320,768]{2,1,0:T(8,128)(2,1)} %bitcast.28, f32[1,320]{1,0:T(1,128)} %or_convert_fusion.mask_ref), custom_call_target="tpu_custom_call" | custom-call | flops 251658240 | bytes 1585152 | tf_op jit(solution)/shard_map/pallas_call | solution.py:62
  56.1 5.0 %all-to-all-start.1 = ((f32[4,32,792]{2,1,0:T(8,128)}), f32[4,32,792]{2,1,0:T(8,128)S(1)}, u32[]{:S(2)}, u32[]{:S(2)}) async-start(f32[4,32,792]{2,1,0:T(8,128)} %bitcast.29), calls=%async_computation.1 | async-start | bytes 917504 | tf_op jit(solution)/shard_map/all_to_all | solution.py:124
  61.2 0.0 copy-done.1
  61.2 1.9 %collective-permute-start = (bf16[1536,384]{1,0:T(8,128)(2,1)S(1)}, bf16[1536,384]{1,0:T(8,128)(2,1)}, u32[]{:S(2)}, u32[]{:S(2)}) collective-permute-start(bf16[1536,384]{1,0:T(8,128)(2,1)S(1)} %copy-done.1), channel_id=1, source_target_pairs={{0,32},{32,0},{1,33},{33,1},{2,34},{34,2},{3,35},{35,3},{4,36},{36... | collective-permute-start | bytes 3538952 | tf_op jit(solution)/shard_map/ppermute | solution.py:142
  63.1 2.4 %collective-permute-start.1 = (bf16[384,1536]{1,0:T(8,128)(2,1)}, bf16[384,1536]{1,0:T(8,128)(2,1)}, u32[]{:S(2)}, u32[]{:S(2)}) collective-permute-start(bf16[384,1536]{1,0:T(8,128)(2,1)} %param.28), channel_id=1, source_target_pairs={{0,32},{32,0},{1,33},{33,1},{2,34},{34,2},{3,35},{35,3},{4,36},{36... | collective-permute-start | bytes 3538952 | tf_op jit(solution)/shard_map/ppermute | solution.py:143
  65.5 0.0 copy-done.7
  65.5 0.0 copy-done.8
  65.6 0.0 copy-done.5
  65.6 3.3 %all-to-all-done.1 = f32[4,32,792]{2,1,0:T(8,128)S(1)} async-done(((f32[4,32,792]{2,1,0:T(8,128)}), f32[4,32,792]{2,1,0:T(8,128)S(1)}, u32[]{:S(2)}, u32[]{:S(2)}) %all-to-all-start.1) | async-done | bytes 405536 | tf_op jit(solution)/shard_map/all_to_all | solution.py:124
  68.9 0.1 fusion.35
  69.0 0.3 mul.150
  69.3 0.0 copy-start.3
  69.3 0.3 mul.151
  69.6 0.1 div.40
  69.8 0.1 div.41
  69.9 0.0 all-gather.3.cloned.1.call-done
  70.0 0.3 copy-done.3
  70.2 2.6 %fusion.49 = (f32[32]{0:T(128)S(1)}, f32[32,1536]{1,0:T(8,128)S(1)}) fusion(bf16[768,1536]{0,1:T(8,128)(2,1)} %all-gather.3.cloned.1.call-done, f32[32,768]{1,0:T(8,128)S(1)} %fusion.2, f32[32,768]{1,0:T(8,128)S(1)} %div.41, f32[1536]{0:T(1024)S(1)} %reduce.3, bf16[1,1,32,1536]{3,2,1,0:T(8,128)(2,1)S(1)} %copy-done.3), kind=kOutput, calls=%fused_computation.81 | convolution fusion | flops 75743200 | bytes 2857088 | tf_op jit(solution)/shard_map/dot_general | solution.py:133
  72.8 0.2 multiply_reduce_fusion.1
  73.0 0.1 add_convert_fusion.1
  73.1 14.8 %all_gather.11 = bf16[128,1536]{1,0:T(8,128)(2,1)S(1)} all-gather(bf16[32,1536]{1,0:T(8,128)(2,1)S(1)} %add_convert_fusion.1), channel_id=1, replica_groups=mesh['cfg'=2,'ry'=4,'rc'=2,'sz'=8,'sx'=4] {'ry'}, dimensions={0}, use_global_device_ids=true | all-gather | bytes 491520 | tf_op jit(solution)/shard_map/all_gather | solution.py:144
  87.9 2.0 %fusion.21 = f32[128,1536]{1,0:T(8,128)S(1)} fusion(bf16[384,1536]{1,0:T(8,128)(2,1)} %param.28, bf16[128,1536]{1,0:T(8,128)(2,1)S(1)} %all_gather.11, bf16[1536,384]{1,0:T(8,128)(2,1)S(1)} %copy-done.1), kind=kOutput, calls=%fused_computation.31 | convolution fusion | flops 302432256 | bytes 3538944 | tf_op jit(solution)/shard_map/dot_general | solution.py:153
  89.9 0.0 copy-start.9
  89.9 0.0 copy-start.10
  90.0 0.0 copy-start.6
  90.0 0.0 collective-permute-done
  90.0 0.0 collective-permute-done.1
  90.0 3.1 %fusion = bf16[128,1536]{1,0:T(8,128)(2,1)} fusion(f32[128,1536]{1,0:T(8,128)S(1)} %fusion.21, bf16[384,1536]{1,0:T(8,128)(2,1)} %collective-permute-done.1, bf16[128,1536]{1,0:T(8,128)(2,1)S(1)} %all_gather.11, bf16[1536,384]{1,0:T(8,128)(2,1)} %collective-permute-done), kind=kOutput, calls=%fused_computation.1 | convolution fusion | flops 302825472 | bytes 3932160 | tf_op jit(solution)/shard_map/dot_general | solution.py:154
  93.1 5.7 %all-to-all-start.2 = ((bf16[4,32,1536]{2,1,0:T(8,128)(2,1)}), bf16[4,32,1536]{2,1,0:T(8,128)(2,1)S(1)}, u32[]{:S(2)}, u32[]{:S(2)}) async-start(bf16[4,32,1536]{2,1,0:T(8,128)(2,1)} %bitcast.8), calls=%async_computation.2 | async-start | bytes 786432 | tf_op jit(solution)/shard_map/all_to_all | solution.py:160
  98.8 0.0 copy-done.9
  98.8 0.0 copy-start.4
  98.8 0.0 copy-done.10
  98.9 0.0 copy-done.6
  98.9 6.4 %all-to-all-done.2 = bf16[4,32,1536]{2,1,0:T(8,128)(2,1)S(1)} async-done(((bf16[4,32,1536]{2,1,0:T(8,128)(2,1)}), bf16[4,32,1536]{2,1,0:T(8,128)(2,1)S(1)}, u32[]{:S(2)}, u32[]{:S(2)}) %all-to-all-start.2) | async-done | bytes 393248 | tf_op jit(solution)/shard_map/all_to_all | solution.py:160
  105.3 0.1 convert_reduce_fusion
  105.4 0.1 fusion.48
  105.5 0.2 multiply_reduce_fusion
  105.7 0.0 copy-done
  105.7 0.2 fusion.19
  106.0 3.8 %collective-permute-start.2 = (f32[32,64]{1,0:T(8,128)S(1)}, f32[32,64]{1,0:T(8,128)S(1)}, u32[]{:S(2)}, u32[]{:S(2)}) collective-permute-start(f32[32,64]{1,0:T(8,128)S(1)} %fusion.19), channel_id=1, source_target_pairs={{0,256},{256,0},{1,257},{257,1},{2,258},{258,2},{3,259},{259,3},{4... | collective-permute-start | bytes 24584 | tf_op jit(solution)/shard_map/ppermute | solution.py:24
  110.5 5.1 %collective-permute-done.2 = f32[32,64]{1,0:T(8,128)S(1)} collective-permute-done((f32[32,64]{1,0:T(8,128)S(1)}, f32[32,64]{1,0:T(8,128)S(1)}, u32[]{:S(2)}, u32[]{:S(2)}) %collective-permute-start.2) | collective-permute-done | bytes 8224 | tf_op jit(solution)/shard_map/ppermute | solution.py:24
  115.5 0.6 multiply_reduce_fusion.2
  116.1 1.4 pad_maximum_fusion
  117.5 0.6 broadcast_in_dim.8
  118.1 5.7 %all-to-all-start.3 = ((f32[32,1,2]{2,1,0:T(1,128)}), f32[32,1,2]{2,1,0:T(1,128)S(1)}, u32[]{:S(2)}, u32[]{:S(2)}) async-start(f32[32,1,2]{2,1,0:T(1,128)} %broadcast_in_dim.8), calls=%async_computation.3 | async-start | bytes 32768 | tf_op jit(solution)/shard_map/all_to_all | solution.py:174
  123.8 0.0 copy-done.4
  123.8 0.7 bitcast_add_fusion
  124.5 8.9 %all-to-all-done.3 = f32[32,1,2]{2,1,0:T(1,128)S(1)} async-done(((f32[32,1,2]{2,1,0:T(1,128)}), f32[32,1,2]{2,1,0:T(1,128)S(1)}, u32[]{:S(2)}, u32[]{:S(2)}) %all-to-all-start.3) | async-done | bytes 288 | tf_op jit(solution)/shard_map/all_to_all | solution.py:174
  133.3 0.1 copy.22
  133.4 0.6 slice_reduce_fusion.1
  (12 shorter events, 0.2 us)
Async XLA Ops:
  7.2 98.6 %copy-start = (bf16[1536,64]{0,1:T(8,128)(2,1)S(1)}, bf16[1536,64]{0,1:T(8,128)(2,1)}, u32[]{:S(2)}) copy-start(bf16[1536,64]{0,1:T(8,128)(2,1)} %param.29) | copy-start | bytes 589828
  7.2 62.8 %all-gather.3.cloned.1.call-start = ((), (), s32[]{:S(2)}) async-start(), calls=%async_computation.4 | async-start | bytes 2654208 | tf_op jit(solution)/shard_map/all_gather | solution.py:135
  9.4 40.7 %all-to-all-start = ((bf16[4,32,768]{2,1,0:T(8,128)(2,1)}), bf16[4,32,768]{2,1,0:T(8,128)(2,1)S(1)}, u32[]{:S(2)}, u32[]{:S(2)}) async-start(bf16[4,32,768]{2,1,0:T(8,128)(2,1)} %broadcast_in_dim.7), calls=%async_computation | async-start | bytes 393216 | tf_op jit(solution)/shard_map/all_to_all | solution.py:109
  50.1 0.7 copy-start.2
  50.7 10.4 %copy-start.1 = (bf16[1536,384]{1,0:T(8,128)(2,1)S(1)}, bf16[1536,384]{1,0:T(8,128)(2,1)}, u32[]{:S(2)}) copy-start(bf16[1536,384]{1,0:T(8,128)(2,1)} %param.27) | copy-start | bytes 3538948
  50.7 14.8 %copy-start.7 = (f32[1,1,1536]{2,1,0:T(1,128)S(1)}, f32[1,1,1536]{2,1,0:T(1,128)}, u32[]{:S(2)}) copy-start(f32[1,1,1536]{2,1,0:T(1,128)} %param.20) | copy-start | bytes 18436
  50.7 14.8 %copy-start.8 = (f32[1,1,1536]{2,1,0:T(1,128)S(1)}, f32[1,1,1536]{2,1,0:T(1,128)}, u32[]{:S(2)}) copy-start(f32[1,1,1536]{2,1,0:T(1,128)} %param.21) | copy-start | bytes 18436
  50.7 14.8 %copy-start.5 = (f32[1,1,1536]{2,1,0:T(1,128)S(1)}, f32[1,1,1536]{2,1,0:T(1,128)}, u32[]{:S(2)}) copy-start(f32[1,1,1536]{2,1,0:T(1,128)} %param.22) | copy-start | bytes 18436
  56.1 12.8 %all-to-all-start.1 = ((f32[4,32,792]{2,1,0:T(8,128)}), f32[4,32,792]{2,1,0:T(8,128)S(1)}, u32[]{:S(2)}, u32[]{:S(2)}) async-start(f32[4,32,792]{2,1,0:T(8,128)} %bitcast.29), calls=%async_computation.1 | async-start | bytes 917504 | tf_op jit(solution)/shard_map/all_to_all | solution.py:124
  61.2 28.8 %collective-permute-start = (bf16[1536,384]{1,0:T(8,128)(2,1)S(1)}, bf16[1536,384]{1,0:T(8,128)(2,1)}, u32[]{:S(2)}, u32[]{:S(2)}) collective-permute-start(bf16[1536,384]{1,0:T(8,128)(2,1)S(1)} %copy-done.1), channel_id=1, source_target_pairs={{0,32},{32,0},{1,33},{33,1},{2,34},{34,2},{3,35},{35,3},{4,36},{36... | collective-permute-start | bytes 3538952 | tf_op jit(solution)/shard_map/ppermute | solution.py:142
  63.1 26.9 %collective-permute-start.1 = (bf16[384,1536]{1,0:T(8,128)(2,1)}, bf16[384,1536]{1,0:T(8,128)(2,1)}, u32[]{:S(2)}, u32[]{:S(2)}) collective-permute-start(bf16[384,1536]{1,0:T(8,128)(2,1)} %param.28), channel_id=1, source_target_pairs={{0,32},{32,0},{1,33},{33,1},{2,34},{34,2},{3,35},{35,3},{4,36},{36... | collective-permute-start | bytes 3538952 | tf_op jit(solution)/shard_map/ppermute | solution.py:143
  69.3 0.9 copy-start.3
  89.9 8.9 %copy-start.9 = (f32[1,1,1536]{2,1,0:T(1,128)S(1)}, f32[1,1,1536]{2,1,0:T(1,128)}, u32[]{:S(2)}) copy-start(f32[1,1,1536]{2,1,0:T(1,128)} %param.23) | copy-start | bytes 18436
  89.9 8.9 %copy-start.10 = (f32[1,1,1536]{2,1,0:T(1,128)S(1)}, f32[1,1,1536]{2,1,0:T(1,128)}, u32[]{:S(2)}) copy-start(f32[1,1,1536]{2,1,0:T(1,128)} %param.24) | copy-start | bytes 18436
  90.0 8.9 %copy-start.6 = (f32[1,1,1536]{2,1,0:T(1,128)S(1)}, f32[1,1,1536]{2,1,0:T(1,128)}, u32[]{:S(2)}) copy-start(f32[1,1,1536]{2,1,0:T(1,128)} %param.25) | copy-start | bytes 18436
  93.1 12.2 %all-to-all-start.2 = ((bf16[4,32,1536]{2,1,0:T(8,128)(2,1)}), bf16[4,32,1536]{2,1,0:T(8,128)(2,1)S(1)}, u32[]{:S(2)}, u32[]{:S(2)}) async-start(bf16[4,32,1536]{2,1,0:T(8,128)(2,1)} %bitcast.8), calls=%async_computation.2 | async-start | bytes 786432 | tf_op jit(solution)/shard_map/all_to_all | solution.py:160
  98.8 25.0 %copy-start.4 = (f32[1,32,32]{2,1,0:T(8,128)S(1)}, f32[1,32,32]{2,1,0:T(8,128)}, u32[]{:S(2)}) copy-start(f32[1,32,32]{2,1,0:T(8,128)} %param.30) | copy-start | bytes 12292
  106.0 9.5 %collective-permute-start.2 = (f32[32,64]{1,0:T(8,128)S(1)}, f32[32,64]{1,0:T(8,128)S(1)}, u32[]{:S(2)}, u32[]{:S(2)}) collective-permute-start(f32[32,64]{1,0:T(8,128)S(1)} %fusion.19), channel_id=1, source_target_pairs={{0,256},{256,0},{1,257},{257,1},{2,258},{258,2},{3,259},{259,3},{4... | collective-permute-start | bytes 24584 | tf_op jit(solution)/shard_map/ppermute | solution.py:24
  118.1 15.3 %all-to-all-start.3 = ((f32[32,1,2]{2,1,0:T(1,128)}), f32[32,1,2]{2,1,0:T(1,128)S(1)}, u32[]{:S(2)}, u32[]{:S(2)}) async-start(f32[32,1,2]{2,1,0:T(1,128)} %broadcast_in_dim.8), calls=%async_computation.3 | async-start | bytes 32768 | tf_op jit(solution)/shard_map/all_to_all | solution.py:174
Sparse Core Ops, SparseCore 0:
  10.1 44.5 all-gather.2

commit v8 on v7

--- a/solution.py
+++ b/solution.py
@@ -164,10 +164,12 @@
     velocity = jnp.dot(modulated, w_out, preferred_element_type=jnp.float32)
     half_width = velocity.shape[1] // lax.axis_size("cfg")
     side_index = lax.axis_index("cfg")
-    received = swapped(velocity, "cfg", 0)
-    is_cond = side_index == 0
-    cond_part = jnp.where(is_cond, velocity, received)
-    uncond = jnp.where(is_cond, received, velocity)
+    n_cfg = lax.axis_size("cfg")
+    halves = lax.all_to_all(
+        jnp.broadcast_to(velocity[None], (n_cfg,) + velocity.shape), "cfg", 0, 0, tiled=True
+    )
+    cond_part = halves[0]
+    uncond = halves[1]
     guided_full = uncond + guidance_weight * (cond_part - uncond)
     partials = jnp.stack([jnp.sum(guided_full * guided_full), jnp.max(jnp.abs(guided_full))])
     n_seq = lax.axis_size(("sz", "sx"))

time: 143 us -> 150 us (1.049)
  the two profiles are of different devices: /device:TPU:56 before, /device:TPU:2 now
where the time goes in v8:
time: 150 us; the launch traced here: 149 us
  blocking collectives  45.7 us (30%)
  starting transfers between devices  35.2 us (23%)
  waiting for transfers between devices  26.2 us (17%)
  between operations  17.4 us (12%)
  matrix products  7.88 us (5%)
  other arithmetic  5.56 us (4%)
  Pallas kernels  5.37 us (4%)
  local copies, waits for them, and re-layouts  5.34 us (4%)
    all_gather x1, blocking collectives, per_device(): piece = lax.all_gather(key_value[:, 0, 0], 'sz', axis=1, tiled=True)  30.8 us
    all_gather x1, blocking collectives, per_device(): line_in = lax.all_gather(mlp_in, 'ry', axis=0, tiled=True)  14.9 us
    all_to_all x1, starting transfers between devices, per_device(): lax.all_to_all(jnp.broadcast_to(query[0, 0][None], (n_x,) + query.shape[2...  9.24 us
    all_to_all x1, waiting for transfers between devices, per_device(): lax.all_to_all(mlp_parts, 'ry', 0, 0, tiled=True).astype(jnp.float32)  8.77 us
    all_to_all x1, waiting for transfers between devices, per_device(): lax.all_to_all(jnp.broadcast_to(partials[None], (n_seq, 2)), ('sz', 'sx')...  7.82 us
    all_to_all x1, waiting for transfers between devices, per_device(): lax.all_to_all(jnp.broadcast_to(velocity[None], (n_cfg,) + velocity.shape...  7.12 us
    all_to_all x1, starting transfers between devices, per_device(): lax.all_to_all(jnp.broadcast_to(partials[None], (n_seq, 2)), ('sz', 'sx')...  6.68 us
    all_to_all x1, starting transfers between devices, per_device(): lax.all_to_all(jnp.broadcast_to(velocity[None], (n_cfg,) + velocity.shape...  5.56 us
  transfers between devices with their start and end apart: 8, of which 4 were waited for; matrix products, arithmetic and copies ran while one was open for 6% of the time, Pallas kernels for 4%

profile of v8, /device:TPU:2, one launch (start us, length us, event | category | flops | bytes accessed | tf_op | source)
XLA Modules:
  0.0 148.7 jit_solution(15893034965711086417)
XLA Ops:
  7.2 0.0 copy-start
  7.2 0.0 all-gather.3.cloned.1.call-start
  7.2 0.7 all-gather.3.cloned.1.call-update
  7.9 1.5 broadcast_in_dim.9
  9.4 9.2 %all-to-all-start = ((bf16[4,32,768]{2,1,0:T(8,128)(2,1)}), bf16[4,32,768]{2,1,0:T(8,128)(2,1)S(1)}, u32[]{:S(2)}, u32[]{:S(2)}) async-start(bf16[4,32,768]{2,1,0:T(8,128)(2,1)} %broadcast_in_dim.9), calls=%async_computation | async-start | bytes 393216 | tf_op jit(solution)/shard_map/all_to_all | solution.py:109
  18.6 30.8 %all-gather = bf16[2,1,1,320,768]{4,3,0,2,1:T(8,128)(2,1)} all-gather(bf16[2,1,1,40,768]{4,3,0,2,1:T(8,128)(2,1)} %bitcast.45), channel_id=2, replica_groups=mesh['cfg'=2,'ry'=4,'rc'=2,'sz'=8,'sx'=4] {'sz'}, dimensions={3}, use_global_device_ids=true | all-gather | bytes 1105920 | tf_op jit(solution)/shard_map/all_gather | solution.py:112
  50.1 0.6 or_convert_fusion.mask_ref
  50.7 0.0 all-to-all-done
  50.7 0.7 copy-done.2
  51.3 0.0 copy-start.1
  51.3 0.0 copy-start.7
  51.3 5.4 %shard_map.175 = f32[128,792]{1,0:T(8,128)} custom-call(bf16[128,768]{1,0:T(8,128)(2,1)} %bitcast.44, bf16[2,320,768]{2,1,0:T(8,128)(2,1)} %bitcast.42, f32[1,320]{1,0:T(1,128)} %or_convert_fusion.mask_ref), custom_call_target="tpu_custom_call" | custom-call | flops 251658240 | bytes 1585152 | tf_op jit(solution)/shard_map/pallas_call | solution.py:62
  56.7 4.8 %all-to-all-start.1 = ((f32[4,32,792]{2,1,0:T(8,128)}), f32[4,32,792]{2,1,0:T(8,128)S(1)}, u32[]{:S(2)}, u32[]{:S(2)}) async-start(f32[4,32,792]{2,1,0:T(8,128)} %bitcast.43), calls=%async_computation.1 | async-start | bytes 917504 | tf_op jit(solution)/shard_map/all_to_all | solution.py:124
  61.5 0.0 copy-done.1
  61.5 1.9 %collective-permute-start = (bf16[1536,384]{1,0:T(8,128)(2,1)S(1)}, bf16[1536,384]{1,0:T(8,128)(2,1)}, u32[]{:S(2)}, u32[]{:S(2)}) collective-permute-start(bf16[1536,384]{1,0:T(8,128)(2,1)S(1)} %copy-done.1), channel_id=1, source_target_pairs={{0,32},{32,0},{1,33},{33,1},{2,34},{34,2},{3,35},{35,3},{4,36},{36... | collective-permute-start | bytes 3538952 | tf_op jit(solution)/shard_map/ppermute | solution.py:142
  63.4 2.4 %collective-permute-start.1 = (bf16[384,1536]{1,0:T(8,128)(2,1)}, bf16[384,1536]{1,0:T(8,128)(2,1)}, u32[]{:S(2)}, u32[]{:S(2)}) collective-permute-start(bf16[384,1536]{1,0:T(8,128)(2,1)} %param.28), channel_id=1, source_target_pairs={{0,32},{32,0},{1,33},{33,1},{2,34},{34,2},{3,35},{35,3},{4,36},{36... | collective-permute-start | bytes 3538952 | tf_op jit(solution)/shard_map/ppermute | solution.py:143
  65.9 0.0 copy-done.7
  65.9 0.0 copy-done.8
  65.9 0.0 copy-done.5
  66.0 1.8 %all-to-all-done.1 = f32[4,32,792]{2,1,0:T(8,128)S(1)} async-done(((f32[4,32,792]{2,1,0:T(8,128)}), f32[4,32,792]{2,1,0:T(8,128)S(1)}, u32[]{:S(2)}, u32[]{:S(2)}) %all-to-all-start.1) | async-done | bytes 405536 | tf_op jit(solution)/shard_map/all_to_all | solution.py:124
  67.8 0.1 fusion.35
  67.9 0.3 mul.150
  68.2 0.0 copy-start.3
  68.2 0.3 mul.151
  68.5 0.1 div.40
  68.7 0.1 div.41
  68.8 0.0 all-gather.3.cloned.1.call-done
  68.9 0.3 copy-done.3
  69.1 2.6 %fusion.53 = (f32[32]{0:T(128)S(1)}, f32[32,1536]{1,0:T(8,128)S(1)}) fusion(bf16[768,1536]{0,1:T(8,128)(2,1)} %all-gather.3.cloned.1.call-done, f32[32,768]{1,0:T(8,128)S(1)} %fusion.2, f32[32,768]{1,0:T(8,128)S(1)} %div.41, f32[1536]{0:T(1024)S(1)} %reduce.3, bf16[1,1,32,1536]{3,2,1,0:T(8,128)(2,1)S(1)} %copy-done.3), kind=kOutput, calls=%fused_computation.85 | convolution fusion | flops 75743200 | bytes 2857088 | tf_op jit(solution)/shard_map/dot_general | solution.py:133
  71.7 0.2 multiply_reduce_fusion.1
  71.9 0.1 add_convert_fusion.1
  72.0 14.9 %all_gather.11 = bf16[128,1536]{1,0:T(8,128)(2,1)S(1)} all-gather(bf16[32,1536]{1,0:T(8,128)(2,1)S(1)} %add_convert_fusion.1), channel_id=1, replica_groups=mesh['cfg'=2,'ry'=4,'rc'=2,'sz'=8,'sx'=4] {'ry'}, dimensions={0}, use_global_device_ids=true | all-gather | bytes 491520 | tf_op jit(solution)/shard_map/all_gather | solution.py:144
  87.0 2.0 %fusion.21 = f32[128,1536]{1,0:T(8,128)S(1)} fusion(bf16[384,1536]{1,0:T(8,128)(2,1)} %param.28, bf16[128,1536]{1,0:T(8,128)(2,1)S(1)} %all_gather.11, bf16[1536,384]{1,0:T(8,128)(2,1)S(1)} %copy-done.1), kind=kOutput, calls=%fused_computation.31 | convolution fusion | flops 302432256 | bytes 3538944 | tf_op jit(solution)/shard_map/dot_general | solution.py:153
  89.0 0.0 copy-start.9
  89.0 0.0 copy-start.10
  89.0 0.0 copy-start.6
  89.0 0.0 collective-permute-done
  89.0 0.0 collective-permute-done.1
  89.0 3.1 %fusion = bf16[128,1536]{1,0:T(8,128)(2,1)} fusion(f32[128,1536]{1,0:T(8,128)S(1)} %fusion.21, bf16[384,1536]{1,0:T(8,128)(2,1)} %collective-permute-done.1, bf16[128,1536]{1,0:T(8,128)(2,1)S(1)} %all_gather.11, bf16[1536,384]{1,0:T(8,128)(2,1)} %collective-permute-done), kind=kOutput, calls=%fused_computation.1 | convolution fusion | flops 302825472 | bytes 3932160 | tf_op jit(solution)/shard_map/dot_general | solution.py:154
  92.1 4.6 %all-to-all-start.2 = ((bf16[4,32,1536]{2,1,0:T(8,128)(2,1)}), bf16[4,32,1536]{2,1,0:T(8,128)(2,1)S(1)}, u32[]{:S(2)}, u32[]{:S(2)}) async-start(bf16[4,32,1536]{2,1,0:T(8,128)(2,1)} %bitcast.8), calls=%async_computation.2 | async-start | bytes 786432 | tf_op jit(solution)/shard_map/all_to_all | solution.py:160
  96.7 0.0 copy-done.9
  96.7 0.0 copy-done.10
  96.8 0.0 copy-done.6
  96.8 8.8 %all-to-all-done.2 = bf16[4,32,1536]{2,1,0:T(8,128)(2,1)S(1)} async-done(((bf16[4,32,1536]{2,1,0:T(8,128)(2,1)}), bf16[4,32,1536]{2,1,0:T(8,128)(2,1)S(1)}, u32[]{:S(2)}, u32[]{:S(2)}) %all-to-all-start.2) | async-done | bytes 393248 | tf_op jit(solution)/shard_map/all_to_all | solution.py:160
  105.6 0.1 convert_reduce_fusion
  105.6 0.1 fusion.52
  105.8 0.2 multiply_reduce_fusion
  106.0 0.0 copy-done
  106.0 0.2 fusion.19
  106.2 0.7 reshape.174
  106.9 5.6 %all-to-all-start.3 = ((f32[2,1,2048]{2,1,0:T(1,128)}), f32[2,1,2048]{2,1,0:T(1,128)S(1)}, u32[]{:S(2)}, u32[]{:S(2)}) async-start(f32[2,1,2048]{2,1,0:T(1,128)} %reshape.174), calls=%async_computation.3 | async-start | bytes 32768 | tf_op jit(solution)/shard_map/all_to_all | solution.py:168
  113.2 7.1 %all-to-all-done.3 = f32[2,1,2048]{2,1,0:T(1,128)S(1)} async-done(((f32[2,1,2048]{2,1,0:T(1,128)}), f32[2,1,2048]{2,1,0:T(1,128)S(1)}, u32[]{:S(2)}, u32[]{:S(2)}) %all-to-all-start.3) | async-done | bytes 16416 | tf_op jit(solution)/shard_map/all_to_all | solution.py:168
  120.3 0.5 broadcast.237
  120.8 0.7 reduce.11
  121.5 0.1 reshape.175
  121.6 0.6 multiply_reduce_fusion.2
  122.2 1.4 pad_maximum_fusion
  123.5 0.6 broadcast_in_dim.11
  124.2 6.7 %all-to-all-start.4 = ((f32[32,1,2]{2,1,0:T(1,128)}), f32[32,1,2]{2,1,0:T(1,128)S(1)}, u32[]{:S(2)}, u32[]{:S(2)}) async-start(f32[32,1,2]{2,1,0:T(1,128)} %broadcast_in_dim.11), calls=%async_computation.4 | async-start | bytes 32768 | tf_op jit(solution)/shard_map/all_to_all | solution.py:176
  130.8 0.0 copy-done.4
  130.9 0.7 bitcast_add_fusion
  131.5 7.8 %all-to-all-done.4 = f32[32,1,2]{2,1,0:T(1,128)S(1)} async-done(((f32[32,1,2]{2,1,0:T(1,128)}), f32[32,1,2]{2,1,0:T(1,128)S(1)}, u32[]{:S(2)}, u32[]{:S(2)}) %all-to-all-start.4) | async-done | bytes 288 | tf_op jit(solution)/shard_map/all_to_all | solution.py:176
  139.4 0.1 copy.22
  139.4 0.6 slice_reduce_fusion.1
  (17 shorter events, 0.2 us)
Async XLA Ops:
  7.2 98.8 %copy-start = (bf16[1536,64]{0,1:T(8,128)(2,1)S(1)}, bf16[1536,64]{0,1:T(8,128)(2,1)}, u32[]{:S(2)}) copy-start(bf16[1536,64]{0,1:T(8,128)(2,1)} %param.29) | copy-start | bytes 589828
  7.2 61.7 %all-gather.3.cloned.1.call-start = ((), (), s32[]{:S(2)}) async-start(), calls=%async_computation.5 | async-start | bytes 2654208 | tf_op jit(solution)/shard_map/all_gather | solution.py:135
  9.4 41.3 %all-to-all-start = ((bf16[4,32,768]{2,1,0:T(8,128)(2,1)}), bf16[4,32,768]{2,1,0:T(8,128)(2,1)S(1)}, u32[]{:S(2)}, u32[]{:S(2)}) async-start(bf16[4,32,768]{2,1,0:T(8,128)(2,1)} %broadcast_in_dim.9), calls=%async_computation | async-start | bytes 393216 | tf_op jit(solution)/shard_map/all_to_all | solution.py:109
  50.7 0.7 copy-start.2
  51.3 10.2 %copy-start.1 = (bf16[1536,384]{1,0:T(8,128)(2,1)S(1)}, bf16[1536,384]{1,0:T(8,128)(2,1)}, u32[]{:S(2)}) copy-start(bf16[1536,384]{1,0:T(8,128)(2,1)} %param.27) | copy-start | bytes 3538948
  51.3 14.5 %copy-start.7 = (f32[1,1,1536]{2,1,0:T(1,128)S(1)}, f32[1,1,1536]{2,1,0:T(1,128)}, u32[]{:S(2)}) copy-start(f32[1,1,1536]{2,1,0:T(1,128)} %param.20) | copy-start | bytes 18436
  51.3 14.6 %copy-start.8 = (f32[1,1,1536]{2,1,0:T(1,128)S(1)}, f32[1,1,1536]{2,1,0:T(1,128)}, u32[]{:S(2)}) copy-start(f32[1,1,1536]{2,1,0:T(1,128)} %param.21) | copy-start | bytes 18436
  51.3 14.6 %copy-start.5 = (f32[1,1,1536]{2,1,0:T(1,128)S(1)}, f32[1,1,1536]{2,1,0:T(1,128)}, u32[]{:S(2)}) copy-start(f32[1,1,1536]{2,1,0:T(1,128)} %param.22) | copy-start | bytes 18436
  56.7 11.1 %all-to-all-start.1 = ((f32[4,32,792]{2,1,0:T(8,128)}), f32[4,32,792]{2,1,0:T(8,128)S(1)}, u32[]{:S(2)}, u32[]{:S(2)}) async-start(f32[4,32,792]{2,1,0:T(8,128)} %bitcast.43), calls=%async_computation.1 | async-start | bytes 917504 | tf_op jit(solution)/shard_map/all_to_all | solution.py:124
  61.5 27.5 %collective-permute-start = (bf16[1536,384]{1,0:T(8,128)(2,1)S(1)}, bf16[1536,384]{1,0:T(8,128)(2,1)}, u32[]{:S(2)}, u32[]{:S(2)}) collective-permute-start(bf16[1536,384]{1,0:T(8,128)(2,1)S(1)} %copy-done.1), channel_id=1, source_target_pairs={{0,32},{32,0},{1,33},{33,1},{2,34},{34,2},{3,35},{35,3},{4,36},{36... | collective-permute-start | bytes 3538952 | tf_op jit(solution)/shard_map/ppermute | solution.py:142
  63.4 25.6 %collective-permute-start.1 = (bf16[384,1536]{1,0:T(8,128)(2,1)}, bf16[384,1536]{1,0:T(8,128)(2,1)}, u32[]{:S(2)}, u32[]{:S(2)}) collective-permute-start(bf16[384,1536]{1,0:T(8,128)(2,1)} %param.28), channel_id=1, source_target_pairs={{0,32},{32,0},{1,33},{33,1},{2,34},{34,2},{3,35},{35,3},{4,36},{36... | collective-permute-start | bytes 3538952 | tf_op jit(solution)/shard_map/ppermute | solution.py:143
  68.2 0.9 copy-start.3
  89.0 7.7 %copy-start.9 = (f32[1,1,1536]{2,1,0:T(1,128)S(1)}, f32[1,1,1536]{2,1,0:T(1,128)}, u32[]{:S(2)}) copy-start(f32[1,1,1536]{2,1,0:T(1,128)} %param.23) | copy-start | bytes 18436
  89.0 7.8 %copy-start.10 = (f32[1,1,1536]{2,1,0:T(1,128)S(1)}, f32[1,1,1536]{2,1,0:T(1,128)}, u32[]{:S(2)}) copy-start(f32[1,1,1536]{2,1,0:T(1,128)} %param.24) | copy-start | bytes 18436
  89.0 7.8 %copy-start.6 = (f32[1,1,1536]{2,1,0:T(1,128)S(1)}, f32[1,1,1536]{2,1,0:T(1,128)}, u32[]{:S(2)}) copy-start(f32[1,1,1536]{2,1,0:T(1,128)} %param.25) | copy-start | bytes 18436
  92.1 13.5 %all-to-all-start.2 = ((bf16[4,32,1536]{2,1,0:T(8,128)(2,1)}), bf16[4,32,1536]{2,1,0:T(8,128)(2,1)S(1)}, u32[]{:S(2)}, u32[]{:S(2)}) async-start(bf16[4,32,1536]{2,1,0:T(8,128)(2,1)} %bitcast.8), calls=%async_computation.2 | async-start | bytes 786432 | tf_op jit(solution)/shard_map/all_to_all | solution.py:160
  96.7 34.2 %copy-start.4 = (f32[1,32,32]{2,1,0:T(8,128)S(1)}, f32[1,32,32]{2,1,0:T(8,128)}, u32[]{:S(2)}) copy-start(f32[1,32,32]{2,1,0:T(8,128)} %param.30) | copy-start | bytes 12292
  106.9 13.3 %all-to-all-start.3 = ((f32[2,1,2048]{2,1,0:T(1,128)}), f32[2,1,2048]{2,1,0:T(1,128)S(1)}, u32[]{:S(2)}, u32[]{:S(2)}) async-start(f32[2,1,2048]{2,1,0:T(1,128)} %reshape.174), calls=%async_computation.3 | async-start | bytes 32768 | tf_op jit(solution)/shard_map/all_to_all | solution.py:168
  124.2 15.2 %all-to-all-start.4 = ((f32[32,1,2]{2,1,0:T(1,128)}), f32[32,1,2]{2,1,0:T(1,128)S(1)}, u32[]{:S(2)}, u32[]{:S(2)}) async-start(f32[32,1,2]{2,1,0:T(1,128)} %broadcast_in_dim.11), calls=%async_computation.4 | async-start | bytes 32768 | tf_op jit(solution)/shard_map/all_to_all | solution.py:176
Sparse Core Ops, SparseCore 0:
  10.1 46.8 all-gather.2

commit v9 on v7

--- a/solution.py
+++ b/solution.py
@@ -1,3 +1,5 @@
+import functools
+
 import jax
 import jax.numpy as jnp
 from jax import lax
@@ -24,12 +26,17 @@
     return lax.ppermute(block, axis, route)
 
 
-def attention_partials_kernel(q_ref, kv_ref, mask_ref, out_ref):
+def attention_partials_kernel(rows_dev, img_dev, n_x, q_ref, kv_ref, info_ref, out_ref):
     rows = q_ref.shape[0]
     lanes = 2 * HD
     lane = lax.broadcasted_iota(jnp.int32, (1, lanes), 1)
     low = lane < HD
-    usable = mask_ref[...] > 0
+    keys = kv_ref.shape[1]
+    position = lax.broadcasted_iota(jnp.int32, (1, keys), 1)
+    within = position % rows_dev
+    source = (position // rows_dev) * n_x + info_ref[0:1, 1:2]
+    text_slot = source * (rows_dev - img_dev) + within - img_dev
+    usable = (within < img_dev) | (text_slot < info_ref[0:1, 0:1])
     factor = HD ** (-0.5)
     maxes = []
     sums = []
@@ -56,11 +63,11 @@
     out_ref[:, width : width + HEADS] = jnp.concatenate(maxes, axis=1)
     out_ref[:, width + HEADS : width + 2 * HEADS] = jnp.concatenate(sums, axis=1)
 
-def attention_partials(q, kv, mask):
+def attention_partials(q, kv, info, rows_dev, img_dev, n_x):
     rows = q.shape[0]
     width = HEADS * HD
     return pl.pallas_call(
-        attention_partials_kernel,
+        functools.partial(attention_partials_kernel, rows_dev, img_dev, n_x),
         out_shape=jax.ShapeDtypeStruct((rows, width + 2 * HEADS), jnp.float32),
         in_specs=[pl.BlockSpec(memory_space=pltpu.VMEM)] * 3,
         out_specs=pl.BlockSpec(memory_space=pltpu.VMEM),
@@ -69,7 +76,7 @@
             transcendentals=2 * rows * kv.shape[1] * HEADS,
             bytes_accessed=q.size * 2 + kv.size * 2 + rows * (width + 2 * HEADS) * 4,
         ),
-    )(q, kv, mask)
+    )(q, kv, info)
 
 
 def modulate_rows(hidden, shift_row, scale_row):
@@ -112,14 +119,10 @@
     piece = lax.all_gather(key_value[:, 0, 0], "sz", axis=1, tiled=True)
     q_rows = query_rows.shape[0]
     piece_rows = piece.shape[1]
-    positions = jnp.arange(piece_rows, dtype=jnp.int32)
-    within = positions % rows_dev
-    source = (positions // rows_dev) * n_x + x_index
-    text_slot = source * txt_dev + within - img_dev
-    usable = ((within < img_dev) | (text_slot < length)).astype(jnp.float32)[None, :]
     width = HEADS * HD
+    info = jnp.stack([length, x_index.astype(jnp.int32)]).reshape(1, 2)
     packed = attention_partials(
-        query_rows, piece.reshape(2, piece_rows, width), usable
+        query_rows, piece.reshape(2, piece_rows, width), info, rows_dev, img_dev, n_x
     ).reshape(n_x, img_dev, width + 2 * HEADS)
     got = lax.all_to_all(packed, "sx", 0, 0, tiled=True)
     got_out = got[:, :, :width].reshape(n_x, img_dev, HEADS, HD)
@@ -169,7 +172,13 @@
     cond_part = jnp.where(is_cond, velocity, received)
     uncond = jnp.where(is_cond, received, velocity)
     guided_full = uncond + guidance_weight * (cond_part - uncond)
-    partials = jnp.stack([jnp.sum(guided_full * guided_full), jnp.max(jnp.abs(guided_full))])
+    square_sum, largest = lax.reduce(
+        (guided_full * guided_full, jnp.abs(guided_full)),
+        (jnp.float32(0), jnp.float32(0)),
+        lambda a, b: (a[0] + b[0], jnp.maximum(a[1], b[1])),
+        (0, 1),
+    )
+    partials = jnp.stack([square_sum, largest])
     n_seq = lax.axis_size(("sz", "sx"))
     gathered = lax.all_to_all(
         jnp.broadcast_to(partials[None], (n_seq, 2)), ("sz", "sx"), 0, 0, tiled=True

time: 143 us -> 143 us (level)
  no operation moved by 1% of the time
where the time goes in v9:
time: 143 us
  blocking collectives  49.9 us (35%)
  starting transfers between devices  28.9 us (20%)
  waiting for transfers between devices  24.3 us (17%)
  between operations  17.4 us (12%)
  matrix products  7.87 us (6%)
  Pallas kernels  5.39 us (4%)
  other arithmetic  4.91 us (3%)
  local copies, waits for them, and re-layouts  4.03 us (3%)
    all_gather x1, blocking collectives, per_device(): piece = lax.all_gather(key_value[:, 0, 0], 'sz', axis=1, tiled=True)  35.1 us
    all_gather x1, blocking collectives, per_device(): line_in = lax.all_gather(mlp_in, 'ry', axis=0, tiled=True)  14.8 us
    all_to_all x1, waiting for transfers between devices, per_device(): lax.all_to_all(jnp.broadcast_to(partials[None], (n_seq, 2)), ('sz', 'sx')...  8.88 us
    all_to_all x1, waiting for transfers between devices, per_device(): lax.all_to_all(mlp_parts, 'ry', 0, 0, tiled=True).astype(jnp.float32)  6.41 us
    all_to_all x1, starting transfers between devices, per_device(): lax.all_to_all(mlp_parts, 'ry', 0, 0, tiled=True).astype(jnp.float32)  5.71 us
    all_to_all x1, starting transfers between devices, per_device(): lax.all_to_all(jnp.broadcast_to(partials[None], (n_seq, 2)), ('sz', 'sx')...  5.68 us
    pallas_call x1, Pallas kernels, attention_partials(): pl.pallas_call(functools.partial(attention_partials_kernel, rows_dev, img...  5.39 us
    ppermute x1, waiting for transfers between devices, swapped(): return lax.ppermute(block, axis, route)  5.06 us
  transfers between devices with their start and end apart: 8, of which 4 were waited for; matrix products, arithmetic and copies ran while one was open for 6% of the time, Pallas kernels for 4%

profile of v9, /device:TPU:56, one launch (start us, length us, event | category | flops | bytes accessed | tf_op | source)
XLA Modules:
  0.0 142.8 jit_solution(529875455735905643)
XLA Ops:
  7.2 0.0 copy-start
  7.2 0.0 all-gather.3.cloned.1.call-start
  7.2 0.7 all-gather.3.cloned.1.call-update
  7.9 1.5 %broadcast_in_dim.7 = bf16[4,32,768]{2,1,0:T(8,128)(2,1)} broadcast(bf16[32,768]{1,0:T(8,128)(2,1)} %bitcast.35), dimensions={1,2} | broadcast | bytes 245760 | tf_op jit(solution)/shard_map/broadcast_in_dim | solution.py:117
  9.4 4.3 %all-to-all-start = ((bf16[4,32,768]{2,1,0:T(8,128)(2,1)}), bf16[4,32,768]{2,1,0:T(8,128)(2,1)S(1)}, u32[]{:S(2)}, u32[]{:S(2)}) async-start(bf16[4,32,768]{2,1,0:T(8,128)(2,1)} %broadcast_in_dim.7), calls=%async_computation | async-start | bytes 393216 | tf_op jit(solution)/shard_map/all_to_all | solution.py:116
  13.7 35.1 %all-gather = bf16[2,1,1,320,768]{4,3,0,2,1:T(8,128)(2,1)} all-gather(bf16[2,1,1,40,768]{4,3,0,2,1:T(8,128)(2,1)} %bitcast.34), channel_id=2, replica_groups=mesh['cfg'=2,'ry'=4,'rc'=2,'sz'=8,'sx'=4] {'sz'}, dimensions={3}, use_global_device_ids=true | all-gather | bytes 1105920 | tf_op jit(solution)/shard_map/all_gather | solution.py:119
  49.5 0.6 add_bitcast_fusion.info_ref
  50.1 0.0 all-to-all-done
  50.1 0.0 copy-start.2
  50.1 0.7 copy-done.2
  50.7 0.0 copy-start.1
  50.7 0.0 copy-start.7
  50.8 0.0 copy-start.8
  50.8 0.0 copy-start.5
  50.8 5.4 %shard_map.175 = f32[128,792]{1,0:T(8,128)} custom-call(bf16[128,768]{1,0:T(8,128)(2,1)} %bitcast.33, bf16[2,320,768]{2,1,0:T(8,128)(2,1)} %bitcast.31, s32[1,2]{1,0:T(1,128)} %add_bitcast_fusion.info_ref), custom_call_target="tpu_custom_call" | custom-call | flops 251658240 | bytes 1585152 | tf_op jit(solution)/shard_map/pallas_call | solution.py:69
  56.1 5.0 %all-to-all-start.1 = ((f32[4,32,792]{2,1,0:T(8,128)}), f32[4,32,792]{2,1,0:T(8,128)S(1)}, u32[]{:S(2)}, u32[]{:S(2)}) async-start(f32[4,32,792]{2,1,0:T(8,128)} %bitcast.32), calls=%async_computation.1 | async-start | bytes 917504 | tf_op jit(solution)/shard_map/all_to_all | solution.py:127
  61.2 0.0 copy-done.1
  61.2 1.9 %collective-permute-start = (bf16[1536,384]{1,0:T(8,128)(2,1)S(1)}, bf16[1536,384]{1,0:T(8,128)(2,1)}, u32[]{:S(2)}, u32[]{:S(2)}) collective-permute-start(bf16[1536,384]{1,0:T(8,128)(2,1)S(1)} %copy-done.1), channel_id=1, source_target_pairs={{0,32},{32,0},{1,33},{33,1},{2,34},{34,2},{3,35},{35,3},{4,36},{36... | collective-permute-start | bytes 3538952 | tf_op jit(solution)/shard_map/ppermute | solution.py:145
  63.1 2.4 %collective-permute-start.1 = (bf16[384,1536]{1,0:T(8,128)(2,1)}, bf16[384,1536]{1,0:T(8,128)(2,1)}, u32[]{:S(2)}, u32[]{:S(2)}) collective-permute-start(bf16[384,1536]{1,0:T(8,128)(2,1)} %param.28), channel_id=1, source_target_pairs={{0,32},{32,0},{1,33},{33,1},{2,34},{34,2},{3,35},{35,3},{4,36},{36... | collective-permute-start | bytes 3538952 | tf_op jit(solution)/shard_map/ppermute | solution.py:146
  65.5 0.0 copy-done.7
  65.6 0.0 copy-done.8
  65.6 0.0 copy-done.5
  65.6 3.3 %all-to-all-done.1 = f32[4,32,792]{2,1,0:T(8,128)S(1)} async-done(((f32[4,32,792]{2,1,0:T(8,128)}), f32[4,32,792]{2,1,0:T(8,128)S(1)}, u32[]{:S(2)}, u32[]{:S(2)}) %all-to-all-start.1) | async-done | bytes 405536 | tf_op jit(solution)/shard_map/all_to_all | solution.py:127
  68.9 0.1 fusion.35
  69.0 0.3 mul.120
  69.3 0.0 copy-start.3
  69.4 0.3 mul.121
  69.7 0.1 div.26
  69.8 0.1 div.27
  69.9 0.0 all-gather.3.cloned.1.call-done
  70.0 0.3 copy-done.3
  70.2 2.6 %fusion.45 = (f32[32]{0:T(128)S(1)}, f32[32,1536]{1,0:T(8,128)S(1)}) fusion(bf16[768,1536]{0,1:T(8,128)(2,1)} %all-gather.3.cloned.1.call-done, f32[32,768]{1,0:T(8,128)S(1)} %fusion.2, f32[32,768]{1,0:T(8,128)S(1)} %div.27, f32[1536]{0:T(1024)S(1)} %reduce.19, bf16[1,1,32,1536]{3,2,1,0:T(8,128)(2,1)S(1)} %copy-done.3), kind=kOutput, calls=%fused_computation.71 | convolution fusion | flops 75743200 | bytes 2857088 | tf_op jit(solution)/shard_map/dot_general | solution.py:136
  72.8 0.2 multiply_reduce_fusion.1
  73.0 0.1 add_convert_fusion.1
  73.2 14.8 %all_gather.11 = bf16[128,1536]{1,0:T(8,128)(2,1)S(1)} all-gather(bf16[32,1536]{1,0:T(8,128)(2,1)S(1)} %add_convert_fusion.1), channel_id=1, replica_groups=mesh['cfg'=2,'ry'=4,'rc'=2,'sz'=8,'sx'=4] {'ry'}, dimensions={0}, use_global_device_ids=true | all-gather | bytes 491520 | tf_op jit(solution)/shard_map/all_gather | solution.py:147
  87.9 2.0 %fusion.21 = f32[128,1536]{1,0:T(8,128)S(1)} fusion(bf16[384,1536]{1,0:T(8,128)(2,1)} %param.28, bf16[128,1536]{1,0:T(8,128)(2,1)S(1)} %all_gather.11, bf16[1536,384]{1,0:T(8,128)(2,1)S(1)} %copy-done.1), kind=kOutput, calls=%fused_computation.31 | convolution fusion | flops 302432256 | bytes 3538944 | tf_op jit(solution)/shard_map/dot_general | solution.py:156
  89.9 0.0 copy-start.9
  90.0 0.0 copy-start.10
  90.0 0.0 copy-start.6
  90.0 0.0 collective-permute-done
  90.0 0.0 collective-permute-done.1
  90.0 3.1 %fusion = bf16[128,1536]{1,0:T(8,128)(2,1)} fusion(f32[128,1536]{1,0:T(8,128)S(1)} %fusion.21, bf16[384,1536]{1,0:T(8,128)(2,1)} %collective-permute-done.1, bf16[128,1536]{1,0:T(8,128)(2,1)S(1)} %all_gather.11, bf16[1536,384]{1,0:T(8,128)(2,1)} %collective-permute-done), kind=kOutput, calls=%fused_computation.1 | convolution fusion | flops 302825472 | bytes 3932160 | tf_op jit(solution)/shard_map/dot_general | solution.py:157
  93.1 5.7 %all-to-all-start.2 = ((bf16[4,32,1536]{2,1,0:T(8,128)(2,1)}), bf16[4,32,1536]{2,1,0:T(8,128)(2,1)S(1)}, u32[]{:S(2)}, u32[]{:S(2)}) async-start(bf16[4,32,1536]{2,1,0:T(8,128)(2,1)} %bitcast.10), calls=%async_computation.2 | async-start | bytes 786432 | tf_op jit(solution)/shard_map/all_to_all | solution.py:163
  98.8 0.0 copy-done.9
  98.8 0.0 copy-start.4
  98.8 0.0 copy-done.10
  98.9 0.0 copy-done.6
  98.9 6.4 %all-to-all-done.2 = bf16[4,32,1536]{2,1,0:T(8,128)(2,1)S(1)} async-done(((bf16[4,32,1536]{2,1,0:T(8,128)(2,1)}), bf16[4,32,1536]{2,1,0:T(8,128)(2,1)S(1)}, u32[]{:S(2)}, u32[]{:S(2)}) %all-to-all-start.2) | async-done | bytes 393248 | tf_op jit(solution)/shard_map/all_to_all | solution.py:163
  105.3 0.1 convert_reduce_fusion
  105.4 0.1 fusion.44
  105.5 0.2 multiply_reduce_fusion
  105.7 0.0 copy-done
  105.7 0.2 fusion.19
  106.0 3.8 %collective-permute-start.2 = (f32[32,64]{1,0:T(8,128)S(1)}, f32[32,64]{1,0:T(8,128)S(1)}, u32[]{:S(2)}, u32[]{:S(2)}) collective-permute-start(f32[32,64]{1,0:T(8,128)S(1)} %fusion.19), channel_id=1, source_target_pairs={{0,256},{256,0},{1,257},{257,1},{2,258},{258,2},{3,259},{259,3},{4... | collective-permute-start | bytes 24584 | tf_op jit(solution)/shard_map/ppermute | solution.py:26
  110.5 5.1 %collective-permute-done.2 = f32[32,64]{1,0:T(8,128)S(1)} collective-permute-done((f32[32,64]{1,0:T(8,128)S(1)}, f32[32,64]{1,0:T(8,128)S(1)}, u32[]{:S(2)}, u32[]{:S(2)}) %collective-permute-start.2) | collective-permute-done | bytes 8224 | tf_op jit(solution)/shard_map/ppermute | solution.py:26
  115.5 0.6 abs_reduce_fusion
  116.2 1.4 pad_maximum_fusion
  117.5 0.6 broadcast_in_dim.8
  118.1 5.7 %all-to-all-start.3 = ((f32[32,1,2]{2,1,0:T(1,128)}), f32[32,1,2]{2,1,0:T(1,128)S(1)}, u32[]{:S(2)}, u32[]{:S(2)}) async-start(f32[32,1,2]{2,1,0:T(1,128)} %broadcast_in_dim.8), calls=%async_computation.3 | async-start | bytes 32768 | tf_op jit(solution)/shard_map/all_to_all | solution.py:183
  123.8 0.0 copy-done.4
  123.8 0.7 bitcast_add_fusion
  124.5 8.9 %all-to-all-done.3 = f32[32,1,2]{2,1,0:T(1,128)S(1)} async-done(((f32[32,1,2]{2,1,0:T(1,128)}), f32[32,1,2]{2,1,0:T(1,128)S(1)}, u32[]{:S(2)}, u32[]{:S(2)}) %all-to-all-start.3) | async-done | bytes 288 | tf_op jit(solution)/shard_map/all_to_all | solution.py:183
  133.4 0.1 copy.22
  133.5 0.6 slice_reduce_fusion.1
  (13 shorter events, 0.2 us)
Async XLA Ops:
  7.2 98.6 %copy-start = (bf16[1536,64]{0,1:T(8,128)(2,1)S(1)}, bf16[1536,64]{0,1:T(8,128)(2,1)}, u32[]{:S(2)}) copy-start(bf16[1536,64]{0,1:T(8,128)(2,1)} %param.29) | copy-start | bytes 589828
  7.2 62.8 %all-gather.3.cloned.1.call-start = ((), (), s32[]{:S(2)}) async-start(), calls=%async_computation.4 | async-start | bytes 2654208 | tf_op jit(solution)/shard_map/all_gather | solution.py:138
  9.4 40.7 %all-to-all-start = ((bf16[4,32,768]{2,1,0:T(8,128)(2,1)}), bf16[4,32,768]{2,1,0:T(8,128)(2,1)S(1)}, u32[]{:S(2)}, u32[]{:S(2)}) async-start(bf16[4,32,768]{2,1,0:T(8,128)(2,1)} %broadcast_in_dim.7), calls=%async_computation | async-start | bytes 393216 | tf_op jit(solution)/shard_map/all_to_all | solution.py:116
  50.1 0.7 copy-start.2
  50.7 10.4 %copy-start.1 = (bf16[1536,384]{1,0:T(8,128)(2,1)S(1)}, bf16[1536,384]{1,0:T(8,128)(2,1)}, u32[]{:S(2)}) copy-start(bf16[1536,384]{1,0:T(8,128)(2,1)} %param.27) | copy-start | bytes 3538948
  50.7 14.8 %copy-start.7 = (f32[1,1,1536]{2,1,0:T(1,128)S(1)}, f32[1,1,1536]{2,1,0:T(1,128)}, u32[]{:S(2)}) copy-start(f32[1,1,1536]{2,1,0:T(1,128)} %param.20) | copy-start | bytes 18436
  50.8 14.8 %copy-start.8 = (f32[1,1,1536]{2,1,0:T(1,128)S(1)}, f32[1,1,1536]{2,1,0:T(1,128)}, u32[]{:S(2)}) copy-start(f32[1,1,1536]{2,1,0:T(1,128)} %param.21) | copy-start | bytes 18436
  50.8 14.8 %copy-start.5 = (f32[1,1,1536]{2,1,0:T(1,128)S(1)}, f32[1,1,1536]{2,1,0:T(1,128)}, u32[]{:S(2)}) copy-start(f32[1,1,1536]{2,1,0:T(1,128)} %param.22) | copy-start | bytes 18436
  56.1 12.8 %all-to-all-start.1 = ((f32[4,32,792]{2,1,0:T(8,128)}), f32[4,32,792]{2,1,0:T(8,128)S(1)}, u32[]{:S(2)}, u32[]{:S(2)}) async-start(f32[4,32,792]{2,1,0:T(8,128)} %bitcast.32), calls=%async_computation.1 | async-start | bytes 917504 | tf_op jit(solution)/shard_map/all_to_all | solution.py:127
  61.2 28.8 %collective-permute-start = (bf16[1536,384]{1,0:T(8,128)(2,1)S(1)}, bf16[1536,384]{1,0:T(8,128)(2,1)}, u32[]{:S(2)}, u32[]{:S(2)}) collective-permute-start(bf16[1536,384]{1,0:T(8,128)(2,1)S(1)} %copy-done.1), channel_id=1, source_target_pairs={{0,32},{32,0},{1,33},{33,1},{2,34},{34,2},{3,35},{35,3},{4,36},{36... | collective-permute-start | bytes 3538952 | tf_op jit(solution)/shard_map/ppermute | solution.py:145
  63.1 26.9 %collective-permute-start.1 = (bf16[384,1536]{1,0:T(8,128)(2,1)}, bf16[384,1536]{1,0:T(8,128)(2,1)}, u32[]{:S(2)}, u32[]{:S(2)}) collective-permute-start(bf16[384,1536]{1,0:T(8,128)(2,1)} %param.28), channel_id=1, source_target_pairs={{0,32},{32,0},{1,33},{33,1},{2,34},{34,2},{3,35},{35,3},{4,36},{36... | collective-permute-start | bytes 3538952 | tf_op jit(solution)/shard_map/ppermute | solution.py:146
  69.3 0.9 copy-start.3
  89.9 8.9 %copy-start.9 = (f32[1,1,1536]{2,1,0:T(1,128)S(1)}, f32[1,1,1536]{2,1,0:T(1,128)}, u32[]{:S(2)}) copy-start(f32[1,1,1536]{2,1,0:T(1,128)} %param.23) | copy-start | bytes 18436
  90.0 8.9 %copy-start.10 = (f32[1,1,1536]{2,1,0:T(1,128)S(1)}, f32[1,1,1536]{2,1,0:T(1,128)}, u32[]{:S(2)}) copy-start(f32[1,1,1536]{2,1,0:T(1,128)} %param.24) | copy-start | bytes 18436
  90.0 8.9 %copy-start.6 = (f32[1,1,1536]{2,1,0:T(1,128)S(1)}, f32[1,1,1536]{2,1,0:T(1,128)}, u32[]{:S(2)}) copy-start(f32[1,1,1536]{2,1,0:T(1,128)} %param.25) | copy-start | bytes 18436
  93.1 12.2 %all-to-all-start.2 = ((bf16[4,32,1536]{2,1,0:T(8,128)(2,1)}), bf16[4,32,1536]{2,1,0:T(8,128)(2,1)S(1)}, u32[]{:S(2)}, u32[]{:S(2)}) async-start(bf16[4,32,1536]{2,1,0:T(8,128)(2,1)} %bitcast.10), calls=%async_computation.2 | async-start | bytes 786432 | tf_op jit(solution)/shard_map/all_to_all | solution.py:163
  98.8 25.0 %copy-start.4 = (f32[1,32,32]{2,1,0:T(8,128)S(1)}, f32[1,32,32]{2,1,0:T(8,128)}, u32[]{:S(2)}) copy-start(f32[1,32,32]{2,1,0:T(8,128)} %param.30) | copy-start | bytes 12292
  106.0 9.5 %collective-permute-start.2 = (f32[32,64]{1,0:T(8,128)S(1)}, f32[32,64]{1,0:T(8,128)S(1)}, u32[]{:S(2)}, u32[]{:S(2)}) collective-permute-start(f32[32,64]{1,0:T(8,128)S(1)} %fusion.19), channel_id=1, source_target_pairs={{0,256},{256,0},{1,257},{257,1},{2,258},{258,2},{3,259},{259,3},{4... | collective-permute-start | bytes 24584 | tf_op jit(solution)/shard_map/ppermute | solution.py:26
  118.1 15.3 %all-to-all-start.3 = ((f32[32,1,2]{2,1,0:T(1,128)}), f32[32,1,2]{2,1,0:T(1,128)S(1)}, u32[]{:S(2)}, u32[]{:S(2)}) async-start(f32[32,1,2]{2,1,0:T(1,128)} %broadcast_in_dim.8), calls=%async_computation.3 | async-start | bytes 32768 | tf_op jit(solution)/shard_map/all_to_all | solution.py:183
Sparse Core Ops, SparseCore 0:
  10.1 44.5 all-gather.2

commit v10 on v7

--- a/solution.py
+++ b/solution.py
@@ -70,6 +70,36 @@
             bytes_accessed=q.size * 2 + kv.size * 2 + rows * (width + 2 * HEADS) * 4,
         ),
     )(q, kv, mask)
+
+
+def mlp_partials_kernel(x_ref, up_a_ref, up_b_ref, down_a_ref, down_b_ref, out_ref):
+    x = x_ref[...]
+    inner_a = jax.nn.gelu(
+        jnp.dot(x, up_a_ref[...], preferred_element_type=jnp.float32), approximate=True
+    ).astype(jnp.bfloat16)
+    inner_b = jax.nn.gelu(
+        jnp.dot(x, up_b_ref[...], preferred_element_type=jnp.float32), approximate=True
+    ).astype(jnp.bfloat16)
+    out_ref[...] = (
+        jnp.dot(inner_a, down_a_ref[...], preferred_element_type=jnp.float32)
+        + jnp.dot(inner_b, down_b_ref[...], preferred_element_type=jnp.float32)
+    ).astype(out_ref.dtype)
+
+def mlp_partials(x, up_a, up_b, down_a, down_b):
+    rows, width = x.shape
+    units = up_a.shape[1]
+    return pl.pallas_call(
+        mlp_partials_kernel,
+        out_shape=jax.ShapeDtypeStruct((rows, down_a.shape[1]), jnp.bfloat16),
+        in_specs=[pl.BlockSpec(memory_space=pltpu.VMEM)] * 5,
+        out_specs=pl.BlockSpec(memory_space=pltpu.VMEM),
+        compiler_params=pltpu.CompilerParams(vmem_limit_bytes=32 * 1024 * 1024),
+        cost_estimate=pl.CostEstimate(
+            flops=8 * rows * width * units,
+            transcendentals=2 * rows * units,
+            bytes_accessed=2 * (x.size + 4 * up_a.size + rows * down_a.shape[1]),
+        ),
+    )(x, up_a, up_b, down_a, down_b)
 
 
 def modulate_rows(hidden, shift_row, scale_row):
@@ -142,18 +172,8 @@
     up_other = lax.ppermute(w_up, "rc", pair)
     down_other = lax.ppermute(w_down, "rc", pair)
     line_in = lax.all_gather(mlp_in, "ry", axis=0, tiled=True)
-    inner_own = jax.nn.gelu(
-        jnp.dot(line_in, w_up, preferred_element_type=jnp.float32), approximate=True
-    ).astype(jnp.bfloat16)
-    inner_other = jax.nn.gelu(
-        jnp.dot(line_in, up_other, preferred_element_type=jnp.float32), approximate=True
-    ).astype(jnp.bfloat16)
     mlp_parts = (
-        (
-            jnp.dot(inner_own, w_down, preferred_element_type=jnp.float32)
-            + jnp.dot(inner_other, down_other, preferred_element_type=jnp.float32)
-        )
-        .astype(jnp.bfloat16)
+        mlp_partials(line_in, w_up, up_other, w_down, down_other)
         .reshape(n_y, img_dev, w_down.shape[1])
     )
     mlp_out = jnp.sum(

time: 143 us -> 146 us (1.021)
  matrix products: 7.88 us -> 2.8 us
  local copies, waits for them, and re-layouts: 4.03 us -> 8.3 us
  Pallas kernels: 5.38 us -> 8.79 us
    dot_general x2 -> x0, matrix products: 5.08 us -> none  [the longest x1 3.09 us: per_device(): jnp.dot(inner_other, down_other, preferred_element_type=jnp.float32)]
    pallas_call x0 -> x1, Pallas kernels: none -> 3.5 us  [mlp_partials(): pl.pallas_call(mlp_partials_kernel, out_shape=jax.ShapeDtypeStruct((rows,...]
    div x2, local copies, waits for them, and re-layouts: 0.23 us -> 2.52 us  [per_device(): numerator / denominator[:, :, None]]
    mul x2, local copies, waits for them, and re-layouts: 0.62 us -> 2.86 us  [per_device(): numerator = jnp.sum(rescale[:, :, :, None] * got_out, axis=0)]
  transfers between devices with their start and end apart: 8 -> 8, of which waited for: 4 -> 4; matrix products, arithmetic and copies ran while one was open for 6% -> 8% of each run, Pallas kernels for 4% -> 4%
where the time goes in v10:
time: 146 us; the launch traced here: 145 us
  blocking collectives  49.9 us (34%)
  starting transfers between devices  29 us (20%)
  waiting for transfers between devices  24.3 us (17%)
  between operations  17.4 us (12%)
  Pallas kernels  8.79 us (6%)
  local copies, waits for them, and re-layouts  8.3 us (6%)
  other arithmetic  4.86 us (3%)
  matrix products  2.8 us (2%)
    all_gather x1, blocking collectives, per_device(): piece = lax.all_gather(key_value[:, 0, 0], 'sz', axis=1, tiled=True)  35.1 us
    all_gather x1, blocking collectives, per_device(): line_in = lax.all_gather(mlp_in, 'ry', axis=0, tiled=True)  14.8 us
    all_to_all x1, waiting for transfers between devices, per_device(): lax.all_to_all(jnp.broadcast_to(partials[None], (n_seq, 2)), ('sz', 'sx')...  8.88 us
    all_to_all x1, waiting for transfers between devices, per_device(): lax.all_to_all(mlp_parts, 'ry', 0, 0, tiled=True).astype(jnp.float32)  6.41 us
    all_to_all x1, starting transfers between devices, per_device(): lax.all_to_all(mlp_parts, 'ry', 0, 0, tiled=True).astype(jnp.float32)  5.87 us
    all_to_all x1, starting transfers between devices, per_device(): lax.all_to_all(jnp.broadcast_to(partials[None], (n_seq, 2)), ('sz', 'sx')...  5.67 us
    pallas_call x1, Pallas kernels, attention_partials(): pl.pallas_call(attention_partials_kernel, out_shape=jax.ShapeDtypeStruct(...  5.29 us
    ppermute x1, waiting for transfers between devices, swapped(): return lax.ppermute(block, axis, route)  5.07 us
  transfers between devices with their start and end apart: 8, of which 4 were waited for; matrix products, arithmetic and copies ran while one was open for 8% of the time, Pallas kernels for 4%

profile of v10, /device:TPU:56, one launch (start us, length us, event | category | flops | bytes accessed | tf_op | source)
XLA Modules:
  0.0 145.4 jit_solution(8629165508237701807)
XLA Ops:
  7.2 0.0 copy-start
  7.2 0.0 copy-start.1
  7.2 0.0 copy-start.2
  7.2 0.0 copy-start.7
  7.2 0.0 copy-start.8
  7.2 0.0 all-gather.3.cloned.1.call-start
  7.3 0.7 all-gather.3.cloned.1.call-update
  8.0 0.0 copy-start.5
  8.0 1.5 %broadcast_in_dim.7 = bf16[4,32,768]{2,1,0:T(8,128)(2,1)} broadcast(bf16[32,768]{1,0:T(8,128)(2,1)} %bitcast.26), dimensions={1,2} | broadcast | bytes 245760 | tf_op jit(solution)/shard_map/broadcast_in_dim | solution.py:140
  9.5 4.3 %all-to-all-start = ((bf16[4,32,768]{2,1,0:T(8,128)(2,1)}), bf16[4,32,768]{2,1,0:T(8,128)(2,1)S(1)}, u32[]{:S(2)}, u32[]{:S(2)}) async-start(bf16[4,32,768]{2,1,0:T(8,128)(2,1)} %broadcast_in_dim.7), calls=%async_computation | async-start | bytes 393216 | tf_op jit(solution)/shard_map/all_to_all | solution.py:139
  13.8 35.1 %all-gather = bf16[2,1,1,320,768]{4,3,0,2,1:T(8,128)(2,1)} all-gather(bf16[2,1,1,40,768]{4,3,0,2,1:T(8,128)(2,1)} %bitcast.25), channel_id=2, replica_groups=mesh['cfg'=2,'ry'=4,'rc'=2,'sz'=8,'sx'=4] {'sz'}, dimensions={3}, use_global_device_ids=true | all-gather | bytes 1105920 | tf_op jit(solution)/shard_map/all_gather | solution.py:142
  49.6 0.6 or_convert_fusion.mask_ref
  50.1 0.0 all-to-all-done
  50.1 0.0 copy-start.3
  50.2 0.7 copy-done.3
  50.8 5.3 %shard_map.175 = f32[128,792]{1,0:T(8,128)} custom-call(bf16[128,768]{1,0:T(8,128)(2,1)} %bitcast.24, bf16[2,320,768]{2,1,0:T(8,128)(2,1)} %bitcast.22, f32[1,320]{1,0:T(1,128)} %or_convert_fusion.mask_ref), custom_call_target="tpu_custom_call" | custom-call | flops 251658240 | bytes 1585152 | tf_op jit(solution)/shard_map/pallas_call | solution.py:62
  56.1 5.0 %all-to-all-start.1 = ((f32[4,32,792]{2,1,0:T(8,128)}), f32[4,32,792]{2,1,0:T(8,128)S(1)}, u32[]{:S(2)}, u32[]{:S(2)}) async-start(f32[4,32,792]{2,1,0:T(8,128)} %bitcast.23), calls=%async_computation.1 | async-start | bytes 917504 | tf_op jit(solution)/shard_map/all_to_all | solution.py:154
  61.1 0.0 copy-done.1
  61.1 1.9 %collective-permute-start = (bf16[1536,384]{1,0:T(8,128)(2,1)S(1)}, bf16[1536,384]{1,0:T(8,128)(2,1)}, u32[]{:S(2)}, u32[]{:S(2)}) collective-permute-start(bf16[1536,384]{1,0:T(8,128)(2,1)S(1)} %copy-done.1), channel_id=1, source_target_pairs={{0,32},{32,0},{1,33},{33,1},{2,34},{34,2},{3,35},{35,3},{4,36},{36... | collective-permute-start | bytes 3538952 | tf_op jit(solution)/shard_map/ppermute | solution.py:172
  63.1 0.0 copy-done.2
  63.1 2.4 %collective-permute-start.1 = (bf16[384,1536]{1,0:T(8,128)(2,1)S(1)}, bf16[384,1536]{1,0:T(8,128)(2,1)}, u32[]{:S(2)}, u32[]{:S(2)}) collective-permute-start(bf16[384,1536]{1,0:T(8,128)(2,1)S(1)} %copy-done.2), channel_id=1, source_target_pairs={{0,32},{32,0},{1,33},{33,1},{2,34},{34,2},{3,35},{35,3},{4,36},{36... | collective-permute-start | bytes 3538952 | tf_op jit(solution)/shard_map/ppermute | solution.py:173
  65.5 0.0 copy-done.7
  65.5 0.0 copy-done.8
  65.6 0.0 copy-done.5
  65.6 3.3 %all-to-all-done.1 = f32[4,32,792]{2,1,0:T(8,128)S(1)} async-done(((f32[4,32,792]{2,1,0:T(8,128)}), f32[4,32,792]{2,1,0:T(8,128)S(1)}, u32[]{:S(2)}, u32[]{:S(2)}) %all-to-all-start.1) | async-done | bytes 405536 | tf_op jit(solution)/shard_map/all_to_all | solution.py:154
  68.9 0.1 fusion.7
  69.0 1.4 mul.126
  70.3 1.5 %mul.127 = f32[4,32,768]{2,1,0:T(8,128)S(1)} reshape(f32[4,32,12,64]{3,2,1,0:T(8,128)} %mul.126) | data formatting | bytes 786432 | tf_op jit(solution)/shard_map/mul | solution.py:160
  71.8 0.8 div.40
  72.7 1.7 %div.41 = f32[32,768]{1,0:T(8,128)} reshape(f32[32,12,64]{2,1,0:T(8,128)} %div.40) | data formatting | bytes 196608 | tf_op jit(solution)/shard_map/div | solution.py:162
  74.4 0.0 all-gather.3.cloned.1.call-done
  74.4 2.6 %fusion.13 = (f32[32]{0:T(128)S(1)}, f32[32,1536]{1,0:T(8,128)S(1)}) fusion(bf16[768,1536]{0,1:T(8,128)(2,1)} %all-gather.3.cloned.1.call-done, f32[32,768]{1,0:T(8,128)S(1)} %fusion.1, f32[32,768]{1,0:T(8,128)} %div.41, f32[1536]{0:T(1024)S(1)} %reduce.3, bf16[1,1,32,1536]{3,2,1,0:T(8,128)(2,1)} %param.18), kind=kOutput, calls=%fused_computation.44 | convolution fusion | flops 75743200 | bytes 2857088 | tf_op jit(solution)/shard_map/dot_general | solution.py:163
  77.0 0.2 multiply_reduce_fusion.1
  77.2 0.1 add_convert_fusion.1
  77.3 14.8 %all_gather.11.x_ref = bf16[128,1536]{1,0:T(8,128)(2,1)S(1)} all-gather(bf16[32,1536]{1,0:T(8,128)(2,1)S(1)} %add_convert_fusion.1), channel_id=1, replica_groups=mesh['cfg'=2,'ry'=4,'rc'=2,'sz'=8,'sx'=4] {'ry'}, dimensions={0}, use_global_device_ids=true | all-gather | bytes 491520 | tf_op jit(solution)/shard_map/all_gather | solution.py:174
  92.1 0.0 copy-start.9
  92.1 0.0 copy-start.10
  92.1 0.0 copy-start.6
  92.1 0.0 collective-permute-done.up_b_ref
  92.1 0.0 collective-permute-done.1.down_b_ref
  92.1 3.5 %shard_map.176 = bf16[128,1536]{1,0:T(8,128)(2,1)} custom-call(bf16[128,1536]{1,0:T(8,128)(2,1)S(1)} %all_gather.11.x_ref, bf16[1536,384]{1,0:T(8,128)(2,1)S(1)} %copy-done.1, bf16[1536,384]{1,0:T(8,128)(2,1)} %collective-permute-done.up_b_ref, bf16[384,1536]{1,0:T(8,128)(2,1)S(1)} %copy-done.2, bf16[384,1536]{1,0:T(8,128)(2,1)} %collective-permute-done.1.down_b_ref), custom_call_target="tpu_custom_call" | custom-call | flops 603979776 | bytes 5505024 | tf_op jit(solution)/shard_map/pallas_call | solution.py:91
  95.6 0.0 copy-start.4
  95.6 5.9 %all-to-all-start.2 = ((bf16[4,32,1536]{2,1,0:T(8,128)(2,1)}), bf16[4,32,1536]{2,1,0:T(8,128)(2,1)S(1)}, u32[]{:S(2)}, u32[]{:S(2)}) async-start(bf16[4,32,1536]{2,1,0:T(8,128)(2,1)} %bitcast.8), calls=%async_computation.2 | async-start | bytes 786432 | tf_op jit(solution)/shard_map/all_to_all | solution.py:180
  101.5 0.0 copy-done.9
  101.5 0.0 copy-done.10
  101.6 0.0 copy-done.6
  101.6 6.4 %all-to-all-done.2 = bf16[4,32,1536]{2,1,0:T(8,128)(2,1)S(1)} async-done(((bf16[4,32,1536]{2,1,0:T(8,128)(2,1)}), bf16[4,32,1536]{2,1,0:T(8,128)(2,1)S(1)}, u32[]{:S(2)}, u32[]{:S(2)}) %all-to-all-start.2) | async-done | bytes 393248 | tf_op jit(solution)/shard_map/all_to_all | solution.py:180
  108.0 0.1 convert_reduce_fusion
  108.1 0.1 fusion.12
  108.2 0.2 multiply_reduce_fusion
  108.4 0.0 copy-done
  108.4 0.2 fusion.2
  108.7 3.8 %collective-permute-start.2 = (f32[32,64]{1,0:T(8,128)S(1)}, f32[32,64]{1,0:T(8,128)S(1)}, u32[]{:S(2)}, u32[]{:S(2)}) collective-permute-start(f32[32,64]{1,0:T(8,128)S(1)} %fusion.2), channel_id=1, source_target_pairs={{0,256},{256,0},{1,257},{257,1},{2,258},{258,2},{3,259},{259,3},{4... | collective-permute-start | bytes 24584 | tf_op jit(solution)/shard_map/ppermute | solution.py:24
  113.1 5.1 %collective-permute-done.2 = f32[32,64]{1,0:T(8,128)S(1)} collective-permute-done((f32[32,64]{1,0:T(8,128)S(1)}, f32[32,64]{1,0:T(8,128)S(1)}, u32[]{:S(2)}, u32[]{:S(2)}) %collective-permute-start.2) | collective-permute-done | bytes 8224 | tf_op jit(solution)/shard_map/ppermute | solution.py:24
  118.2 0.6 multiply_reduce_fusion.2
  118.8 1.4 pad_maximum_fusion
  120.2 0.6 broadcast_in_dim.8
  120.8 5.7 %all-to-all-start.3 = ((f32[32,1,2]{2,1,0:T(1,128)}), f32[32,1,2]{2,1,0:T(1,128)S(1)}, u32[]{:S(2)}, u32[]{:S(2)}) async-start(f32[32,1,2]{2,1,0:T(1,128)} %broadcast_in_dim.8), calls=%async_computation.3 | async-start | bytes 32768 | tf_op jit(solution)/shard_map/all_to_all | solution.py:194
  126.5 0.0 copy-done.4
  126.5 0.7 bitcast_add_fusion
  127.2 8.9 %all-to-all-done.3 = f32[32,1,2]{2,1,0:T(1,128)S(1)} async-done(((f32[32,1,2]{2,1,0:T(1,128)}), f32[32,1,2]{2,1,0:T(1,128)S(1)}, u32[]{:S(2)}, u32[]{:S(2)}) %all-to-all-start.3) | async-done | bytes 288 | tf_op jit(solution)/shard_map/all_to_all | solution.py:194
  136.1 0.1 copy.22
  136.1 0.6 slice_reduce_fusion.1
  (12 shorter events, 0.2 us)
Async XLA Ops:
  7.2 101.3 %copy-start = (bf16[1536,64]{0,1:T(8,128)(2,1)S(1)}, bf16[1536,64]{0,1:T(8,128)(2,1)}, u32[]{:S(2)}) copy-start(bf16[1536,64]{0,1:T(8,128)(2,1)} %param.29) | copy-start | bytes 589828
  7.2 54.0 %copy-start.1 = (bf16[1536,384]{1,0:T(8,128)(2,1)S(1)}, bf16[1536,384]{1,0:T(8,128)(2,1)}, u32[]{:S(2)}) copy-start(bf16[1536,384]{1,0:T(8,128)(2,1)} %up_a_ref.1) | copy-start | bytes 3538948
  7.2 55.9 %copy-start.2 = (bf16[384,1536]{1,0:T(8,128)(2,1)S(1)}, bf16[384,1536]{1,0:T(8,128)(2,1)}, u32[]{:S(2)}) copy-start(bf16[384,1536]{1,0:T(8,128)(2,1)} %down_a_ref.1) | copy-start | bytes 3538948
  7.2 58.3 %copy-start.7 = (f32[1,1,1536]{2,1,0:T(1,128)S(1)}, f32[1,1,1536]{2,1,0:T(1,128)}, u32[]{:S(2)}) copy-start(f32[1,1,1536]{2,1,0:T(1,128)} %param.20) | copy-start | bytes 18436
  7.2 58.3 %copy-start.8 = (f32[1,1,1536]{2,1,0:T(1,128)S(1)}, f32[1,1,1536]{2,1,0:T(1,128)}, u32[]{:S(2)}) copy-start(f32[1,1,1536]{2,1,0:T(1,128)} %param.21) | copy-start | bytes 18436
  7.2 67.2 %all-gather.3.cloned.1.call-start = ((), (), s32[]{:S(2)}) async-start(), calls=%async_computation.4 | async-start | bytes 2654208 | tf_op jit(solution)/shard_map/all_gather | solution.py:165
  8.0 57.6 %copy-start.5 = (f32[1,1,1536]{2,1,0:T(1,128)S(1)}, f32[1,1,1536]{2,1,0:T(1,128)}, u32[]{:S(2)}) copy-start(f32[1,1,1536]{2,1,0:T(1,128)} %param.22) | copy-start | bytes 18436
  9.5 40.7 %all-to-all-start = ((bf16[4,32,768]{2,1,0:T(8,128)(2,1)}), bf16[4,32,768]{2,1,0:T(8,128)(2,1)S(1)}, u32[]{:S(2)}, u32[]{:S(2)}) async-start(bf16[4,32,768]{2,1,0:T(8,128)(2,1)} %broadcast_in_dim.7), calls=%async_computation | async-start | bytes 393216 | tf_op jit(solution)/shard_map/all_to_all | solution.py:139
  50.1 0.7 copy-start.3
  56.1 12.8 %all-to-all-start.1 = ((f32[4,32,792]{2,1,0:T(8,128)}), f32[4,32,792]{2,1,0:T(8,128)S(1)}, u32[]{:S(2)}, u32[]{:S(2)}) async-start(f32[4,32,792]{2,1,0:T(8,128)} %bitcast.23), calls=%async_computation.1 | async-start | bytes 917504 | tf_op jit(solution)/shard_map/all_to_all | solution.py:154
  61.1 31.0 %collective-permute-start = (bf16[1536,384]{1,0:T(8,128)(2,1)S(1)}, bf16[1536,384]{1,0:T(8,128)(2,1)}, u32[]{:S(2)}, u32[]{:S(2)}) collective-permute-start(bf16[1536,384]{1,0:T(8,128)(2,1)S(1)} %copy-done.1), channel_id=1, source_target_pairs={{0,32},{32,0},{1,33},{33,1},{2,34},{34,2},{3,35},{35,3},{4,36},{36... | collective-permute-start | bytes 3538952 | tf_op jit(solution)/shard_map/ppermute | solution.py:172
  63.1 29.1 %collective-permute-start.1 = (bf16[384,1536]{1,0:T(8,128)(2,1)S(1)}, bf16[384,1536]{1,0:T(8,128)(2,1)}, u32[]{:S(2)}, u32[]{:S(2)}) collective-permute-start(bf16[384,1536]{1,0:T(8,128)(2,1)S(1)} %copy-done.2), channel_id=1, source_target_pairs={{0,32},{32,0},{1,33},{33,1},{2,34},{34,2},{3,35},{35,3},{4,36},{36... | collective-permute-start | bytes 3538952 | tf_op jit(solution)/shard_map/ppermute | solution.py:173
  92.1 9.4 %copy-start.9 = (f32[1,1,1536]{2,1,0:T(1,128)S(1)}, f32[1,1,1536]{2,1,0:T(1,128)}, u32[]{:S(2)}) copy-start(f32[1,1,1536]{2,1,0:T(1,128)} %param.23) | copy-start | bytes 18436
  92.1 9.4 %copy-start.10 = (f32[1,1,1536]{2,1,0:T(1,128)S(1)}, f32[1,1,1536]{2,1,0:T(1,128)}, u32[]{:S(2)}) copy-start(f32[1,1,1536]{2,1,0:T(1,128)} %param.24) | copy-start | bytes 18436
  92.1 9.5 %copy-start.6 = (f32[1,1,1536]{2,1,0:T(1,128)S(1)}, f32[1,1,1536]{2,1,0:T(1,128)}, u32[]{:S(2)}) copy-start(f32[1,1,1536]{2,1,0:T(1,128)} %param.25) | copy-start | bytes 18436
  95.6 30.9 %copy-start.4 = (f32[1,32,32]{2,1,0:T(8,128)S(1)}, f32[1,32,32]{2,1,0:T(8,128)}, u32[]{:S(2)}) copy-start(f32[1,32,32]{2,1,0:T(8,128)} %param.30) | copy-start | bytes 12292
  95.6 12.4 %all-to-all-start.2 = ((bf16[4,32,1536]{2,1,0:T(8,128)(2,1)}), bf16[4,32,1536]{2,1,0:T(8,128)(2,1)S(1)}, u32[]{:S(2)}, u32[]{:S(2)}) async-start(bf16[4,32,1536]{2,1,0:T(8,128)(2,1)} %bitcast.8), calls=%async_computation.2 | async-start | bytes 786432 | tf_op jit(solution)/shard_map/all_to_all | solution.py:180
  108.7 9.5 %collective-permute-start.2 = (f32[32,64]{1,0:T(8,128)S(1)}, f32[32,64]{1,0:T(8,128)S(1)}, u32[]{:S(2)}, u32[]{:S(2)}) collective-permute-start(f32[32,64]{1,0:T(8,128)S(1)} %fusion.2), channel_id=1, source_target_pairs={{0,256},{256,0},{1,257},{257,1},{2,258},{258,2},{3,259},{259,3},{4... | collective-permute-start | bytes 24584 | tf_op jit(solution)/shard_map/ppermute | solution.py:24
  120.8 15.3 %all-to-all-start.3 = ((f32[32,1,2]{2,1,0:T(1,128)}), f32[32,1,2]{2,1,0:T(1,128)S(1)}, u32[]{:S(2)}, u32[]{:S(2)}) async-start(f32[32,1,2]{2,1,0:T(1,128)} %broadcast_in_dim.8), calls=%async_computation.3 | async-start | bytes 32768 | tf_op jit(solution)/shard_map/all_to_all | solution.py:194
Sparse Core Ops, SparseCore 0:
  10.1 44.5 all-gather.2

commit v11 on v10

--- a/solution.py
+++ b/solution.py
@@ -157,7 +157,9 @@
     got_sum = got[:, :, width + HEADS :]
     row_max = jnp.max(got_max, axis=0)
     rescale = jnp.exp(got_max - row_max[None])
-    numerator = jnp.sum(rescale[:, :, :, None] * got_out, axis=0)
+    numerator = jnp.einsum(
+        "iqh,iqhd->qhd", rescale, got_out, precision=lax.Precision.HIGHEST
+    )
     denominator = jnp.sum(rescale * got_sum, axis=0)
     attended = (numerator / denominator[:, :, None]).reshape(img_dev, width).astype(jnp.bfloat16)
     projected = jnp.dot(

time: 146 us -> 148 us (1.014)
  matrix products: 2.8 us -> 7.16 us
  local copies, waits for them, and re-layouts: 8.3 us -> 5.35 us
    dot_general x0 -> x1, matrix products: none -> 4.36 us  [per_device(): jnp.einsum('iqh,iqhd->qhd', rescale, got_out, precision=lax.Precision.HIG...]
    mul x2 -> x0, local copies, waits for them, and re-layouts: 2.86 us -> none  [per_device(): numerator = jnp.sum(rescale[:, :, :, None] * got_out, axis=0)]
    div x2 -> x0, local copies, waits for them, and re-layouts: 2.52 us -> none  [per_device(): numerator / denominator[:, :, None]]
  transfers between devices with their start and end apart: 8 -> 8, of which waited for: 4 -> 4; matrix products, arithmetic and copies ran while one was open for 8% -> 9% of each run, Pallas kernels for 4% -> 4%
where the time goes in v11:
time: 148 us; the launch traced here: 147 us
  blocking collectives  49.9 us (34%)
  starting transfers between devices  29 us (20%)
  waiting for transfers between devices  24.3 us (16%)
  between operations  17.4 us (12%)
  Pallas kernels  8.79 us (6%)
  matrix products  7.16 us (5%)
  local copies, waits for them, and re-layouts  5.35 us (4%)
  other arithmetic  4.96 us (3%)
    all_gather x1, blocking collectives, per_device(): piece = lax.all_gather(key_value[:, 0, 0], 'sz', axis=1, tiled=True)  35.1 us
    all_gather x1, blocking collectives, per_device(): line_in = lax.all_gather(mlp_in, 'ry', axis=0, tiled=True)  14.8 us
    all_to_all x1, waiting for transfers between devices, per_device(): lax.all_to_all(jnp.broadcast_to(partials[None], (n_seq, 2)), ('sz', 'sx')...  8.88 us
    all_to_all x1, waiting for transfers between devices, per_device(): lax.all_to_all(mlp_parts, 'ry', 0, 0, tiled=True).astype(jnp.float32)  6.41 us
    all_to_all x1, starting transfers between devices, per_device(): lax.all_to_all(mlp_parts, 'ry', 0, 0, tiled=True).astype(jnp.float32)  5.87 us
    all_to_all x1, starting transfers between devices, per_device(): lax.all_to_all(jnp.broadcast_to(partials[None], (n_seq, 2)), ('sz', 'sx')...  5.67 us
    pallas_call x1, Pallas kernels, attention_partials(): pl.pallas_call(attention_partials_kernel, out_shape=jax.ShapeDtypeStruct(...  5.29 us
    ppermute x1, waiting for transfers between devices, swapped(): return lax.ppermute(block, axis, route)  5.07 us
  transfers between devices with their start and end apart: 8, of which 4 were waited for; matrix products, arithmetic and copies ran while one was open for 9% of the time, Pallas kernels for 4%

profile of v11, /device:TPU:56, one launch (start us, length us, event | category | flops | bytes accessed | tf_op | source)
XLA Modules:
  0.0 147.0 jit_solution(3670253748740486540)
XLA Ops:
  7.2 0.0 copy-start
  7.2 0.0 copy-start.1
  7.2 0.0 copy-start.2
  7.2 0.0 copy-start.8
  7.2 0.0 copy-start.9
  7.2 0.0 all-gather.3.cloned.1.call-start
  7.3 0.7 all-gather.3.cloned.1.call-update
  8.0 0.0 copy-start.6
  8.0 1.5 %broadcast_in_dim.7 = bf16[4,32,768]{2,1,0:T(8,128)(2,1)} broadcast(bf16[32,768]{1,0:T(8,128)(2,1)} %bitcast.34), dimensions={1,2} | broadcast | bytes 245760 | tf_op jit(solution)/shard_map/broadcast_in_dim | solution.py:140
  9.5 4.3 %all-to-all-start = ((bf16[4,32,768]{2,1,0:T(8,128)(2,1)}), bf16[4,32,768]{2,1,0:T(8,128)(2,1)S(1)}, u32[]{:S(2)}, u32[]{:S(2)}) async-start(bf16[4,32,768]{2,1,0:T(8,128)(2,1)} %broadcast_in_dim.7), calls=%async_computation | async-start | bytes 393216 | tf_op jit(solution)/shard_map/all_to_all | solution.py:139
  13.8 35.1 %all-gather = bf16[2,1,1,320,768]{4,3,0,2,1:T(8,128)(2,1)} all-gather(bf16[2,1,1,40,768]{4,3,0,2,1:T(8,128)(2,1)} %bitcast.33), channel_id=2, replica_groups=mesh['cfg'=2,'ry'=4,'rc'=2,'sz'=8,'sx'=4] {'sz'}, dimensions={3}, use_global_device_ids=true | all-gather | bytes 1105920 | tf_op jit(solution)/shard_map/all_gather | solution.py:142
  49.6 0.6 or_convert_fusion.mask_ref
  50.1 0.0 all-to-all-done
  50.1 0.0 copy-start.3
  50.2 0.7 copy-done.3
  50.8 5.3 %shard_map.175 = f32[128,792]{1,0:T(8,128)} custom-call(bf16[128,768]{1,0:T(8,128)(2,1)} %bitcast.32, bf16[2,320,768]{2,1,0:T(8,128)(2,1)} %bitcast.30, f32[1,320]{1,0:T(1,128)} %or_convert_fusion.mask_ref), custom_call_target="tpu_custom_call" | custom-call | flops 251658240 | bytes 1585152 | tf_op jit(solution)/shard_map/pallas_call | solution.py:62
  56.1 5.0 %all-to-all-start.1 = ((f32[4,32,792]{2,1,0:T(8,128)}), f32[4,32,792]{2,1,0:T(8,128)S(1)}, u32[]{:S(2)}, u32[]{:S(2)}) async-start(f32[4,32,792]{2,1,0:T(8,128)} %bitcast.31), calls=%async_computation.1 | async-start | bytes 917504 | tf_op jit(solution)/shard_map/all_to_all | solution.py:154
  61.1 0.0 copy-done.1
  61.1 1.9 %collective-permute-start = (bf16[1536,384]{1,0:T(8,128)(2,1)S(1)}, bf16[1536,384]{1,0:T(8,128)(2,1)}, u32[]{:S(2)}, u32[]{:S(2)}) collective-permute-start(bf16[1536,384]{1,0:T(8,128)(2,1)S(1)} %copy-done.1), channel_id=1, source_target_pairs={{0,32},{32,0},{1,33},{33,1},{2,34},{34,2},{3,35},{35,3},{4,36},{36... | collective-permute-start | bytes 3538952 | tf_op jit(solution)/shard_map/ppermute | solution.py:174
  63.1 0.0 copy-done.2
  63.1 2.4 %collective-permute-start.1 = (bf16[384,1536]{1,0:T(8,128)(2,1)S(1)}, bf16[384,1536]{1,0:T(8,128)(2,1)}, u32[]{:S(2)}, u32[]{:S(2)}) collective-permute-start(bf16[384,1536]{1,0:T(8,128)(2,1)S(1)} %copy-done.2), channel_id=1, source_target_pairs={{0,32},{32,0},{1,33},{33,1},{2,34},{34,2},{3,35},{35,3},{4,36},{36... | collective-permute-start | bytes 3538952 | tf_op jit(solution)/shard_map/ppermute | solution.py:175
  65.5 0.0 copy-done.8
  65.5 0.0 copy-done.9
  65.6 0.0 copy-done.6
  65.6 3.3 %all-to-all-done.1 = f32[4,32,792]{2,1,0:T(8,128)S(1)} async-done(((f32[4,32,792]{2,1,0:T(8,128)}), f32[4,32,792]{2,1,0:T(8,128)S(1)}, u32[]{:S(2)}, u32[]{:S(2)}) %all-to-all-start.1) | async-done | bytes 405536 | tf_op jit(solution)/shard_map/all_to_all | solution.py:154
  68.9 0.0 copy-start.4
  68.9 0.1 fusion.9
  69.0 1.0 copy.23
  70.0 1.3 reshape.159
  71.3 4.4 %fusion.1 = f32[32,12,1,64]{3,2,1,0:T(1,128)S(1)} fusion(f32[4,32,12,1]{0,3,2,1:T(1,128)} %copy.23, f32[4,32,12,64]{3,2,1,0:T(8,128)} %reshape.159), kind=kOutput, calls=%fused_computation.3 | convolution fusion | flops 1179648 | bytes 497664 | tf_op jit(solution)/shard_map/iqh,iqhd->qhd/dot_general | solution.py:160
  75.6 0.1 fusion.3
  75.8 0.1 convert_element_type.35
  75.9 0.0 all-gather.3.cloned.1.call-done
  76.0 0.0 copy-done.4
  76.0 2.6 %fusion.16 = (f32[32]{0:T(128)S(1)}, f32[32,1536]{1,0:T(8,128)S(1)}) fusion(bf16[32,768]{1,0:T(8,128)(2,1)S(1)} %convert_element_type.35, bf16[768,1536]{0,1:T(8,128)(2,1)} %all-gather.3.cloned.1.call-done, f32[1536]{0:T(1024)S(1)} %reduce.2, bf16[1,1,32,1536]{3,2,1,0:T(8,128)(2,1)S(1)} %copy-done.4), kind=kOutput, calls=%fused_computation.46 | convolution fusion | flops 75694048 | bytes 2709632 | tf_op jit(solution)/shard_map/dot_general | solution.py:165
  78.5 0.2 multiply_reduce_fusion.1
  78.8 0.1 add_convert_fusion.1
  78.9 14.8 %all_gather.11.x_ref = bf16[128,1536]{1,0:T(8,128)(2,1)S(1)} all-gather(bf16[32,1536]{1,0:T(8,128)(2,1)S(1)} %add_convert_fusion.1), channel_id=1, replica_groups=mesh['cfg'=2,'ry'=4,'rc'=2,'sz'=8,'sx'=4] {'ry'}, dimensions={0}, use_global_device_ids=true | all-gather | bytes 491520 | tf_op jit(solution)/shard_map/all_gather | solution.py:176
  93.6 0.0 copy-start.10
  93.6 0.0 copy-start.11
  93.6 0.0 collective-permute-done.up_b_ref
  93.7 0.0 collective-permute-done.1.down_b_ref
  93.7 3.5 %shard_map.176 = bf16[128,1536]{1,0:T(8,128)(2,1)} custom-call(bf16[128,1536]{1,0:T(8,128)(2,1)S(1)} %all_gather.11.x_ref, bf16[1536,384]{1,0:T(8,128)(2,1)S(1)} %copy-done.1, bf16[1536,384]{1,0:T(8,128)(2,1)} %collective-permute-done.up_b_ref, bf16[384,1536]{1,0:T(8,128)(2,1)S(1)} %copy-done.2, bf16[384,1536]{1,0:T(8,128)(2,1)} %collective-permute-done.1.down_b_ref), custom_call_target="tpu_custom_call" | custom-call | flops 603979776 | bytes 5505024 | tf_op jit(solution)/shard_map/pallas_call | solution.py:91
  97.2 5.9 %all-to-all-start.2 = ((bf16[4,32,1536]{2,1,0:T(8,128)(2,1)}), bf16[4,32,1536]{2,1,0:T(8,128)(2,1)S(1)}, u32[]{:S(2)}, u32[]{:S(2)}) async-start(bf16[4,32,1536]{2,1,0:T(8,128)(2,1)} %bitcast.10), calls=%async_computation.2 | async-start | bytes 786432 | tf_op jit(solution)/shard_map/all_to_all | solution.py:182
  103.0 0.0 copy-done.10
  103.1 0.0 copy-done.11
  103.1 0.0 copy-done.7
  103.1 6.4 %all-to-all-done.2 = bf16[4,32,1536]{2,1,0:T(8,128)(2,1)S(1)} async-done(((bf16[4,32,1536]{2,1,0:T(8,128)(2,1)}), bf16[4,32,1536]{2,1,0:T(8,128)(2,1)S(1)}, u32[]{:S(2)}, u32[]{:S(2)}) %all-to-all-start.2) | async-done | bytes 393248 | tf_op jit(solution)/shard_map/all_to_all | solution.py:182
  109.6 0.1 convert_reduce_fusion
  109.6 0.1 fusion.15
  109.8 0.2 multiply_reduce_fusion
  110.0 0.0 copy-done
  110.0 0.2 fusion.4
  110.2 3.8 %collective-permute-start.2 = (f32[32,64]{1,0:T(8,128)S(1)}, f32[32,64]{1,0:T(8,128)S(1)}, u32[]{:S(2)}, u32[]{:S(2)}) collective-permute-start(f32[32,64]{1,0:T(8,128)S(1)} %fusion.4), channel_id=1, source_target_pairs={{0,256},{256,0},{1,257},{257,1},{2,258},{258,2},{3,259},{259,3},{4... | collective-permute-start | bytes 24584 | tf_op jit(solution)/shard_map/ppermute | solution.py:24
  114.7 5.1 %collective-permute-done.2 = f32[32,64]{1,0:T(8,128)S(1)} collective-permute-done((f32[32,64]{1,0:T(8,128)S(1)}, f32[32,64]{1,0:T(8,128)S(1)}, u32[]{:S(2)}, u32[]{:S(2)}) %collective-permute-start.2) | collective-permute-done | bytes 8224 | tf_op jit(solution)/shard_map/ppermute | solution.py:24
  119.8 0.6 multiply_reduce_fusion.2
  120.4 1.4 pad_maximum_fusion
  121.7 0.6 broadcast_in_dim.8
  122.3 5.7 %all-to-all-start.3 = ((f32[32,1,2]{2,1,0:T(1,128)}), f32[32,1,2]{2,1,0:T(1,128)S(1)}, u32[]{:S(2)}, u32[]{:S(2)}) async-start(f32[32,1,2]{2,1,0:T(1,128)} %broadcast_in_dim.8), calls=%async_computation.3 | async-start | bytes 32768 | tf_op jit(solution)/shard_map/all_to_all | solution.py:196
  128.0 0.0 copy-done.5
  128.0 0.7 bitcast_add_fusion
  128.7 8.9 %all-to-all-done.3 = f32[32,1,2]{2,1,0:T(1,128)S(1)} async-done(((f32[32,1,2]{2,1,0:T(1,128)}), f32[32,1,2]{2,1,0:T(1,128)S(1)}, u32[]{:S(2)}, u32[]{:S(2)}) %all-to-all-start.3) | async-done | bytes 288 | tf_op jit(solution)/shard_map/all_to_all | solution.py:196
  137.6 0.1 copy.22
  137.7 0.6 slice_reduce_fusion.1
  (14 shorter events, 0.2 us)
Async XLA Ops:
  7.2 102.8 %copy-start = (bf16[1536,64]{0,1:T(8,128)(2,1)S(1)}, bf16[1536,64]{0,1:T(8,128)(2,1)}, u32[]{:S(2)}) copy-start(bf16[1536,64]{0,1:T(8,128)(2,1)} %param.29) | copy-start | bytes 589828
  7.2 54.0 %copy-start.1 = (bf16[1536,384]{1,0:T(8,128)(2,1)S(1)}, bf16[1536,384]{1,0:T(8,128)(2,1)}, u32[]{:S(2)}) copy-start(bf16[1536,384]{1,0:T(8,128)(2,1)} %up_a_ref.1) | copy-start | bytes 3538948
  7.2 55.9 %copy-start.2 = (bf16[384,1536]{1,0:T(8,128)(2,1)S(1)}, bf16[384,1536]{1,0:T(8,128)(2,1)}, u32[]{:S(2)}) copy-start(bf16[384,1536]{1,0:T(8,128)(2,1)} %down_a_ref.1) | copy-start | bytes 3538948
  7.2 58.3 %copy-start.8 = (f32[1,1,1536]{2,1,0:T(1,128)S(1)}, f32[1,1,1536]{2,1,0:T(1,128)}, u32[]{:S(2)}) copy-start(f32[1,1,1536]{2,1,0:T(1,128)} %param.20) | copy-start | bytes 18436
  7.2 58.3 %copy-start.9 = (f32[1,1,1536]{2,1,0:T(1,128)S(1)}, f32[1,1,1536]{2,1,0:T(1,128)}, u32[]{:S(2)}) copy-start(f32[1,1,1536]{2,1,0:T(1,128)} %param.21) | copy-start | bytes 18436
  7.2 68.7 %all-gather.3.cloned.1.call-start = ((), (), s32[]{:S(2)}) async-start(), calls=%async_computation.4 | async-start | bytes 2654208 | tf_op jit(solution)/shard_map/all_gather | solution.py:167
  8.0 57.6 %copy-start.6 = (f32[1,1,1536]{2,1,0:T(1,128)S(1)}, f32[1,1,1536]{2,1,0:T(1,128)}, u32[]{:S(2)}) copy-start(f32[1,1,1536]{2,1,0:T(1,128)} %param.22) | copy-start | bytes 18436
  9.5 40.7 %all-to-all-start = ((bf16[4,32,768]{2,1,0:T(8,128)(2,1)}), bf16[4,32,768]{2,1,0:T(8,128)(2,1)S(1)}, u32[]{:S(2)}, u32[]{:S(2)}) async-start(bf16[4,32,768]{2,1,0:T(8,128)(2,1)} %broadcast_in_dim.7), calls=%async_computation | async-start | bytes 393216 | tf_op jit(solution)/shard_map/all_to_all | solution.py:139
  50.1 0.7 copy-start.3
  56.1 12.8 %all-to-all-start.1 = ((f32[4,32,792]{2,1,0:T(8,128)}), f32[4,32,792]{2,1,0:T(8,128)S(1)}, u32[]{:S(2)}, u32[]{:S(2)}) async-start(f32[4,32,792]{2,1,0:T(8,128)} %bitcast.31), calls=%async_computation.1 | async-start | bytes 917504 | tf_op jit(solution)/shard_map/all_to_all | solution.py:154
  61.1 32.5 %collective-permute-start = (bf16[1536,384]{1,0:T(8,128)(2,1)S(1)}, bf16[1536,384]{1,0:T(8,128)(2,1)}, u32[]{:S(2)}, u32[]{:S(2)}) collective-permute-start(bf16[1536,384]{1,0:T(8,128)(2,1)S(1)} %copy-done.1), channel_id=1, source_target_pairs={{0,32},{32,0},{1,33},{33,1},{2,34},{34,2},{3,35},{35,3},{4,36},{36... | collective-permute-start | bytes 3538952 | tf_op jit(solution)/shard_map/ppermute | solution.py:174
  63.1 30.6 %collective-permute-start.1 = (bf16[384,1536]{1,0:T(8,128)(2,1)S(1)}, bf16[384,1536]{1,0:T(8,128)(2,1)}, u32[]{:S(2)}, u32[]{:S(2)}) collective-permute-start(bf16[384,1536]{1,0:T(8,128)(2,1)S(1)} %copy-done.2), channel_id=1, source_target_pairs={{0,32},{32,0},{1,33},{33,1},{2,34},{34,2},{3,35},{35,3},{4,36},{36... | collective-permute-start | bytes 3538952 | tf_op jit(solution)/shard_map/ppermute | solution.py:175
  68.9 7.1 %copy-start.4 = (bf16[1,1,32,1536]{3,2,1,0:T(8,128)(2,1)S(1)}, bf16[1,1,32,1536]{3,2,1,0:T(8,128)(2,1)}, u32[]{:S(2)}) copy-start(bf16[1,1,32,1536]{3,2,1,0:T(8,128)(2,1)} %param.18) | copy-start | bytes 294916
  93.6 9.4 %copy-start.10 = (f32[1,1,1536]{2,1,0:T(1,128)S(1)}, f32[1,1,1536]{2,1,0:T(1,128)}, u32[]{:S(2)}) copy-start(f32[1,1,1536]{2,1,0:T(1,128)} %param.23) | copy-start | bytes 18436
  93.6 9.4 %copy-start.11 = (f32[1,1,1536]{2,1,0:T(1,128)S(1)}, f32[1,1,1536]{2,1,0:T(1,128)}, u32[]{:S(2)}) copy-start(f32[1,1,1536]{2,1,0:T(1,128)} %param.24) | copy-start | bytes 18436
  93.6 9.5 %copy-start.7 = (f32[1,1,1536]{2,1,0:T(1,128)S(1)}, f32[1,1,1536]{2,1,0:T(1,128)}, u32[]{:S(2)}) copy-start(f32[1,1,1536]{2,1,0:T(1,128)} %param.25) | copy-start | bytes 18436
  97.2 30.9 %copy-start.5 = (f32[1,32,32]{2,1,0:T(8,128)S(1)}, f32[1,32,32]{2,1,0:T(8,128)}, u32[]{:S(2)}) copy-start(f32[1,32,32]{2,1,0:T(8,128)} %param.30) | copy-start | bytes 12292
  97.2 12.4 %all-to-all-start.2 = ((bf16[4,32,1536]{2,1,0:T(8,128)(2,1)}), bf16[4,32,1536]{2,1,0:T(8,128)(2,1)S(1)}, u32[]{:S(2)}, u32[]{:S(2)}) async-start(bf16[4,32,1536]{2,1,0:T(8,128)(2,1)} %bitcast.10), calls=%async_computation.2 | async-start | bytes 786432 | tf_op jit(solution)/shard_map/all_to_all | solution.py:182
  110.2 9.5 %collective-permute-start.2 = (f32[32,64]{1,0:T(8,128)S(1)}, f32[32,64]{1,0:T(8,128)S(1)}, u32[]{:S(2)}, u32[]{:S(2)}) collective-permute-start(f32[32,64]{1,0:T(8,128)S(1)} %fusion.4), channel_id=1, source_target_pairs={{0,256},{256,0},{1,257},{257,1},{2,258},{258,2},{3,259},{259,3},{4... | collective-permute-start | bytes 24584 | tf_op jit(solution)/shard_map/ppermute | solution.py:24
  122.3 15.3 %all-to-all-start.3 = ((f32[32,1,2]{2,1,0:T(1,128)}), f32[32,1,2]{2,1,0:T(1,128)S(1)}, u32[]{:S(2)}, u32[]{:S(2)}) async-start(f32[32,1,2]{2,1,0:T(1,128)} %broadcast_in_dim.8), calls=%async_computation.3 | async-start | bytes 32768 | tf_op jit(solution)/shard_map/all_to_all | solution.py:196
Sparse Core Ops, SparseCore 0:
  10.1 44.5 all-gather.2

commit v12 on v7

--- a/solution.py
+++ b/solution.py
@@ -106,10 +106,18 @@
     factor = HD ** (-0.5)
     n_x = lax.axis_size("sx")
     x_index = lax.axis_index("sx")
-    query_rows = lax.all_to_all(
-        jnp.broadcast_to(query[0, 0][None], (n_x,) + query.shape[2:]), "sx", 0, 0, tiled=True
-    ).reshape(n_x * img_dev, query.shape[3])
-    piece = lax.all_gather(key_value[:, 0, 0], "sz", axis=1, tiled=True)
+    n_z = lax.axis_size("sz")
+    kv_blocks = lax.all_to_all(
+        jnp.broadcast_to(key_value[:, 0, 0][None], (n_z,) + key_value[:, 0, 0].shape),
+        "sz",
+        0,
+        0,
+        tiled=True,
+    )
+    query_rows = lax.all_gather(query[0, 0], "sx", axis=0, tiled=True)
+    piece = jnp.swapaxes(kv_blocks, 0, 1).reshape(
+        2, n_z * rows_dev, key_value.shape[4]
+    )
     q_rows = query_rows.shape[0]
     piece_rows = piece.shape[1]
     positions = jnp.arange(piece_rows, dtype=jnp.int32)

time: 143 us -> 141 us (0.986)
  blocking collectives: 49.9 us -> 28.3 us
  waiting for transfers between devices: 24.3 us -> 39.3 us
  starting transfers between devices: 28.9 us -> 32 us
    all_gather x1, blocking collectives: 35.1 us -> 13.2 us  [per_device(): query_rows = lax.all_gather(query[0, 0], 'sx', axis=0, tiled=True)]
    all_to_all x1, waiting for transfers between devices: 0.01 us -> 12.9 us  [per_device(): lax.all_to_all(jnp.broadcast_to(key_value[:, 0, 0][None], (n_z,) + key_va...]
    all_to_all x1, starting transfers between devices: 4.29 us -> 10.4 us  [per_device(): lax.all_to_all(jnp.broadcast_to(key_value[:, 0, 0][None], (n_z,) + key_va...]
    all_to_all x1, starting transfers between devices: 5.66 us -> 3.85 us  [per_device(): lax.all_to_all(jnp.broadcast_to(partials[None], (n_seq, 2)), ('sz', 'sx')...]
  transfers between devices with their start and end apart: 8 -> 8, of which waited for: 4 -> 5; matrix products, arithmetic and copies ran while one was open for 6% -> 7% of each run, Pallas kernels for 4% -> 4%
where the time goes in v12:
time: 141 us; the launch traced here: 140 us
  waiting for transfers between devices  39.3 us (28%)
  starting transfers between devices  32 us (23%)
  blocking collectives  28.3 us (20%)
  between operations  17.4 us (12%)
  matrix products  7.88 us (6%)
  Pallas kernels  5.39 us (4%)
  other arithmetic  4.86 us (3%)
  local copies, waits for them, and re-layouts  4.8 us (3%)
    all_gather x1, blocking collectives, per_device(): line_in = lax.all_gather(mlp_in, 'ry', axis=0, tiled=True)  15.1 us
    all_gather x1, blocking collectives, per_device(): query_rows = lax.all_gather(query[0, 0], 'sx', axis=0, tiled=True)  13.2 us
    all_to_all x1, waiting for transfers between devices, per_device(): lax.all_to_all(jnp.broadcast_to(key_value[:, 0, 0][None], (n_z,) + key_va...  12.9 us
    all_to_all x1, starting transfers between devices, per_device(): lax.all_to_all(jnp.broadcast_to(key_value[:, 0, 0][None], (n_z,) + key_va...  10.4 us
    all_to_all x1, waiting for transfers between devices, per_device(): lax.all_to_all(jnp.broadcast_to(partials[None], (n_seq, 2)), ('sz', 'sx')...  8.88 us
    all_to_all x1, waiting for transfers between devices, per_device(): lax.all_to_all(mlp_parts, 'ry', 0, 0, tiled=True).astype(jnp.float32)  6.41 us
    all_to_all x1, starting transfers between devices, per_device(): lax.all_to_all(mlp_parts, 'ry', 0, 0, tiled=True).astype(jnp.float32)  6.14 us
    ppermute x1, waiting for transfers between devices, swapped(): return lax.ppermute(block, axis, route)  5.93 us
  transfers between devices with their start and end apart: 8, of which 5 were waited for; matrix products, arithmetic and copies ran while one was open for 7% of the time, Pallas kernels for 4%

profile of v12, /device:TPU:56, one launch (start us, length us, event | category | flops | bytes accessed | tf_op | source)
XLA Modules:
  0.0 140.0 jit_solution(9507960177655974866)
XLA Ops:
  7.2 0.0 copy-start
  7.2 0.0 all-gather.3.cloned.1.call-start
  7.2 0.7 all-gather.3.cloned.1.call-update
  7.9 1.9 %broadcast_in_dim.7 = bf16[8,2,40,768]{3,2,1,0:T(8,128)(2,1)} broadcast(bf16[2,40,768]{2,1,0:T(8,128)(2,1)} %bitcast.32), dimensions={1,2,3} | broadcast | bytes 1105920 | tf_op jit(solution)/shard_map/broadcast_in_dim | solution.py:111
  9.8 0.0 copy-start.3
  9.8 10.4 %all-to-all-start = ((bf16[8,2,40,768]{3,2,1,0:T(8,128)(2,1)}), bf16[8,2,40,768]{3,2,1,0:T(8,128)(2,1)S(1)}, u32[]{:S(2)}, u32[]{:S(2)}) async-start(bf16[8,2,40,768]{3,2,1,0:T(8,128)(2,1)} %broadcast_in_dim.7), calls=%async_computation | async-start | bytes 1966080 | tf_op jit(solution)/shard_map/all_to_all | solution.py:110
  20.9 0.0 copy-done.3
  20.9 13.2 %all-gather = bf16[1,1,128,768]{3,2,1,0:T(8,128)(2,1)} all-gather(bf16[1,1,32,768]{3,2,1,0:T(8,128)(2,1)S(1)} %copy-done.3), channel_id=2, replica_groups=mesh['cfg'=2,'ry'=4,'rc'=2,'sz'=8,'sx'=4] {'sx'}, dimensions={2}, use_global_device_ids=true | all-gather | bytes 245760 | tf_op jit(solution)/shard_map/all_gather | solution.py:117
  34.2 0.6 or_convert_fusion.mask_ref
  34.7 12.9 %all-to-all-done = bf16[8,2,40,768]{3,2,1,0:T(8,128)(2,1)S(1)} async-done(((bf16[8,2,40,768]{3,2,1,0:T(8,128)(2,1)}), bf16[8,2,40,768]{3,2,1,0:T(8,128)(2,1)S(1)}, u32[]{:S(2)}, u32[]{:S(2)}) %all-to-all-start) | async-done | bytes 983072 | tf_op jit(solution)/shard_map/all_to_all | solution.py:110
  47.6 1.0 copy.19
  48.6 0.0 copy-start.1
  48.6 0.0 copy-start.7
  48.6 0.0 copy-start.8
  48.6 5.4 %shard_map.175 = f32[128,792]{1,0:T(8,128)} custom-call(bf16[128,768]{1,0:T(8,128)(2,1)} %bitcast.31, bf16[2,320,768]{2,1,0:T(8,128)(2,1)} %bitcast.29, f32[1,320]{1,0:T(1,128)} %or_convert_fusion.mask_ref), custom_call_target="tpu_custom_call" | custom-call | flops 251658240 | bytes 1585152 | tf_op jit(solution)/shard_map/pallas_call | solution.py:62
  54.0 4.3 %all-to-all-start.1 = ((f32[4,32,792]{2,1,0:T(8,128)}), f32[4,32,792]{2,1,0:T(8,128)S(1)}, u32[]{:S(2)}, u32[]{:S(2)}) async-start(f32[4,32,792]{2,1,0:T(8,128)} %bitcast.30), calls=%async_computation.1 | async-start | bytes 917504 | tf_op jit(solution)/shard_map/all_to_all | solution.py:132
  58.3 0.0 copy-done.1
  58.3 1.9 %collective-permute-start = (bf16[1536,384]{1,0:T(8,128)(2,1)S(1)}, bf16[1536,384]{1,0:T(8,128)(2,1)}, u32[]{:S(2)}, u32[]{:S(2)}) collective-permute-start(bf16[1536,384]{1,0:T(8,128)(2,1)S(1)} %copy-done.1), channel_id=1, source_target_pairs={{0,32},{32,0},{1,33},{33,1},{2,34},{34,2},{3,35},{35,3},{4,36},{36... | collective-permute-start | bytes 3538952 | tf_op jit(solution)/shard_map/ppermute | solution.py:150
  60.2 2.4 %collective-permute-start.1 = (bf16[384,1536]{1,0:T(8,128)(2,1)}, bf16[384,1536]{1,0:T(8,128)(2,1)}, u32[]{:S(2)}, u32[]{:S(2)}) collective-permute-start(bf16[384,1536]{1,0:T(8,128)(2,1)} %param.28), channel_id=1, source_target_pairs={{0,32},{32,0},{1,33},{33,1},{2,34},{34,2},{3,35},{35,3},{4,36},{36... | collective-permute-start | bytes 3538952 | tf_op jit(solution)/shard_map/ppermute | solution.py:151
  62.7 0.0 copy-done.7
  62.7 0.0 copy-done.8
  62.7 0.0 copy-done.5
  62.8 4.5 %all-to-all-done.1 = f32[4,32,792]{2,1,0:T(8,128)S(1)} async-done(((f32[4,32,792]{2,1,0:T(8,128)}), f32[4,32,792]{2,1,0:T(8,128)S(1)}, u32[]{:S(2)}, u32[]{:S(2)}) %all-to-all-start.1) | async-done | bytes 405536 | tf_op jit(solution)/shard_map/all_to_all | solution.py:132
  67.3 0.1 fusion.35
  67.4 0.3 mul.150
  67.7 0.0 copy-start.2
  67.7 0.3 mul.151
  68.0 0.1 div.40
  68.1 0.1 div.41
  68.3 0.0 all-gather.3.cloned.1.call-done
  68.3 0.3 copy-done.2
  68.6 2.6 %fusion.49 = (f32[32]{0:T(128)S(1)}, f32[32,1536]{1,0:T(8,128)S(1)}) fusion(bf16[768,1536]{0,1:T(8,128)(2,1)} %all-gather.3.cloned.1.call-done, f32[32,768]{1,0:T(8,128)S(1)} %fusion.2, f32[32,768]{1,0:T(8,128)S(1)} %div.41, f32[1536]{0:T(1024)S(1)} %reduce.3, bf16[1,1,32,1536]{3,2,1,0:T(8,128)(2,1)S(1)} %copy-done.2), kind=kOutput, calls=%fused_computation.81 | convolution fusion | flops 75743200 | bytes 2857088 | tf_op jit(solution)/shard_map/dot_general | solution.py:141
  71.2 0.2 multiply_reduce_fusion.1
  71.4 0.1 add_convert_fusion.1
  71.5 15.1 %all_gather.11 = bf16[128,1536]{1,0:T(8,128)(2,1)S(1)} all-gather(bf16[32,1536]{1,0:T(8,128)(2,1)S(1)} %add_convert_fusion.1), channel_id=1, replica_groups=mesh['cfg'=2,'ry'=4,'rc'=2,'sz'=8,'sx'=4] {'ry'}, dimensions={0}, use_global_device_ids=true | all-gather | bytes 491520 | tf_op jit(solution)/shard_map/all_gather | solution.py:152
  86.6 2.0 %fusion.21 = f32[128,1536]{1,0:T(8,128)S(1)} fusion(bf16[384,1536]{1,0:T(8,128)(2,1)} %param.28, bf16[128,1536]{1,0:T(8,128)(2,1)S(1)} %all_gather.11, bf16[1536,384]{1,0:T(8,128)(2,1)S(1)} %copy-done.1), kind=kOutput, calls=%fused_computation.31 | convolution fusion | flops 302432256 | bytes 3538944 | tf_op jit(solution)/shard_map/dot_general | solution.py:161
  88.6 0.0 copy-start.9
  88.6 0.0 copy-start.10
  88.6 0.0 copy-start.6
  88.6 0.0 collective-permute-done
  88.6 0.0 collective-permute-done.1
  88.7 3.1 %fusion = bf16[128,1536]{1,0:T(8,128)(2,1)} fusion(f32[128,1536]{1,0:T(8,128)S(1)} %fusion.21, bf16[384,1536]{1,0:T(8,128)(2,1)} %collective-permute-done.1, bf16[128,1536]{1,0:T(8,128)(2,1)S(1)} %all_gather.11, bf16[1536,384]{1,0:T(8,128)(2,1)} %collective-permute-done), kind=kOutput, calls=%fused_computation.1 | convolution fusion | flops 302825472 | bytes 3932160 | tf_op jit(solution)/shard_map/dot_general | solution.py:162
  91.7 6.1 %all-to-all-start.2 = ((bf16[4,32,1536]{2,1,0:T(8,128)(2,1)}), bf16[4,32,1536]{2,1,0:T(8,128)(2,1)S(1)}, u32[]{:S(2)}, u32[]{:S(2)}) async-start(bf16[4,32,1536]{2,1,0:T(8,128)(2,1)} %bitcast.8), calls=%async_computation.2 | async-start | bytes 786432 | tf_op jit(solution)/shard_map/all_to_all | solution.py:168
  97.9 0.0 copy-done.9
  97.9 0.0 copy-start.4
  97.9 0.0 copy-done.10
  97.9 0.0 copy-done.6
  98.0 6.4 %all-to-all-done.2 = bf16[4,32,1536]{2,1,0:T(8,128)(2,1)S(1)} async-done(((bf16[4,32,1536]{2,1,0:T(8,128)(2,1)}), bf16[4,32,1536]{2,1,0:T(8,128)(2,1)S(1)}, u32[]{:S(2)}, u32[]{:S(2)}) %all-to-all-start.2) | async-done | bytes 393248 | tf_op jit(solution)/shard_map/all_to_all | solution.py:168
  104.4 0.1 convert_reduce_fusion
  104.5 0.1 fusion.48
  104.6 0.2 multiply_reduce_fusion
  104.8 0.0 copy-done
  104.8 0.2 fusion.19
  105.0 2.9 %collective-permute-start.2 = (f32[32,64]{1,0:T(8,128)S(1)}, f32[32,64]{1,0:T(8,128)S(1)}, u32[]{:S(2)}, u32[]{:S(2)}) collective-permute-start(f32[32,64]{1,0:T(8,128)S(1)} %fusion.19), channel_id=1, source_target_pairs={{0,256},{256,0},{1,257},{257,1},{2,258},{258,2},{3,259},{259,3},{4... | collective-permute-start | bytes 24584 | tf_op jit(solution)/shard_map/ppermute | solution.py:24
  108.7 5.9 %collective-permute-done.2 = f32[32,64]{1,0:T(8,128)S(1)} collective-permute-done((f32[32,64]{1,0:T(8,128)S(1)}, f32[32,64]{1,0:T(8,128)S(1)}, u32[]{:S(2)}, u32[]{:S(2)}) %collective-permute-start.2) | collective-permute-done | bytes 8224 | tf_op jit(solution)/shard_map/ppermute | solution.py:24
  114.6 0.6 multiply_reduce_fusion.2
  115.2 1.4 pad_maximum_fusion
  116.6 0.6 broadcast_in_dim.8
  117.2 3.9 %all-to-all-start.3 = ((f32[32,1,2]{2,1,0:T(1,128)}), f32[32,1,2]{2,1,0:T(1,128)S(1)}, u32[]{:S(2)}, u32[]{:S(2)}) async-start(f32[32,1,2]{2,1,0:T(1,128)} %broadcast_in_dim.8), calls=%async_computation.3 | async-start | bytes 32768 | tf_op jit(solution)/shard_map/all_to_all | solution.py:182
  121.0 0.0 copy-done.4
  121.0 0.7 bitcast_add_fusion
  121.7 8.9 %all-to-all-done.3 = f32[32,1,2]{2,1,0:T(1,128)S(1)} async-done(((f32[32,1,2]{2,1,0:T(1,128)}), f32[32,1,2]{2,1,0:T(1,128)S(1)}, u32[]{:S(2)}, u32[]{:S(2)}) %all-to-all-start.3) | async-done | bytes 288 | tf_op jit(solution)/shard_map/all_to_all | solution.py:182
  130.6 0.1 copy.20
  130.7 0.6 slice_reduce_fusion.1
  (13 shorter events, 0.2 us)
Async XLA Ops:
  7.2 97.6 %copy-start = (bf16[1536,64]{0,1:T(8,128)(2,1)S(1)}, bf16[1536,64]{0,1:T(8,128)(2,1)}, u32[]{:S(2)}) copy-start(bf16[1536,64]{0,1:T(8,128)(2,1)} %param.29) | copy-start | bytes 589828
  7.2 61.1 %all-gather.3.cloned.1.call-start = ((), (), s32[]{:S(2)}) async-start(), calls=%async_computation.4 | async-start | bytes 2654208 | tf_op jit(solution)/shard_map/all_gather | solution.py:143
  9.8 11.1 %copy-start.3 = (bf16[1,1,32,768]{3,2,1,0:T(8,128)(2,1)S(1)}, bf16[1,1,32,768]{3,2,1,0:T(8,128)(2,1)}, u32[]{:S(2)}) copy-start(bf16[1,1,32,768]{3,2,1,0:T(8,128)(2,1)} %param.16) | copy-start | bytes 147460
  9.8 37.8 %all-to-all-start = ((bf16[8,2,40,768]{3,2,1,0:T(8,128)(2,1)}), bf16[8,2,40,768]{3,2,1,0:T(8,128)(2,1)S(1)}, u32[]{:S(2)}, u32[]{:S(2)}) async-start(bf16[8,2,40,768]{3,2,1,0:T(8,128)(2,1)} %broadcast_in_dim.7), calls=%async_computation | async-start | bytes 1966080 | tf_op jit(solution)/shard_map/all_to_all | solution.py:110
  48.6 9.7 %copy-start.1 = (bf16[1536,384]{1,0:T(8,128)(2,1)S(1)}, bf16[1536,384]{1,0:T(8,128)(2,1)}, u32[]{:S(2)}) copy-start(bf16[1536,384]{1,0:T(8,128)(2,1)} %param.27) | copy-start | bytes 3538948
  48.6 14.0 %copy-start.7 = (f32[1,1,1536]{2,1,0:T(1,128)S(1)}, f32[1,1,1536]{2,1,0:T(1,128)}, u32[]{:S(2)}) copy-start(f32[1,1,1536]{2,1,0:T(1,128)} %param.20) | copy-start | bytes 18436
  48.6 14.1 %copy-start.8 = (f32[1,1,1536]{2,1,0:T(1,128)S(1)}, f32[1,1,1536]{2,1,0:T(1,128)}, u32[]{:S(2)}) copy-start(f32[1,1,1536]{2,1,0:T(1,128)} %param.21) | copy-start | bytes 18436
  48.6 14.1 %copy-start.5 = (f32[1,1,1536]{2,1,0:T(1,128)S(1)}, f32[1,1,1536]{2,1,0:T(1,128)}, u32[]{:S(2)}) copy-start(f32[1,1,1536]{2,1,0:T(1,128)} %param.22) | copy-start | bytes 18436
  54.0 13.2 %all-to-all-start.1 = ((f32[4,32,792]{2,1,0:T(8,128)}), f32[4,32,792]{2,1,0:T(8,128)S(1)}, u32[]{:S(2)}, u32[]{:S(2)}) async-start(f32[4,32,792]{2,1,0:T(8,128)} %bitcast.30), calls=%async_computation.1 | async-start | bytes 917504 | tf_op jit(solution)/shard_map/all_to_all | solution.py:132
  58.3 30.3 %collective-permute-start = (bf16[1536,384]{1,0:T(8,128)(2,1)S(1)}, bf16[1536,384]{1,0:T(8,128)(2,1)}, u32[]{:S(2)}, u32[]{:S(2)}) collective-permute-start(bf16[1536,384]{1,0:T(8,128)(2,1)S(1)} %copy-done.1), channel_id=1, source_target_pairs={{0,32},{32,0},{1,33},{33,1},{2,34},{34,2},{3,35},{35,3},{4,36},{36... | collective-permute-start | bytes 3538952 | tf_op jit(solution)/shard_map/ppermute | solution.py:150
  60.2 28.4 %collective-permute-start.1 = (bf16[384,1536]{1,0:T(8,128)(2,1)}, bf16[384,1536]{1,0:T(8,128)(2,1)}, u32[]{:S(2)}, u32[]{:S(2)}) collective-permute-start(bf16[384,1536]{1,0:T(8,128)(2,1)} %param.28), channel_id=1, source_target_pairs={{0,32},{32,0},{1,33},{33,1},{2,34},{34,2},{3,35},{35,3},{4,36},{36... | collective-permute-start | bytes 3538952 | tf_op jit(solution)/shard_map/ppermute | solution.py:151
  67.7 0.9 copy-start.2
  88.6 9.3 %copy-start.9 = (f32[1,1,1536]{2,1,0:T(1,128)S(1)}, f32[1,1,1536]{2,1,0:T(1,128)}, u32[]{:S(2)}) copy-start(f32[1,1,1536]{2,1,0:T(1,128)} %param.23) | copy-start | bytes 18436
  88.6 9.3 %copy-start.10 = (f32[1,1,1536]{2,1,0:T(1,128)S(1)}, f32[1,1,1536]{2,1,0:T(1,128)}, u32[]{:S(2)}) copy-start(f32[1,1,1536]{2,1,0:T(1,128)} %param.24) | copy-start | bytes 18436
  88.6 9.3 %copy-start.6 = (f32[1,1,1536]{2,1,0:T(1,128)S(1)}, f32[1,1,1536]{2,1,0:T(1,128)}, u32[]{:S(2)}) copy-start(f32[1,1,1536]{2,1,0:T(1,128)} %param.25) | copy-start | bytes 18436
  91.7 12.7 %all-to-all-start.2 = ((bf16[4,32,1536]{2,1,0:T(8,128)(2,1)}), bf16[4,32,1536]{2,1,0:T(8,128)(2,1)S(1)}, u32[]{:S(2)}, u32[]{:S(2)}) async-start(bf16[4,32,1536]{2,1,0:T(8,128)(2,1)} %bitcast.8), calls=%async_computation.2 | async-start | bytes 786432 | tf_op jit(solution)/shard_map/all_to_all | solution.py:168
  97.9 23.2 %copy-start.4 = (f32[1,32,32]{2,1,0:T(8,128)S(1)}, f32[1,32,32]{2,1,0:T(8,128)}, u32[]{:S(2)}) copy-start(f32[1,32,32]{2,1,0:T(8,128)} %param.30) | copy-start | bytes 12292
  105.0 9.5 %collective-permute-start.2 = (f32[32,64]{1,0:T(8,128)S(1)}, f32[32,64]{1,0:T(8,128)S(1)}, u32[]{:S(2)}, u32[]{:S(2)}) collective-permute-start(f32[32,64]{1,0:T(8,128)S(1)} %fusion.19), channel_id=1, source_target_pairs={{0,256},{256,0},{1,257},{257,1},{2,258},{258,2},{3,259},{259,3},{4... | collective-permute-start | bytes 24584 | tf_op jit(solution)/shard_map/ppermute | solution.py:24
  117.2 13.4 %all-to-all-start.3 = ((f32[32,1,2]{2,1,0:T(1,128)}), f32[32,1,2]{2,1,0:T(1,128)S(1)}, u32[]{:S(2)}, u32[]{:S(2)}) async-start(f32[32,1,2]{2,1,0:T(1,128)} %broadcast_in_dim.8), calls=%async_computation.3 | async-start | bytes 32768 | tf_op jit(solution)/shard_map/all_to_all | solution.py:182
Sparse Core Ops, SparseCore 0:
  10.1 44.8 all-gather.2

commit v13 on v12

--- a/solution.py
+++ b/solution.py
@@ -36,8 +36,8 @@
     for pair in range(HEADS // 2):
         cols = slice(pair * lanes, (pair + 1) * lanes)
         q2 = q_ref[:, cols]
-        k2 = kv_ref[0, :, cols]
-        v2 = kv_ref[1, :, cols]
+        k2 = jnp.concatenate([kv_ref[z, 0, :, cols] for z in range(kv_ref.shape[0])], axis=0)
+        v2 = jnp.concatenate([kv_ref[z, 1, :, cols] for z in range(kv_ref.shape[0])], axis=0)
         outs = []
         for half in (low, jnp.logical_not(low)):
             q_half = jnp.where(half, q2, jnp.zeros_like(q2))
@@ -65,8 +65,8 @@
         in_specs=[pl.BlockSpec(memory_space=pltpu.VMEM)] * 3,
         out_specs=pl.BlockSpec(memory_space=pltpu.VMEM),
         cost_estimate=pl.CostEstimate(
-            flops=8 * rows * kv.shape[1] * width,
-            transcendentals=2 * rows * kv.shape[1] * HEADS,
+            flops=8 * rows * kv.shape[0] * kv.shape[2] * width,
+            transcendentals=2 * rows * kv.shape[0] * kv.shape[2] * HEADS,
             bytes_accessed=q.size * 2 + kv.size * 2 + rows * (width + 2 * HEADS) * 4,
         ),
     )(q, kv, mask)
@@ -115,11 +115,8 @@
         tiled=True,
     )
     query_rows = lax.all_gather(query[0, 0], "sx", axis=0, tiled=True)
-    piece = jnp.swapaxes(kv_blocks, 0, 1).reshape(
-        2, n_z * rows_dev, key_value.shape[4]
-    )
     q_rows = query_rows.shape[0]
-    piece_rows = piece.shape[1]
+    piece_rows = n_z * rows_dev
     positions = jnp.arange(piece_rows, dtype=jnp.int32)
     within = positions % rows_dev
     source = (positions // rows_dev) * n_x + x_index
@@ -127,7 +124,7 @@
     usable = ((within < img_dev) | (text_slot < length)).astype(jnp.float32)[None, :]
     width = HEADS * HD
     packed = attention_partials(
-        query_rows, piece.reshape(2, piece_rows, width), usable
+        query_rows, kv_blocks, usable
     ).reshape(n_x, img_dev, width + 2 * HEADS)
     got = lax.all_to_all(packed, "sx", 0, 0, tiled=True)
     got_out = got[:, :, :width].reshape(n_x, img_dev, HEADS, HD)

time: 141 us -> 141 us (level)
  no operation moved by 1% of the time
where the time goes in v13:
time: 141 us; the launch traced here: 140 us
  waiting for transfers between devices  39.3 us (28%)
  starting transfers between devices  32.1 us (23%)
  blocking collectives  28.3 us (20%)
  between operations  17.4 us (12%)
  matrix products  7.87 us (6%)
  Pallas kernels  5.4 us (4%)
  other arithmetic  4.86 us (3%)
  local copies, waits for them, and re-layouts  4.73 us (3%)
    all_gather x1, blocking collectives, per_device(): line_in = lax.all_gather(mlp_in, 'ry', axis=0, tiled=True)  15.1 us
    all_gather x1, blocking collectives, per_device(): query_rows = lax.all_gather(query[0, 0], 'sx', axis=0, tiled=True)  13.2 us
    all_to_all x1, waiting for transfers between devices, per_device(): lax.all_to_all(jnp.broadcast_to(key_value[:, 0, 0][None], (n_z,) + key_va...  12.9 us
    all_to_all x1, starting transfers between devices, per_device(): lax.all_to_all(jnp.broadcast_to(key_value[:, 0, 0][None], (n_z,) + key_va...  10.4 us
    all_to_all x1, waiting for transfers between devices, per_device(): lax.all_to_all(jnp.broadcast_to(partials[None], (n_seq, 2)), ('sz', 'sx')...  8.88 us
    all_to_all x1, waiting for transfers between devices, per_device(): lax.all_to_all(mlp_parts, 'ry', 0, 0, tiled=True).astype(jnp.float32)  6.41 us
    all_to_all x1, starting transfers between devices, per_device(): lax.all_to_all(mlp_parts, 'ry', 0, 0, tiled=True).astype(jnp.float32)  6.15 us
    ppermute x1, waiting for transfers between devices, swapped(): return lax.ppermute(block, axis, route)  5.92 us
  transfers between devices with their start and end apart: 8, of which 5 were waited for; matrix products, arithmetic and copies ran while one was open for 7% of the time, Pallas kernels for 4%

profile of v13, /device:TPU:56, one launch (start us, length us, event | category | flops | bytes accessed | tf_op | source)
XLA Modules:
  0.0 139.9 jit_solution(3712323807412502256)
XLA Ops:
  7.2 0.0 copy-start
  7.2 0.0 all-gather.3.cloned.1.call-start
  7.2 0.7 all-gather.3.cloned.1.call-update
  7.9 1.9 %broadcast_in_dim.7 = bf16[8,2,40,768]{3,2,1,0:T(8,128)(2,1)} broadcast(bf16[2,40,768]{2,1,0:T(8,128)(2,1)} %bitcast.28), dimensions={1,2,3} | broadcast | bytes 1105920 | tf_op jit(solution)/shard_map/broadcast_in_dim | solution.py:111
  9.8 0.0 copy-start.4
  9.8 10.4 %all-to-all-start = ((bf16[8,2,40,768]{3,2,1,0:T(8,128)(2,1)}), bf16[8,2,40,768]{3,2,1,0:T(8,128)(2,1)S(1)}, u32[]{:S(2)}, u32[]{:S(2)}) async-start(bf16[8,2,40,768]{3,2,1,0:T(8,128)(2,1)} %broadcast_in_dim.7), calls=%async_computation | async-start | bytes 1966080 | tf_op jit(solution)/shard_map/all_to_all | solution.py:110
  20.9 0.0 copy-done.4
  20.9 13.2 %all-gather = bf16[1,1,128,768]{3,2,1,0:T(8,128)(2,1)} all-gather(bf16[1,1,32,768]{3,2,1,0:T(8,128)(2,1)S(1)} %copy-done.4), channel_id=2, replica_groups=mesh['cfg'=2,'ry'=4,'rc'=2,'sz'=8,'sx'=4] {'sx'}, dimensions={2}, use_global_device_ids=true | all-gather | bytes 245760 | tf_op jit(solution)/shard_map/all_gather | solution.py:117
  34.2 0.6 or_convert_fusion.mask_ref
  34.7 12.9 %all-to-all-done.kv_ref = bf16[8,2,40,768]{3,2,1,0:T(8,128)(2,1)S(1)} async-done(((bf16[8,2,40,768]{3,2,1,0:T(8,128)(2,1)}), bf16[8,2,40,768]{3,2,1,0:T(8,128)(2,1)S(1)}, u32[]{:S(2)}, u32[]{:S(2)}) %all-to-all-start) | async-done | bytes 983072 | tf_op jit(solution)/shard_map/all_to_all | solution.py:110
  47.6 0.0 copy-start.2
  47.6 0.9 copy-done.2
  48.6 0.0 copy-start.1
  48.6 0.0 copy-start.8
  48.6 0.0 copy-start.6
  48.6 5.4 %shard_map.175 = f32[128,792]{1,0:T(8,128)} custom-call(bf16[128,768]{1,0:T(8,128)(2,1)} %bitcast.27, bf16[8,2,40,768]{3,2,1,0:T(8,128)(2,1)} %copy-done.2, f32[1,320]{1,0:T(1,128)} %or_convert_fusion.mask_ref), custom_call_target="tpu_custom_call" | custom-call | flops 251658240 | bytes 1585152 | tf_op jit(solution)/shard_map/pallas_call | solution.py:62
  54.0 4.3 %all-to-all-start.1 = ((f32[4,32,792]{2,1,0:T(8,128)}), f32[4,32,792]{2,1,0:T(8,128)S(1)}, u32[]{:S(2)}, u32[]{:S(2)}) async-start(f32[4,32,792]{2,1,0:T(8,128)} %bitcast.26), calls=%async_computation.1 | async-start | bytes 917504 | tf_op jit(solution)/shard_map/all_to_all | solution.py:129
  58.3 0.0 copy-done.1
  58.3 1.9 %collective-permute-start = (bf16[1536,384]{1,0:T(8,128)(2,1)S(1)}, bf16[1536,384]{1,0:T(8,128)(2,1)}, u32[]{:S(2)}, u32[]{:S(2)}) collective-permute-start(bf16[1536,384]{1,0:T(8,128)(2,1)S(1)} %copy-done.1), channel_id=1, source_target_pairs={{0,32},{32,0},{1,33},{33,1},{2,34},{34,2},{3,35},{35,3},{4,36},{36... | collective-permute-start | bytes 3538952 | tf_op jit(solution)/shard_map/ppermute | solution.py:147
  60.2 2.4 %collective-permute-start.1 = (bf16[384,1536]{1,0:T(8,128)(2,1)}, bf16[384,1536]{1,0:T(8,128)(2,1)}, u32[]{:S(2)}, u32[]{:S(2)}) collective-permute-start(bf16[384,1536]{1,0:T(8,128)(2,1)} %param.28), channel_id=1, source_target_pairs={{0,32},{32,0},{1,33},{33,1},{2,34},{34,2},{3,35},{35,3},{4,36},{36... | collective-permute-start | bytes 3538952 | tf_op jit(solution)/shard_map/ppermute | solution.py:148
  62.6 0.0 copy-done.8
  62.6 0.0 copy-done.9
  62.7 0.0 copy-done.6
  62.7 4.5 %all-to-all-done.1 = f32[4,32,792]{2,1,0:T(8,128)S(1)} async-done(((f32[4,32,792]{2,1,0:T(8,128)}), f32[4,32,792]{2,1,0:T(8,128)S(1)}, u32[]{:S(2)}, u32[]{:S(2)}) %all-to-all-start.1) | async-done | bytes 405536 | tf_op jit(solution)/shard_map/all_to_all | solution.py:129
  67.2 0.1 fusion.35
  67.3 0.3 mul.150
  67.7 0.0 copy-start.3
  67.7 0.3 mul.151
  68.0 0.1 div.40
  68.1 0.1 div.41
  68.2 0.0 all-gather.3.cloned.1.call-done
  68.3 0.3 copy-done.3
  68.6 2.6 %fusion.49 = (f32[32]{0:T(128)S(1)}, f32[32,1536]{1,0:T(8,128)S(1)}) fusion(bf16[768,1536]{0,1:T(8,128)(2,1)} %all-gather.3.cloned.1.call-done, f32[32,768]{1,0:T(8,128)S(1)} %fusion.2, f32[32,768]{1,0:T(8,128)S(1)} %div.41, f32[1536]{0:T(1024)S(1)} %reduce.3, bf16[1,1,32,1536]{3,2,1,0:T(8,128)(2,1)S(1)} %copy-done.3), kind=kOutput, calls=%fused_computation.81 | convolution fusion | flops 75743200 | bytes 2857088 | tf_op jit(solution)/shard_map/dot_general | solution.py:138
  71.1 0.2 multiply_reduce_fusion.1
  71.3 0.1 add_convert_fusion.1
  71.5 15.1 %all_gather.11 = bf16[128,1536]{1,0:T(8,128)(2,1)S(1)} all-gather(bf16[32,1536]{1,0:T(8,128)(2,1)S(1)} %add_convert_fusion.1), channel_id=1, replica_groups=mesh['cfg'=2,'ry'=4,'rc'=2,'sz'=8,'sx'=4] {'ry'}, dimensions={0}, use_global_device_ids=true | all-gather | bytes 491520 | tf_op jit(solution)/shard_map/all_gather | solution.py:149
  86.5 2.0 %fusion.21 = f32[128,1536]{1,0:T(8,128)S(1)} fusion(bf16[384,1536]{1,0:T(8,128)(2,1)} %param.28, bf16[128,1536]{1,0:T(8,128)(2,1)S(1)} %all_gather.11, bf16[1536,384]{1,0:T(8,128)(2,1)S(1)} %copy-done.1), kind=kOutput, calls=%fused_computation.31 | convolution fusion | flops 302432256 | bytes 3538944 | tf_op jit(solution)/shard_map/dot_general | solution.py:158
  88.5 0.0 copy-start.10
  88.5 0.0 copy-start.11
  88.6 0.0 copy-start.7
  88.6 0.0 collective-permute-done
  88.6 0.0 collective-permute-done.1
  88.6 3.1 %fusion = bf16[128,1536]{1,0:T(8,128)(2,1)} fusion(f32[128,1536]{1,0:T(8,128)S(1)} %fusion.21, bf16[384,1536]{1,0:T(8,128)(2,1)} %collective-permute-done.1, bf16[128,1536]{1,0:T(8,128)(2,1)S(1)} %all_gather.11, bf16[1536,384]{1,0:T(8,128)(2,1)} %collective-permute-done), kind=kOutput, calls=%fused_computation.1 | convolution fusion | flops 302825472 | bytes 3932160 | tf_op jit(solution)/shard_map/dot_general | solution.py:159
  91.7 6.2 %all-to-all-start.2 = ((bf16[4,32,1536]{2,1,0:T(8,128)(2,1)}), bf16[4,32,1536]{2,1,0:T(8,128)(2,1)S(1)}, u32[]{:S(2)}, u32[]{:S(2)}) async-start(bf16[4,32,1536]{2,1,0:T(8,128)(2,1)} %bitcast.6), calls=%async_computation.2 | async-start | bytes 786432 | tf_op jit(solution)/shard_map/all_to_all | solution.py:165
  97.8 0.0 copy-done.10
  97.9 0.0 copy-done.11
  97.9 0.0 copy-done.7
  97.9 6.4 %all-to-all-done.2 = bf16[4,32,1536]{2,1,0:T(8,128)(2,1)S(1)} async-done(((bf16[4,32,1536]{2,1,0:T(8,128)(2,1)}), bf16[4,32,1536]{2,1,0:T(8,128)(2,1)S(1)}, u32[]{:S(2)}, u32[]{:S(2)}) %all-to-all-start.2) | async-done | bytes 393248 | tf_op jit(solution)/shard_map/all_to_all | solution.py:165
  104.3 0.1 convert_reduce_fusion
  104.4 0.1 fusion.48
  104.5 0.2 multiply_reduce_fusion
  104.8 0.0 copy-done
  104.8 0.2 fusion.19
  105.0 3.0 %collective-permute-start.2 = (f32[32,64]{1,0:T(8,128)S(1)}, f32[32,64]{1,0:T(8,128)S(1)}, u32[]{:S(2)}, u32[]{:S(2)}) collective-permute-start(f32[32,64]{1,0:T(8,128)S(1)} %fusion.19), channel_id=1, source_target_pairs={{0,256},{256,0},{1,257},{257,1},{2,258},{258,2},{3,259},{259,3},{4... | collective-permute-start | bytes 24584 | tf_op jit(solution)/shard_map/ppermute | solution.py:24
  108.6 5.9 %collective-permute-done.2 = f32[32,64]{1,0:T(8,128)S(1)} collective-permute-done((f32[32,64]{1,0:T(8,128)S(1)}, f32[32,64]{1,0:T(8,128)S(1)}, u32[]{:S(2)}, u32[]{:S(2)}) %collective-permute-start.2) | collective-permute-done | bytes 8224 | tf_op jit(solution)/shard_map/ppermute | solution.py:24
  114.5 0.6 multiply_reduce_fusion.2
  115.2 1.4 pad_maximum_fusion
  116.5 0.6 broadcast_in_dim.8
  117.1 3.9 %all-to-all-start.3 = ((f32[32,1,2]{2,1,0:T(1,128)}), f32[32,1,2]{2,1,0:T(1,128)S(1)}, u32[]{:S(2)}, u32[]{:S(2)}) async-start(f32[32,1,2]{2,1,0:T(1,128)} %broadcast_in_dim.8), calls=%async_computation.3 | async-start | bytes 32768 | tf_op jit(solution)/shard_map/all_to_all | solution.py:179
  121.0 0.0 copy-done.5
  121.0 0.7 bitcast_add_fusion
  121.7 8.9 %all-to-all-done.3 = f32[32,1,2]{2,1,0:T(1,128)S(1)} async-done(((f32[32,1,2]{2,1,0:T(1,128)}), f32[32,1,2]{2,1,0:T(1,128)S(1)}, u32[]{:S(2)}, u32[]{:S(2)}) %all-to-all-start.3) | async-done | bytes 288 | tf_op jit(solution)/shard_map/all_to_all | solution.py:179
  130.6 0.1 copy.19
  130.6 0.6 slice_reduce_fusion.1
  (14 shorter events, 0.2 us)
Async XLA Ops:
  7.2 97.6 %copy-start = (bf16[1536,64]{0,1:T(8,128)(2,1)S(1)}, bf16[1536,64]{0,1:T(8,128)(2,1)}, u32[]{:S(2)}) copy-start(bf16[1536,64]{0,1:T(8,128)(2,1)} %param.29) | copy-start | bytes 589828
  7.2 61.1 %all-gather.3.cloned.1.call-start = ((), (), s32[]{:S(2)}) async-start(), calls=%async_computation.4 | async-start | bytes 2654208 | tf_op jit(solution)/shard_map/all_gather | solution.py:140
  9.8 11.1 %copy-start.4 = (bf16[1,1,32,768]{3,2,1,0:T(8,128)(2,1)S(1)}, bf16[1,1,32,768]{3,2,1,0:T(8,128)(2,1)}, u32[]{:S(2)}) copy-start(bf16[1,1,32,768]{3,2,1,0:T(8,128)(2,1)} %param.16) | copy-start | bytes 147460
  9.8 37.8 %all-to-all-start = ((bf16[8,2,40,768]{3,2,1,0:T(8,128)(2,1)}), bf16[8,2,40,768]{3,2,1,0:T(8,128)(2,1)S(1)}, u32[]{:S(2)}, u32[]{:S(2)}) async-start(bf16[8,2,40,768]{3,2,1,0:T(8,128)(2,1)} %broadcast_in_dim.7), calls=%async_computation | async-start | bytes 1966080 | tf_op jit(solution)/shard_map/all_to_all | solution.py:110
  47.6 1.0 copy-start.2
  48.6 9.7 %copy-start.1 = (bf16[1536,384]{1,0:T(8,128)(2,1)S(1)}, bf16[1536,384]{1,0:T(8,128)(2,1)}, u32[]{:S(2)}) copy-start(bf16[1536,384]{1,0:T(8,128)(2,1)} %param.27) | copy-start | bytes 3538948
  48.6 14.0 %copy-start.8 = (f32[1,1,1536]{2,1,0:T(1,128)S(1)}, f32[1,1,1536]{2,1,0:T(1,128)}, u32[]{:S(2)}) copy-start(f32[1,1,1536]{2,1,0:T(1,128)} %param.20) | copy-start | bytes 18436
  48.6 14.1 %copy-start.9 = (f32[1,1,1536]{2,1,0:T(1,128)S(1)}, f32[1,1,1536]{2,1,0:T(1,128)}, u32[]{:S(2)}) copy-start(f32[1,1,1536]{2,1,0:T(1,128)} %param.21) | copy-start | bytes 18436
  48.6 14.1 %copy-start.6 = (f32[1,1,1536]{2,1,0:T(1,128)S(1)}, f32[1,1,1536]{2,1,0:T(1,128)}, u32[]{:S(2)}) copy-start(f32[1,1,1536]{2,1,0:T(1,128)} %param.22) | copy-start | bytes 18436
  54.0 13.2 %all-to-all-start.1 = ((f32[4,32,792]{2,1,0:T(8,128)}), f32[4,32,792]{2,1,0:T(8,128)S(1)}, u32[]{:S(2)}, u32[]{:S(2)}) async-start(f32[4,32,792]{2,1,0:T(8,128)} %bitcast.26), calls=%async_computation.1 | async-start | bytes 917504 | tf_op jit(solution)/shard_map/all_to_all | solution.py:129
  58.3 30.3 %collective-permute-start = (bf16[1536,384]{1,0:T(8,128)(2,1)S(1)}, bf16[1536,384]{1,0:T(8,128)(2,1)}, u32[]{:S(2)}, u32[]{:S(2)}) collective-permute-start(bf16[1536,384]{1,0:T(8,128)(2,1)S(1)} %copy-done.1), channel_id=1, source_target_pairs={{0,32},{32,0},{1,33},{33,1},{2,34},{34,2},{3,35},{35,3},{4,36},{36... | collective-permute-start | bytes 3538952 | tf_op jit(solution)/shard_map/ppermute | solution.py:147
  60.2 28.4 %collective-permute-start.1 = (bf16[384,1536]{1,0:T(8,128)(2,1)}, bf16[384,1536]{1,0:T(8,128)(2,1)}, u32[]{:S(2)}, u32[]{:S(2)}) collective-permute-start(bf16[384,1536]{1,0:T(8,128)(2,1)} %param.28), channel_id=1, source_target_pairs={{0,32},{32,0},{1,33},{33,1},{2,34},{34,2},{3,35},{35,3},{4,36},{36... | collective-permute-start | bytes 3538952 | tf_op jit(solution)/shard_map/ppermute | solution.py:148
  67.7 0.9 copy-start.3
  88.5 9.3 %copy-start.10 = (f32[1,1,1536]{2,1,0:T(1,128)S(1)}, f32[1,1,1536]{2,1,0:T(1,128)}, u32[]{:S(2)}) copy-start(f32[1,1,1536]{2,1,0:T(1,128)} %param.23) | copy-start | bytes 18436
  88.5 9.3 %copy-start.11 = (f32[1,1,1536]{2,1,0:T(1,128)S(1)}, f32[1,1,1536]{2,1,0:T(1,128)}, u32[]{:S(2)}) copy-start(f32[1,1,1536]{2,1,0:T(1,128)} %param.24) | copy-start | bytes 18436
  88.6 9.3 %copy-start.7 = (f32[1,1,1536]{2,1,0:T(1,128)S(1)}, f32[1,1,1536]{2,1,0:T(1,128)}, u32[]{:S(2)}) copy-start(f32[1,1,1536]{2,1,0:T(1,128)} %param.25) | copy-start | bytes 18436
  91.7 12.7 %all-to-all-start.2 = ((bf16[4,32,1536]{2,1,0:T(8,128)(2,1)}), bf16[4,32,1536]{2,1,0:T(8,128)(2,1)S(1)}, u32[]{:S(2)}, u32[]{:S(2)}) async-start(bf16[4,32,1536]{2,1,0:T(8,128)(2,1)} %bitcast.6), calls=%async_computation.2 | async-start | bytes 786432 | tf_op jit(solution)/shard_map/all_to_all | solution.py:165
  97.8 23.2 %copy-start.5 = (f32[1,32,32]{2,1,0:T(8,128)S(1)}, f32[1,32,32]{2,1,0:T(8,128)}, u32[]{:S(2)}) copy-start(f32[1,32,32]{2,1,0:T(8,128)} %param.30) | copy-start | bytes 12292
  105.0 9.5 %collective-permute-start.2 = (f32[32,64]{1,0:T(8,128)S(1)}, f32[32,64]{1,0:T(8,128)S(1)}, u32[]{:S(2)}, u32[]{:S(2)}) collective-permute-start(f32[32,64]{1,0:T(8,128)S(1)} %fusion.19), channel_id=1, source_target_pairs={{0,256},{256,0},{1,257},{257,1},{2,258},{258,2},{3,259},{259,3},{4... | collective-permute-start | bytes 24584 | tf_op jit(solution)/shard_map/ppermute | solution.py:24
  117.1 13.4 %all-to-all-start.3 = ((f32[32,1,2]{2,1,0:T(1,128)}), f32[32,1,2]{2,1,0:T(1,128)S(1)}, u32[]{:S(2)}, u32[]{:S(2)}) async-start(f32[32,1,2]{2,1,0:T(1,128)} %broadcast_in_dim.8), calls=%async_computation.3 | async-start | bytes 32768 | tf_op jit(solution)/shard_map/all_to_all | solution.py:179
Sparse Core Ops, SparseCore 0:
  10.1 44.8 all-gather.2

commit v14 on v10

--- a/solution.py
+++ b/solution.py
@@ -36,8 +36,8 @@
     for pair in range(HEADS // 2):
         cols = slice(pair * lanes, (pair + 1) * lanes)
         q2 = q_ref[:, cols]
-        k2 = kv_ref[0, :, cols]
-        v2 = kv_ref[1, :, cols]
+        k2 = jnp.concatenate([kv_ref[z, 0, :, cols] for z in range(kv_ref.shape[0])], axis=0)
+        v2 = jnp.concatenate([kv_ref[z, 1, :, cols] for z in range(kv_ref.shape[0])], axis=0)
         outs = []
         for half in (low, jnp.logical_not(low)):
             q_half = jnp.where(half, q2, jnp.zeros_like(q2))
@@ -65,8 +65,8 @@
         in_specs=[pl.BlockSpec(memory_space=pltpu.VMEM)] * 3,
         out_specs=pl.BlockSpec(memory_space=pltpu.VMEM),
         cost_estimate=pl.CostEstimate(
-            flops=8 * rows * kv.shape[1] * width,
-            transcendentals=2 * rows * kv.shape[1] * HEADS,
+            flops=8 * rows * kv.shape[0] * kv.shape[2] * width,
+            transcendentals=2 * rows * kv.shape[0] * kv.shape[2] * HEADS,
             bytes_accessed=q.size * 2 + kv.size * 2 + rows * (width + 2 * HEADS) * 4,
         ),
     )(q, kv, mask)
@@ -136,12 +136,17 @@
     factor = HD ** (-0.5)
     n_x = lax.axis_size("sx")
     x_index = lax.axis_index("sx")
-    query_rows = lax.all_to_all(
-        jnp.broadcast_to(query[0, 0][None], (n_x,) + query.shape[2:]), "sx", 0, 0, tiled=True
-    ).reshape(n_x * img_dev, query.shape[3])
-    piece = lax.all_gather(key_value[:, 0, 0], "sz", axis=1, tiled=True)
+    n_z = lax.axis_size("sz")
+    kv_blocks = lax.all_to_all(
+        jnp.broadcast_to(key_value[:, 0, 0][None], (n_z,) + key_value[:, 0, 0].shape),
+        "sz",
+        0,
+        0,
+        tiled=True,
+    )
+    query_rows = lax.all_gather(query[0, 0], "sx", axis=0, tiled=True)
     q_rows = query_rows.shape[0]
-    piece_rows = piece.shape[1]
+    piece_rows = n_z * rows_dev
     positions = jnp.arange(piece_rows, dtype=jnp.int32)
     within = positions % rows_dev
     source = (positions // rows_dev) * n_x + x_index
@@ -149,7 +154,7 @@
     usable = ((within < img_dev) | (text_slot < length)).astype(jnp.float32)[None, :]
     width = HEADS * HD
     packed = attention_partials(
-        query_rows, piece.reshape(2, piece_rows, width), usable
+        query_rows, kv_blocks, usable
     ).reshape(n_x, img_dev, width + 2 * HEADS)
     got = lax.all_to_all(packed, "sx", 0, 0, tiled=True)
     got_out = got[:, :, :width].reshape(n_x, img_dev, HEADS, HD)

time: 146 us -> 143 us (0.979)
  blocking collectives: 49.9 us -> 29.1 us
  waiting for transfers between devices: 24.3 us -> 37.8 us
  starting transfers between devices: 29 us -> 32.2 us
    all_gather x1, blocking collectives: 35.1 us -> 14 us  [per_device(): query_rows = lax.all_gather(query[0, 0], 'sx', axis=0, tiled=True)]
    all_to_all x1, waiting for transfers between devices: 0.01 us -> 12.1 us  [per_device(): lax.all_to_all(jnp.broadcast_to(key_value[:, 0, 0][None], (n_z,) + key_va...]
    all_to_all x1, starting transfers between devices: 4.29 us -> 10.5 us  [per_device(): lax.all_to_all(jnp.broadcast_to(key_value[:, 0, 0][None], (n_z,) + key_va...]
    all_to_all x1, starting transfers between devices: 5.67 us -> 3.85 us  [per_device(): lax.all_to_all(jnp.broadcast_to(partials[None], (n_seq, 2)), ('sz', 'sx')...]
  transfers between devices with their start and end apart: 8 -> 8, of which waited for: 4 -> 5; matrix products, arithmetic and copies ran while one was open for 8% -> 9% of each run, Pallas kernels for 4% -> 4%
where the time goes in v14:
time: 143 us
  waiting for transfers between devices  37.8 us (26%)
  starting transfers between devices  32.2 us (23%)
  blocking collectives  29.1 us (20%)
  between operations  17.3 us (12%)
  local copies, waits for them, and re-layouts  8.97 us (6%)
  Pallas kernels  8.79 us (6%)
  other arithmetic  5.55 us (4%)
  matrix products  2.8 us (2%)
    all_gather x1, blocking collectives, per_device(): line_in = lax.all_gather(mlp_in, 'ry', axis=0, tiled=True)  15.1 us
    all_gather x1, blocking collectives, per_device(): query_rows = lax.all_gather(query[0, 0], 'sx', axis=0, tiled=True)  14 us
    all_to_all x1, waiting for transfers between devices, per_device(): lax.all_to_all(jnp.broadcast_to(key_value[:, 0, 0][None], (n_z,) + key_va...  12.1 us
    all_to_all x1, starting transfers between devices, per_device(): lax.all_to_all(jnp.broadcast_to(key_value[:, 0, 0][None], (n_z,) + key_va...  10.5 us
    all_to_all x1, waiting for transfers between devices, per_device(): lax.all_to_all(jnp.broadcast_to(partials[None], (n_seq, 2)), ('sz', 'sx')...  8.88 us
    all_to_all x1, waiting for transfers between devices, per_device(): lax.all_to_all(mlp_parts, 'ry', 0, 0, tiled=True).astype(jnp.float32)  6.41 us
    all_to_all x1, starting transfers between devices, per_device(): lax.all_to_all(mlp_parts, 'ry', 0, 0, tiled=True).astype(jnp.float32)  6.27 us
    ppermute x1, waiting for transfers between devices, swapped(): return lax.ppermute(block, axis, route)  5.91 us
  transfers between devices with their start and end apart: 8, of which 5 were waited for; matrix products, arithmetic and copies ran while one was open for 9% of the time, Pallas kernels for 4%

profile of v14, /device:TPU:56, one launch (start us, length us, event | category | flops | bytes accessed | tf_op | source)
XLA Modules:
  0.0 142.6 jit_solution(4464894607532214730)
XLA Ops:
  7.2 0.0 copy-start
  7.2 0.0 all-gather.3.cloned.1.call-start
  7.2 0.7 all-gather.3.cloned.1.call-update
  7.9 1.9 %broadcast_in_dim.7 = bf16[8,2,40,768]{3,2,1,0:T(8,128)(2,1)} broadcast(bf16[2,40,768]{2,1,0:T(8,128)(2,1)} %bitcast.22), dimensions={1,2,3} | broadcast | bytes 1105920 | tf_op jit(solution)/shard_map/broadcast_in_dim | solution.py:141
  9.8 0.0 copy-start.1
  9.8 0.0 copy-start.2
  9.8 0.0 copy-start.7
  9.8 0.0 copy-start.5
  9.8 10.5 %all-to-all-start = ((bf16[8,2,40,768]{3,2,1,0:T(8,128)(2,1)}), bf16[8,2,40,768]{3,2,1,0:T(8,128)(2,1)S(1)}, u32[]{:S(2)}, u32[]{:S(2)}) async-start(bf16[8,2,40,768]{3,2,1,0:T(8,128)(2,1)} %broadcast_in_dim.7), calls=%async_computation | async-start | bytes 1966080 | tf_op jit(solution)/shard_map/all_to_all | solution.py:140
  21.0 14.0 %all-gather = bf16[1,1,128,768]{3,2,1,0:T(8,128)(2,1)} all-gather(bf16[1,1,32,768]{3,2,1,0:T(8,128)(2,1)} %param.16), channel_id=2, replica_groups=mesh['cfg'=2,'ry'=4,'rc'=2,'sz'=8,'sx'=4] {'sx'}, dimensions={2}, use_global_device_ids=true | all-gather | bytes 245760 | tf_op jit(solution)/shard_map/all_gather | solution.py:147
  35.0 0.6 or_convert_fusion.mask_ref
  35.5 12.1 %all-to-all-done.kv_ref = bf16[8,2,40,768]{3,2,1,0:T(8,128)(2,1)S(1)} async-done(((bf16[8,2,40,768]{3,2,1,0:T(8,128)(2,1)}), bf16[8,2,40,768]{3,2,1,0:T(8,128)(2,1)S(1)}, u32[]{:S(2)}, u32[]{:S(2)}) %all-to-all-start) | async-done | bytes 983072 | tf_op jit(solution)/shard_map/all_to_all | solution.py:140
  47.6 0.0 copy-start.3
  47.6 0.9 copy-done.3
  48.6 5.3 %shard_map.175 = f32[128,792]{1,0:T(8,128)} custom-call(bf16[128,768]{1,0:T(8,128)(2,1)} %bitcast.21, bf16[8,2,40,768]{3,2,1,0:T(8,128)(2,1)} %copy-done.3, f32[1,320]{1,0:T(1,128)} %or_convert_fusion.mask_ref), custom_call_target="tpu_custom_call" | custom-call | flops 251658240 | bytes 1585152 | tf_op jit(solution)/shard_map/pallas_call | solution.py:62
  53.9 4.3 %all-to-all-start.1 = ((f32[4,32,792]{2,1,0:T(8,128)}), f32[4,32,792]{2,1,0:T(8,128)S(1)}, u32[]{:S(2)}, u32[]{:S(2)}) async-start(f32[4,32,792]{2,1,0:T(8,128)} %bitcast.20), calls=%async_computation.1 | async-start | bytes 917504 | tf_op jit(solution)/shard_map/all_to_all | solution.py:159
  58.2 0.0 copy-done.1
  58.2 1.9 %collective-permute-start = (bf16[1536,384]{1,0:T(8,128)(2,1)S(1)}, bf16[1536,384]{1,0:T(8,128)(2,1)}, u32[]{:S(2)}, u32[]{:S(2)}) collective-permute-start(bf16[1536,384]{1,0:T(8,128)(2,1)S(1)} %copy-done.1), channel_id=1, source_target_pairs={{0,32},{32,0},{1,33},{33,1},{2,34},{34,2},{3,35},{35,3},{4,36},{36... | collective-permute-start | bytes 3538952 | tf_op jit(solution)/shard_map/ppermute | solution.py:177
  60.1 0.0 copy-done.2
  60.1 2.4 %collective-permute-start.1 = (bf16[384,1536]{1,0:T(8,128)(2,1)S(1)}, bf16[384,1536]{1,0:T(8,128)(2,1)}, u32[]{:S(2)}, u32[]{:S(2)}) collective-permute-start(bf16[384,1536]{1,0:T(8,128)(2,1)S(1)} %copy-done.2), channel_id=1, source_target_pairs={{0,32},{32,0},{1,33},{33,1},{2,34},{34,2},{3,35},{35,3},{4,36},{36... | collective-permute-start | bytes 3538952 | tf_op jit(solution)/shard_map/ppermute | solution.py:178
  62.5 0.0 copy-done.7
  62.5 0.7 reduce.6
  63.3 0.0 copy-done.5
  63.3 3.8 %all-to-all-done.1 = f32[4,32,792]{2,1,0:T(8,128)S(1)} async-done(((f32[4,32,792]{2,1,0:T(8,128)}), f32[4,32,792]{2,1,0:T(8,128)S(1)}, u32[]{:S(2)}, u32[]{:S(2)}) %all-to-all-start.1) | async-done | bytes 405536 | tf_op jit(solution)/shard_map/all_to_all | solution.py:159
  67.1 0.1 fusion.7
  67.2 1.4 mul.126
  68.6 1.5 %mul.127 = f32[4,32,768]{2,1,0:T(8,128)S(1)} reshape(f32[4,32,12,64]{3,2,1,0:T(8,128)} %mul.126) | data formatting | bytes 786432 | tf_op jit(solution)/shard_map/mul | solution.py:165
  70.1 0.8 div.40
  70.9 1.7 %div.41 = f32[32,768]{1,0:T(8,128)} reshape(f32[32,12,64]{2,1,0:T(8,128)} %div.40) | data formatting | bytes 196608 | tf_op jit(solution)/shard_map/div | solution.py:167
  72.6 0.0 all-gather.3.cloned.1.call-done
  72.7 2.6 %fusion.13 = (f32[32]{0:T(128)S(1)}, f32[32,1536]{1,0:T(8,128)S(1)}) fusion(bf16[768,1536]{0,1:T(8,128)(2,1)} %all-gather.3.cloned.1.call-done, f32[32,768]{1,0:T(8,128)S(1)} %fusion.1, f32[32,768]{1,0:T(8,128)} %div.41, f32[1536]{0:T(1024)S(1)} %reduce.3, bf16[1,1,32,1536]{3,2,1,0:T(8,128)(2,1)} %param.18), kind=kOutput, calls=%fused_computation.44 | convolution fusion | flops 75743200 | bytes 2857088 | tf_op jit(solution)/shard_map/dot_general | solution.py:168
  75.3 0.2 multiply_reduce_fusion.1
  75.5 0.1 add_convert_fusion.1
  75.6 15.1 %all_gather.11.x_ref = bf16[128,1536]{1,0:T(8,128)(2,1)S(1)} all-gather(bf16[32,1536]{1,0:T(8,128)(2,1)S(1)} %add_convert_fusion.1), channel_id=1, replica_groups=mesh['cfg'=2,'ry'=4,'rc'=2,'sz'=8,'sx'=4] {'ry'}, dimensions={0}, use_global_device_ids=true | all-gather | bytes 491520 | tf_op jit(solution)/shard_map/all_gather | solution.py:179
  90.7 0.0 copy-start.8
  90.7 0.0 copy-start.9
  90.7 0.0 copy-start.6
  90.7 0.0 collective-permute-done.up_b_ref
  90.7 0.0 collective-permute-done.1.down_b_ref
  90.7 3.5 %shard_map.176 = bf16[128,1536]{1,0:T(8,128)(2,1)} custom-call(bf16[128,1536]{1,0:T(8,128)(2,1)S(1)} %all_gather.11.x_ref, bf16[1536,384]{1,0:T(8,128)(2,1)S(1)} %copy-done.1, bf16[1536,384]{1,0:T(8,128)(2,1)} %collective-permute-done.up_b_ref, bf16[384,1536]{1,0:T(8,128)(2,1)S(1)} %copy-done.2, bf16[384,1536]{1,0:T(8,128)(2,1)} %collective-permute-done.1.down_b_ref), custom_call_target="tpu_custom_call" | custom-call | flops 603979776 | bytes 5505024 | tf_op jit(solution)/shard_map/pallas_call | solution.py:91
  94.2 0.0 copy-start.4
  94.2 6.3 %all-to-all-start.2 = ((bf16[4,32,1536]{2,1,0:T(8,128)(2,1)}), bf16[4,32,1536]{2,1,0:T(8,128)(2,1)S(1)}, u32[]{:S(2)}, u32[]{:S(2)}) async-start(bf16[4,32,1536]{2,1,0:T(8,128)(2,1)} %bitcast.6), calls=%async_computation.2 | async-start | bytes 786432 | tf_op jit(solution)/shard_map/all_to_all | solution.py:185
  100.5 0.0 copy-done.8
  100.5 0.0 copy-done.9
  100.5 0.0 copy-done.6
  100.6 6.4 %all-to-all-done.2 = bf16[4,32,1536]{2,1,0:T(8,128)(2,1)S(1)} async-done(((bf16[4,32,1536]{2,1,0:T(8,128)(2,1)}), bf16[4,32,1536]{2,1,0:T(8,128)(2,1)S(1)}, u32[]{:S(2)}, u32[]{:S(2)}) %all-to-all-start.2) | async-done | bytes 393248 | tf_op jit(solution)/shard_map/all_to_all | solution.py:185
  107.0 0.1 convert_reduce_fusion
  107.0 0.1 fusion.12
  107.2 0.2 multiply_reduce_fusion
  107.4 0.0 copy-done
  107.4 0.2 fusion.2
  107.6 3.0 %collective-permute-start.2 = (f32[32,64]{1,0:T(8,128)S(1)}, f32[32,64]{1,0:T(8,128)S(1)}, u32[]{:S(2)}, u32[]{:S(2)}) collective-permute-start(f32[32,64]{1,0:T(8,128)S(1)} %fusion.2), channel_id=1, source_target_pairs={{0,256},{256,0},{1,257},{257,1},{2,258},{258,2},{3,259},{259,3},{4... | collective-permute-start | bytes 24584 | tf_op jit(solution)/shard_map/ppermute | solution.py:24
  111.3 5.9 %collective-permute-done.2 = f32[32,64]{1,0:T(8,128)S(1)} collective-permute-done((f32[32,64]{1,0:T(8,128)S(1)}, f32[32,64]{1,0:T(8,128)S(1)}, u32[]{:S(2)}, u32[]{:S(2)}) %collective-permute-start.2) | collective-permute-done | bytes 8224 | tf_op jit(solution)/shard_map/ppermute | solution.py:24
  117.2 0.6 multiply_reduce_fusion.2
  117.8 1.4 pad_maximum_fusion
  119.2 0.6 broadcast_in_dim.8
  119.8 3.9 %all-to-all-start.3 = ((f32[32,1,2]{2,1,0:T(1,128)}), f32[32,1,2]{2,1,0:T(1,128)S(1)}, u32[]{:S(2)}, u32[]{:S(2)}) async-start(f32[32,1,2]{2,1,0:T(1,128)} %broadcast_in_dim.8), calls=%async_computation.3 | async-start | bytes 32768 | tf_op jit(solution)/shard_map/all_to_all | solution.py:199
  123.6 0.0 copy-done.4
  123.6 0.7 bitcast_add_fusion
  124.3 8.9 %all-to-all-done.3 = f32[32,1,2]{2,1,0:T(1,128)S(1)} async-done(((f32[32,1,2]{2,1,0:T(1,128)}), f32[32,1,2]{2,1,0:T(1,128)S(1)}, u32[]{:S(2)}, u32[]{:S(2)}) %all-to-all-start.3) | async-done | bytes 288 | tf_op jit(solution)/shard_map/all_to_all | solution.py:199
  133.2 0.1 copy.19
  133.3 0.6 slice_reduce_fusion.1
  (11 shorter events, 0.2 us)
Async XLA Ops:
  7.2 100.2 %copy-start = (bf16[1536,64]{0,1:T(8,128)(2,1)S(1)}, bf16[1536,64]{0,1:T(8,128)(2,1)}, u32[]{:S(2)}) copy-start(bf16[1536,64]{0,1:T(8,128)(2,1)} %param.29) | copy-start | bytes 589828
  7.2 65.5 %all-gather.3.cloned.1.call-start = ((), (), s32[]{:S(2)}) async-start(), calls=%async_computation.4 | async-start | bytes 2654208 | tf_op jit(solution)/shard_map/all_gather | solution.py:170
  9.8 48.3 %copy-start.1 = (bf16[1536,384]{1,0:T(8,128)(2,1)S(1)}, bf16[1536,384]{1,0:T(8,128)(2,1)}, u32[]{:S(2)}) copy-start(bf16[1536,384]{1,0:T(8,128)(2,1)} %up_a_ref.1) | copy-start | bytes 3538948
  9.8 50.3 %copy-start.2 = (bf16[384,1536]{1,0:T(8,128)(2,1)S(1)}, bf16[384,1536]{1,0:T(8,128)(2,1)}, u32[]{:S(2)}) copy-start(bf16[384,1536]{1,0:T(8,128)(2,1)} %down_a_ref.1) | copy-start | bytes 3538948
  9.8 52.7 %copy-start.7 = (f32[1,1,1536]{2,1,0:T(1,128)S(1)}, f32[1,1,1536]{2,1,0:T(1,128)}, u32[]{:S(2)}) copy-start(f32[1,1,1536]{2,1,0:T(1,128)} %param.20) | copy-start | bytes 18436
  9.8 53.4 %copy-start.5 = (f32[1,1,1536]{2,1,0:T(1,128)S(1)}, f32[1,1,1536]{2,1,0:T(1,128)}, u32[]{:S(2)}) copy-start(f32[1,1,1536]{2,1,0:T(1,128)} %param.22) | copy-start | bytes 18436
  9.8 37.8 %all-to-all-start = ((bf16[8,2,40,768]{3,2,1,0:T(8,128)(2,1)}), bf16[8,2,40,768]{3,2,1,0:T(8,128)(2,1)S(1)}, u32[]{:S(2)}, u32[]{:S(2)}) async-start(bf16[8,2,40,768]{3,2,1,0:T(8,128)(2,1)} %broadcast_in_dim.7), calls=%async_computation | async-start | bytes 1966080 | tf_op jit(solution)/shard_map/all_to_all | solution.py:140
  47.6 1.0 copy-start.3
  53.9 13.2 %all-to-all-start.1 = ((f32[4,32,792]{2,1,0:T(8,128)}), f32[4,32,792]{2,1,0:T(8,128)S(1)}, u32[]{:S(2)}, u32[]{:S(2)}) async-start(f32[4,32,792]{2,1,0:T(8,128)} %bitcast.20), calls=%async_computation.1 | async-start | bytes 917504 | tf_op jit(solution)/shard_map/all_to_all | solution.py:159
  58.2 32.5 %collective-permute-start = (bf16[1536,384]{1,0:T(8,128)(2,1)S(1)}, bf16[1536,384]{1,0:T(8,128)(2,1)}, u32[]{:S(2)}, u32[]{:S(2)}) collective-permute-start(bf16[1536,384]{1,0:T(8,128)(2,1)S(1)} %copy-done.1), channel_id=1, source_target_pairs={{0,32},{32,0},{1,33},{33,1},{2,34},{34,2},{3,35},{35,3},{4,36},{36... | collective-permute-start | bytes 3538952 | tf_op jit(solution)/shard_map/ppermute | solution.py:177
  60.1 30.6 %collective-permute-start.1 = (bf16[384,1536]{1,0:T(8,128)(2,1)S(1)}, bf16[384,1536]{1,0:T(8,128)(2,1)}, u32[]{:S(2)}, u32[]{:S(2)}) collective-permute-start(bf16[384,1536]{1,0:T(8,128)(2,1)S(1)} %copy-done.2), channel_id=1, source_target_pairs={{0,32},{32,0},{1,33},{33,1},{2,34},{34,2},{3,35},{35,3},{4,36},{36... | collective-permute-start | bytes 3538952 | tf_op jit(solution)/shard_map/ppermute | solution.py:178
  90.7 9.8 %copy-start.8 = (f32[1,1,1536]{2,1,0:T(1,128)S(1)}, f32[1,1,1536]{2,1,0:T(1,128)}, u32[]{:S(2)}) copy-start(f32[1,1,1536]{2,1,0:T(1,128)} %param.23) | copy-start | bytes 18436
  90.7 9.8 %copy-start.9 = (f32[1,1,1536]{2,1,0:T(1,128)S(1)}, f32[1,1,1536]{2,1,0:T(1,128)}, u32[]{:S(2)}) copy-start(f32[1,1,1536]{2,1,0:T(1,128)} %param.24) | copy-start | bytes 18436
  90.7 9.9 %copy-start.6 = (f32[1,1,1536]{2,1,0:T(1,128)S(1)}, f32[1,1,1536]{2,1,0:T(1,128)}, u32[]{:S(2)}) copy-start(f32[1,1,1536]{2,1,0:T(1,128)} %param.25) | copy-start | bytes 18436
  94.2 29.4 %copy-start.4 = (f32[1,32,32]{2,1,0:T(8,128)S(1)}, f32[1,32,32]{2,1,0:T(8,128)}, u32[]{:S(2)}) copy-start(f32[1,32,32]{2,1,0:T(8,128)} %param.30) | copy-start | bytes 12292
  94.2 12.8 %all-to-all-start.2 = ((bf16[4,32,1536]{2,1,0:T(8,128)(2,1)}), bf16[4,32,1536]{2,1,0:T(8,128)(2,1)S(1)}, u32[]{:S(2)}, u32[]{:S(2)}) async-start(bf16[4,32,1536]{2,1,0:T(8,128)(2,1)} %bitcast.6), calls=%async_computation.2 | async-start | bytes 786432 | tf_op jit(solution)/shard_map/all_to_all | solution.py:185
  107.6 9.5 %collective-permute-start.2 = (f32[32,64]{1,0:T(8,128)S(1)}, f32[32,64]{1,0:T(8,128)S(1)}, u32[]{:S(2)}, u32[]{:S(2)}) collective-permute-start(f32[32,64]{1,0:T(8,128)S(1)} %fusion.2), channel_id=1, source_target_pairs={{0,256},{256,0},{1,257},{257,1},{2,258},{258,2},{3,259},{259,3},{4... | collective-permute-start | bytes 24584 | tf_op jit(solution)/shard_map/ppermute | solution.py:24
  119.8 13.4 %all-to-all-start.3 = ((f32[32,1,2]{2,1,0:T(1,128)}), f32[32,1,2]{2,1,0:T(1,128)S(1)}, u32[]{:S(2)}, u32[]{:S(2)}) async-start(f32[32,1,2]{2,1,0:T(1,128)} %broadcast_in_dim.8), calls=%async_computation.3 | async-start | bytes 32768 | tf_op jit(solution)/shard_map/all_to_all | solution.py:199
Sparse Core Ops, SparseCore 0:
  10.1 44.8 all-gather.2

commit v15 on v13

--- a/solution.py
+++ b/solution.py
@@ -115,6 +115,9 @@
         tiled=True,
     )
     query_rows = lax.all_gather(query[0, 0], "sx", axis=0, tiled=True)
+    up_other = lax.ppermute(w_up, "rc", [(0, 1), (1, 0)])
+    down_other = lax.ppermute(w_down, "rc", [(0, 1), (1, 0)])
+    query_rows, up_other, down_other = lax.optimization_barrier((query_rows, up_other, down_other))
     q_rows = query_rows.shape[0]
     piece_rows = n_z * rows_dev
     positions = jnp.arange(piece_rows, dtype=jnp.int32)
@@ -144,8 +147,6 @@
     mlp_in = modulate_rows(hidden, mlp_shift[0, 0], mlp_scale[0, 0])
     n_y = lax.axis_size("ry")
     pair = [(0, 1), (1, 0)]
-    up_other = lax.ppermute(w_up, "rc", pair)
-    down_other = lax.ppermute(w_down, "rc", pair)
     line_in = lax.all_gather(mlp_in, "ry", axis=0, tiled=True)
     inner_own = jax.nn.gelu(
         jnp.dot(line_in, w_up, preferred_element_type=jnp.float32), approximate=True

time: 141 us -> 141 us (level)
    all_to_all x1, waiting for transfers between devices: 12.9 us -> 7.68 us  [per_device(): lax.all_to_all(jnp.broadcast_to(key_value[:, 0, 0][None], (n_z,) + key_va...]
    all_to_all x1, waiting for transfers between devices: 4.5 us -> 8.85 us  [per_device(): got = lax.all_to_all(packed, 'sx', 0, 0, tiled=True)]
  transfers between devices with their start and end apart: 8 -> 8, of which waited for: 5 -> 5; matrix products, arithmetic and copies ran while one was open for 7% -> 3% of each run, Pallas kernels for 4% -> 4%
where the time goes in v15:
time: 141 us; the launch traced here: 140 us
  waiting for transfers between devices  38.4 us (27%)
  starting transfers between devices  32.1 us (23%)
  blocking collectives  29.1 us (21%)
  between operations  17.4 us (12%)
  matrix products  7.88 us (6%)
  Pallas kernels  5.29 us (4%)
  local copies, waits for them, and re-layouts  4.9 us (3%)
  other arithmetic  4.86 us (3%)
    all_gather x1, blocking collectives, per_device(): line_in = lax.all_gather(mlp_in, 'ry', axis=0, tiled=True)  15.1 us
    all_gather x1, blocking collectives, per_device(): query_rows = lax.all_gather(query[0, 0], 'sx', axis=0, tiled=True)  14 us
    all_to_all x1, starting transfers between devices, per_device(): lax.all_to_all(jnp.broadcast_to(key_value[:, 0, 0][None], (n_z,) + key_va...  10.4 us
    all_to_all x1, waiting for transfers between devices, per_device(): lax.all_to_all(jnp.broadcast_to(partials[None], (n_seq, 2)), ('sz', 'sx')...  8.88 us
    all_to_all x1, waiting for transfers between devices, per_device(): got = lax.all_to_all(packed, 'sx', 0, 0, tiled=True)  8.85 us
    all_to_all x1, waiting for transfers between devices, per_device(): lax.all_to_all(jnp.broadcast_to(key_value[:, 0, 0][None], (n_z,) + key_va...  7.68 us
    all_to_all x1, waiting for transfers between devices, per_device(): lax.all_to_all(mlp_parts, 'ry', 0, 0, tiled=True).astype(jnp.float32)  6.41 us
    all_to_all x1, starting transfers between devices, per_device(): lax.all_to_all(mlp_parts, 'ry', 0, 0, tiled=True).astype(jnp.float32)  6.14 us
  transfers between devices with their start and end apart: 8, of which 5 were waited for; matrix products, arithmetic and copies ran while one was open for 3% of the time, Pallas kernels for 4%

profile of v15, /device:TPU:56, one launch (start us, length us, event | category | flops | bytes accessed | tf_op | source)
XLA Modules:
  0.0 139.9 jit_solution(13654970593204051851)
XLA Ops:
  7.2 0.0 copy-start
  7.2 0.0 all-gather.3.cloned.1.call-start
  7.2 0.7 all-gather.3.cloned.1.call-update
  7.9 0.0 copy-start.2
  7.9 2.0 %broadcast_in_dim.7 = bf16[8,2,40,768]{3,2,1,0:T(8,128)(2,1)} broadcast(bf16[2,40,768]{2,1,0:T(8,128)(2,1)} %bitcast.28), dimensions={1,2,3} | broadcast | bytes 1105920 | tf_op jit(solution)/shard_map/broadcast_in_dim | solution.py:111
  10.0 0.0 copy-start.1
  10.0 10.4 %all-to-all-start = ((bf16[8,2,40,768]{3,2,1,0:T(8,128)(2,1)}), bf16[8,2,40,768]{3,2,1,0:T(8,128)(2,1)S(1)}, u32[]{:S(2)}, u32[]{:S(2)}) async-start(bf16[8,2,40,768]{3,2,1,0:T(8,128)(2,1)} %broadcast_in_dim.7), calls=%async_computation | async-start | bytes 1966080 | tf_op jit(solution)/shard_map/all_to_all | solution.py:110
  20.4 0.0 copy-done.2
  20.4 1.9 %collective-permute-start = (bf16[1536,384]{1,0:T(8,128)(2,1)S(1)}, bf16[1536,384]{1,0:T(8,128)(2,1)}, u32[]{:S(2)}, u32[]{:S(2)}) collective-permute-start(bf16[1536,384]{1,0:T(8,128)(2,1)S(1)} %copy-done.2), channel_id=1, source_target_pairs={{0,32},{32,0},{1,33},{33,1},{2,34},{34,2},{3,35},{35,3},{4,36},{36... | collective-permute-start | bytes 3538952 | tf_op jit(solution)/shard_map/ppermute | solution.py:118
  22.4 0.0 copy-done.1
  22.4 2.4 %collective-permute-start.1 = (bf16[384,1536]{1,0:T(8,128)(2,1)S(1)}, bf16[384,1536]{1,0:T(8,128)(2,1)}, u32[]{:S(2)}, u32[]{:S(2)}) collective-permute-start(bf16[384,1536]{1,0:T(8,128)(2,1)S(1)} %copy-done.1), channel_id=1, source_target_pairs={{0,32},{32,0},{1,33},{33,1},{2,34},{34,2},{3,35},{35,3},{4,36},{36... | collective-permute-start | bytes 3538952 | tf_op jit(solution)/shard_map/ppermute | solution.py:119
  25.4 14.0 %all-gather = bf16[1,1,128,768]{3,2,1,0:T(8,128)(2,1)} all-gather(bf16[1,1,32,768]{3,2,1,0:T(8,128)(2,1)} %param.16), channel_id=2, replica_groups=mesh['cfg'=2,'ry'=4,'rc'=2,'sz'=8,'sx'=4] {'sx'}, dimensions={2}, use_global_device_ids=true | all-gather | bytes 245760 | tf_op jit(solution)/shard_map/all_gather | solution.py:117
  39.4 0.6 or_convert_fusion.mask_ref
  40.0 0.0 collective-permute-done
  40.0 0.0 collective-permute-done.1
  40.0 0.0 copy-start.8
  40.0 0.0 copy-start.9
  40.1 0.0 copy-start.6
  40.1 7.7 %all-to-all-done.kv_ref = bf16[8,2,40,768]{3,2,1,0:T(8,128)(2,1)S(1)} async-done(((bf16[8,2,40,768]{3,2,1,0:T(8,128)(2,1)}), bf16[8,2,40,768]{3,2,1,0:T(8,128)(2,1)S(1)}, u32[]{:S(2)}, u32[]{:S(2)}) %all-to-all-start) | async-done | bytes 983072 | tf_op jit(solution)/shard_map/all_to_all | solution.py:110
  47.7 1.0 copy-done.3
  48.7 5.3 %shard_map.175 = f32[128,792]{1,0:T(8,128)} custom-call(bf16[128,768]{1,0:T(8,128)(2,1)} %bitcast.27, bf16[8,2,40,768]{3,2,1,0:T(8,128)(2,1)} %copy-done.3, f32[1,320]{1,0:T(1,128)} %or_convert_fusion.mask_ref), custom_call_target="tpu_custom_call" | custom-call | flops 251658240 | bytes 1585152 | tf_op jit(solution)/shard_map/pallas_call | solution.py:62
  54.0 4.3 %all-to-all-start.1 = ((f32[4,32,792]{2,1,0:T(8,128)}), f32[4,32,792]{2,1,0:T(8,128)S(1)}, u32[]{:S(2)}, u32[]{:S(2)}) async-start(f32[4,32,792]{2,1,0:T(8,128)} %bitcast.26), calls=%async_computation.1 | async-start | bytes 917504 | tf_op jit(solution)/shard_map/all_to_all | solution.py:132
  58.3 0.0 copy-done.8
  58.3 0.0 copy-done.9
  58.4 0.0 copy-done.6
  58.4 8.8 %all-to-all-done.1 = f32[4,32,792]{2,1,0:T(8,128)S(1)} async-done(((f32[4,32,792]{2,1,0:T(8,128)}), f32[4,32,792]{2,1,0:T(8,128)S(1)}, u32[]{:S(2)}, u32[]{:S(2)}) %all-to-all-start.1) | async-done | bytes 405536 | tf_op jit(solution)/shard_map/all_to_all | solution.py:132
  67.3 0.1 fusion.35
  67.4 0.3 mul.150
  67.7 0.0 copy-start.4
  67.7 0.3 mul.151
  68.0 0.1 div.40
  68.1 0.1 div.41
  68.3 0.0 all-gather.3.cloned.1.call-done
  68.3 0.3 copy-done.4
  68.6 2.6 %fusion.49 = (f32[32]{0:T(128)S(1)}, f32[32,1536]{1,0:T(8,128)S(1)}) fusion(bf16[768,1536]{0,1:T(8,128)(2,1)} %all-gather.3.cloned.1.call-done, f32[32,768]{1,0:T(8,128)S(1)} %fusion.2, f32[32,768]{1,0:T(8,128)S(1)} %div.41, f32[1536]{0:T(1024)S(1)} %reduce.3, bf16[1,1,32,1536]{3,2,1,0:T(8,128)(2,1)S(1)} %copy-done.4), kind=kOutput, calls=%fused_computation.81 | convolution fusion | flops 75743200 | bytes 2857088 | tf_op jit(solution)/shard_map/dot_general | solution.py:141
  71.2 0.2 multiply_reduce_fusion.1
  71.4 0.1 add_convert_fusion.1
  71.5 15.1 %all_gather.11 = bf16[128,1536]{1,0:T(8,128)(2,1)S(1)} all-gather(bf16[32,1536]{1,0:T(8,128)(2,1)S(1)} %add_convert_fusion.1), channel_id=1, replica_groups=mesh['cfg'=2,'ry'=4,'rc'=2,'sz'=8,'sx'=4] {'ry'}, dimensions={0}, use_global_device_ids=true | all-gather | bytes 491520 | tf_op jit(solution)/shard_map/all_gather | solution.py:150
  86.6 2.0 %fusion.21 = f32[128,1536]{1,0:T(8,128)S(1)} fusion(bf16[384,1536]{1,0:T(8,128)(2,1)S(1)} %copy-done.1, bf16[128,1536]{1,0:T(8,128)(2,1)S(1)} %all_gather.11, bf16[1536,384]{1,0:T(8,128)(2,1)} %param.27), kind=kOutput, calls=%fused_computation.31 | convolution fusion | flops 302432256 | bytes 3538944 | tf_op jit(solution)/shard_map/dot_general | solution.py:159
  88.6 0.0 copy-start.10
  88.6 0.0 copy-start.11
  88.6 0.0 copy-start.7
  88.6 3.1 %fusion = bf16[128,1536]{1,0:T(8,128)(2,1)} fusion(f32[128,1536]{1,0:T(8,128)S(1)} %fusion.21, bf16[384,1536]{1,0:T(8,128)(2,1)} %collective-permute-done.1, bf16[128,1536]{1,0:T(8,128)(2,1)S(1)} %all_gather.11, bf16[1536,384]{1,0:T(8,128)(2,1)} %collective-permute-done), kind=kOutput, calls=%fused_computation.1 | convolution fusion | flops 302825472 | bytes 3932160 | tf_op jit(solution)/shard_map/dot_general | solution.py:160
  91.7 6.1 %all-to-all-start.2 = ((bf16[4,32,1536]{2,1,0:T(8,128)(2,1)}), bf16[4,32,1536]{2,1,0:T(8,128)(2,1)S(1)}, u32[]{:S(2)}, u32[]{:S(2)}) async-start(bf16[4,32,1536]{2,1,0:T(8,128)(2,1)} %bitcast.6), calls=%async_computation.2 | async-start | bytes 786432 | tf_op jit(solution)/shard_map/all_to_all | solution.py:166
  97.9 0.0 copy-done.10
  97.9 0.0 copy-done.11
  97.9 0.0 copy-done.7
  98.0 6.4 %all-to-all-done.2 = bf16[4,32,1536]{2,1,0:T(8,128)(2,1)S(1)} async-done(((bf16[4,32,1536]{2,1,0:T(8,128)(2,1)}), bf16[4,32,1536]{2,1,0:T(8,128)(2,1)S(1)}, u32[]{:S(2)}, u32[]{:S(2)}) %all-to-all-start.2) | async-done | bytes 393248 | tf_op jit(solution)/shard_map/all_to_all | solution.py:166
  104.4 0.1 convert_reduce_fusion
  104.4 0.1 fusion.48
  104.6 0.2 multiply_reduce_fusion
  104.8 0.0 copy-done
  104.8 0.2 fusion.19
  105.0 3.0 %collective-permute-start.2 = (f32[32,64]{1,0:T(8,128)S(1)}, f32[32,64]{1,0:T(8,128)S(1)}, u32[]{:S(2)}, u32[]{:S(2)}) collective-permute-start(f32[32,64]{1,0:T(8,128)S(1)} %fusion.19), channel_id=1, source_target_pairs={{0,256},{256,0},{1,257},{257,1},{2,258},{258,2},{3,259},{259,3},{4... | collective-permute-start | bytes 24584 | tf_op jit(solution)/shard_map/ppermute | solution.py:24
  108.6 5.9 %collective-permute-done.2 = f32[32,64]{1,0:T(8,128)S(1)} collective-permute-done((f32[32,64]{1,0:T(8,128)S(1)}, f32[32,64]{1,0:T(8,128)S(1)}, u32[]{:S(2)}, u32[]{:S(2)}) %collective-permute-start.2) | collective-permute-done | bytes 8224 | tf_op jit(solution)/shard_map/ppermute | solution.py:24
  114.6 0.6 multiply_reduce_fusion.2
  115.2 1.4 pad_maximum_fusion
  116.5 0.6 broadcast_in_dim.8
  117.2 3.9 %all-to-all-start.3 = ((f32[32,1,2]{2,1,0:T(1,128)}), f32[32,1,2]{2,1,0:T(1,128)S(1)}, u32[]{:S(2)}, u32[]{:S(2)}) async-start(f32[32,1,2]{2,1,0:T(1,128)} %broadcast_in_dim.8), calls=%async_computation.3 | async-start | bytes 32768 | tf_op jit(solution)/shard_map/all_to_all | solution.py:180
  121.0 0.0 copy-done.5
  121.0 0.7 bitcast_add_fusion
  121.7 8.9 %all-to-all-done.3 = f32[32,1,2]{2,1,0:T(1,128)S(1)} async-done(((f32[32,1,2]{2,1,0:T(1,128)}), f32[32,1,2]{2,1,0:T(1,128)S(1)}, u32[]{:S(2)}, u32[]{:S(2)}) %all-to-all-start.3) | async-done | bytes 288 | tf_op jit(solution)/shard_map/all_to_all | solution.py:180
  130.6 0.1 copy.19
  130.7 0.6 slice_reduce_fusion.1
  (14 shorter events, 0.2 us)
Async XLA Ops:
  7.2 97.6 %copy-start = (bf16[1536,64]{0,1:T(8,128)(2,1)S(1)}, bf16[1536,64]{0,1:T(8,128)(2,1)}, u32[]{:S(2)}) copy-start(bf16[1536,64]{0,1:T(8,128)(2,1)} %param.29) | copy-start | bytes 589828
  7.2 61.1 %all-gather.3.cloned.1.call-start = ((), (), s32[]{:S(2)}) async-start(), calls=%async_computation.4 | async-start | bytes 2654208 | tf_op jit(solution)/shard_map/all_gather | solution.py:143
  7.9 12.5 %copy-start.2 = (bf16[1536,384]{1,0:T(8,128)(2,1)S(1)}, bf16[1536,384]{1,0:T(8,128)(2,1)}, u32[]{:S(2)}) copy-start(bf16[1536,384]{1,0:T(8,128)(2,1)} %param.27) | copy-start | bytes 3538948
  10.0 12.4 %copy-start.1 = (bf16[384,1536]{1,0:T(8,128)(2,1)S(1)}, bf16[384,1536]{1,0:T(8,128)(2,1)}, u32[]{:S(2)}) copy-start(bf16[384,1536]{1,0:T(8,128)(2,1)} %param.28) | copy-start | bytes 3538948
  10.0 37.8 %all-to-all-start = ((bf16[8,2,40,768]{3,2,1,0:T(8,128)(2,1)}), bf16[8,2,40,768]{3,2,1,0:T(8,128)(2,1)S(1)}, u32[]{:S(2)}, u32[]{:S(2)}) async-start(bf16[8,2,40,768]{3,2,1,0:T(8,128)(2,1)} %broadcast_in_dim.7), calls=%async_computation | async-start | bytes 1966080 | tf_op jit(solution)/shard_map/all_to_all | solution.py:110
  20.4 19.6 %collective-permute-start = (bf16[1536,384]{1,0:T(8,128)(2,1)S(1)}, bf16[1536,384]{1,0:T(8,128)(2,1)}, u32[]{:S(2)}, u32[]{:S(2)}) collective-permute-start(bf16[1536,384]{1,0:T(8,128)(2,1)S(1)} %copy-done.2), channel_id=1, source_target_pairs={{0,32},{32,0},{1,33},{33,1},{2,34},{34,2},{3,35},{35,3},{4,36},{36... | collective-permute-start | bytes 3538952 | tf_op jit(solution)/shard_map/ppermute | solution.py:118
  22.4 17.7 %collective-permute-start.1 = (bf16[384,1536]{1,0:T(8,128)(2,1)S(1)}, bf16[384,1536]{1,0:T(8,128)(2,1)}, u32[]{:S(2)}, u32[]{:S(2)}) collective-permute-start(bf16[384,1536]{1,0:T(8,128)(2,1)S(1)} %copy-done.1), channel_id=1, source_target_pairs={{0,32},{32,0},{1,33},{33,1},{2,34},{34,2},{3,35},{35,3},{4,36},{36... | collective-permute-start | bytes 3538952 | tf_op jit(solution)/shard_map/ppermute | solution.py:119
  40.0 18.3 %copy-start.8 = (f32[1,1,1536]{2,1,0:T(1,128)S(1)}, f32[1,1,1536]{2,1,0:T(1,128)}, u32[]{:S(2)}) copy-start(f32[1,1,1536]{2,1,0:T(1,128)} %param.20) | copy-start | bytes 18436
  40.0 18.3 %copy-start.9 = (f32[1,1,1536]{2,1,0:T(1,128)S(1)}, f32[1,1,1536]{2,1,0:T(1,128)}, u32[]{:S(2)}) copy-start(f32[1,1,1536]{2,1,0:T(1,128)} %param.21) | copy-start | bytes 18436
  40.1 18.3 %copy-start.6 = (f32[1,1,1536]{2,1,0:T(1,128)S(1)}, f32[1,1,1536]{2,1,0:T(1,128)}, u32[]{:S(2)}) copy-start(f32[1,1,1536]{2,1,0:T(1,128)} %param.22) | copy-start | bytes 18436
  47.7 1.0 copy-start.3
  54.0 13.2 %all-to-all-start.1 = ((f32[4,32,792]{2,1,0:T(8,128)}), f32[4,32,792]{2,1,0:T(8,128)S(1)}, u32[]{:S(2)}, u32[]{:S(2)}) async-start(f32[4,32,792]{2,1,0:T(8,128)} %bitcast.26), calls=%async_computation.1 | async-start | bytes 917504 | tf_op jit(solution)/shard_map/all_to_all | solution.py:132
  67.7 0.9 copy-start.4
  88.6 9.3 %copy-start.10 = (f32[1,1,1536]{2,1,0:T(1,128)S(1)}, f32[1,1,1536]{2,1,0:T(1,128)}, u32[]{:S(2)}) copy-start(f32[1,1,1536]{2,1,0:T(1,128)} %param.23) | copy-start | bytes 18436
  88.6 9.3 %copy-start.11 = (f32[1,1,1536]{2,1,0:T(1,128)S(1)}, f32[1,1,1536]{2,1,0:T(1,128)}, u32[]{:S(2)}) copy-start(f32[1,1,1536]{2,1,0:T(1,128)} %param.24) | copy-start | bytes 18436
  88.6 9.3 %copy-start.7 = (f32[1,1,1536]{2,1,0:T(1,128)S(1)}, f32[1,1,1536]{2,1,0:T(1,128)}, u32[]{:S(2)}) copy-start(f32[1,1,1536]{2,1,0:T(1,128)} %param.25) | copy-start | bytes 18436
  91.7 12.7 %all-to-all-start.2 = ((bf16[4,32,1536]{2,1,0:T(8,128)(2,1)}), bf16[4,32,1536]{2,1,0:T(8,128)(2,1)S(1)}, u32[]{:S(2)}, u32[]{:S(2)}) async-start(bf16[4,32,1536]{2,1,0:T(8,128)(2,1)} %bitcast.6), calls=%async_computation.2 | async-start | bytes 786432 | tf_op jit(solution)/shard_map/all_to_all | solution.py:166
  97.9 23.2 %copy-start.5 = (f32[1,32,32]{2,1,0:T(8,128)S(1)}, f32[1,32,32]{2,1,0:T(8,128)}, u32[]{:S(2)}) copy-start(f32[1,32,32]{2,1,0:T(8,128)} %param.30) | copy-start | bytes 12292
  105.0 9.5 %collective-permute-start.2 = (f32[32,64]{1,0:T(8,128)S(1)}, f32[32,64]{1,0:T(8,128)S(1)}, u32[]{:S(2)}, u32[]{:S(2)}) collective-permute-start(f32[32,64]{1,0:T(8,128)S(1)} %fusion.19), channel_id=1, source_target_pairs={{0,256},{256,0},{1,257},{257,1},{2,258},{258,2},{3,259},{259,3},{4... | collective-permute-start | bytes 24584 | tf_op jit(solution)/shard_map/ppermute | solution.py:24
  117.2 13.4 %all-to-all-start.3 = ((f32[32,1,2]{2,1,0:T(1,128)}), f32[32,1,2]{2,1,0:T(1,128)S(1)}, u32[]{:S(2)}, u32[]{:S(2)}) async-start(f32[32,1,2]{2,1,0:T(1,128)} %broadcast_in_dim.8), calls=%async_computation.3 | async-start | bytes 32768 | tf_op jit(solution)/shard_map/all_to_all | solution.py:180
Sparse Core Ops, SparseCore 0:
  10.1 44.8 all-gather.2
